TPU v7x, 512 devices: a whole 4x8x8 slice. The times are simulated.
512 devices in a mesh: tri: 32 (over y, z_lo), vir: 16 (over x, z_hi, core).
Axes of the slice: x: 4, y: 8, z: 8 (z_hi: 2, z_lo: 4; z = z_hi * 4 + z_lo), core: 2. Of those that a mesh axis runs over, the one named last changes fastest.
Arguments:
- amps: bfloat16 [96, 768, 768], P('tri', 'vir'), may hold values from -0.21875 to 0.21875
- vvvo: bfloat16 [96, 768, 128], P('tri', 'vir'), may hold values from -6 to 6
- occ_gap: float32 [64], replicated, may hold values from 0.3 to 1
- vir_gap: float32 [768], P('vir'), may hold values from 0.5 to 2
- pair_gap: float32 [128], replicated, may hold values from 0.5 to 2
- block_sizes: int32 [32], replicated, may hold values from 1 to 3, 64 in all
- roots: int32 [32], replicated, may hold values from 0 to 31, each once
- triples: int32 [384, 2], P('tri'), may hold values from 0 to 31
Outputs:
- density: float32 [768, 128], P('vir')
- grad: float32 [96, 768, 128], P('tri', 'vir')
Inputs may be any that keep to these rules, and one draw needn't show every extreme that they name: `block_sizes`: block sizes sum to 64; at least one block has exactly 3 orbitals. `roots`: each tri index stores exactly one block. `triples`: block numbers; a pair may repeat a block.
All inputs are finite; a program needn't handle non-finite values.
Results may differ from a plain program's by a relative error of at most 0.0003.
Values may be sent and summed in bfloat16 or wider, within the bound.
No kernel may reach another device: no remote copies, remote signals or barrier semaphores. Data moves between devices by JAX's collectives and lax.ppermute only.
A program may use at most 64 MiB of HBM per device.

v0:
```python
import jax
import jax.numpy as jnp
from jax import lax
from jax.sharding import Mesh
from jax.sharding import PartitionSpec as P

BMAX = 3
TRI = ("tri_0", "tri_1")


def whole_of(x, axes, dim):
    if not axes:
        return x
    nearer = lax.all_gather(x, axes[-1], axis=dim, tiled=True)
    return whole_of(nearer, axes[:-1], dim)


def from_everyone(x, axis):
    copies = jnp.broadcast_to(x, (lax.axis_size(axis), *x.shape))
    return lax.all_to_all(copies, axis, split_axis=0, concat_axis=0, tiled=True)


def joined_along(pieces, dim):
    pieces = jnp.moveaxis(pieces, 0, dim)
    lengths = pieces.shape
    return pieces.reshape(*lengths[:dim], lengths[dim] * lengths[dim + 1], *lengths[dim + 2 :])


def gather_directly(x, axis, dim):
    pieces = from_everyone(x, axis)
    return joined_along(pieces, dim)


def in_blocks(x, dim, count):
    before, after = (x.shape[:dim], x.shape[dim + 1 :])
    return jnp.moveaxis(x.reshape(*before, count, -1, *after), dim, 0)


def sent_and_summed(x, axis, dim):
    pieces = in_blocks(x, dim, lax.axis_size(axis))
    arrived = lax.all_to_all(pieces, axis, split_axis=0, concat_axis=0, tiled=True)
    return arrived.sum(axis=0)


def of_everyone(x, axis):
    return from_everyone(x, axis).sum(axis=0)


def body(amps, vvvo, occ_gap, vir_gap, pair_gap, block_sizes, roots, triples):
    tri_count = lax.axis_size(TRI)
    my_index = lax.axis_index(TRI)
    pair_count = triples.shape[0]
    vir_local = amps.shape[1]
    vir_count = amps.shape[2]
    pair_width = vvvo.shape[2]
    occ_count = occ_gap.shape[0]
    slot_ids = jnp.arange(BMAX, dtype=jnp.int32)
    blocks = jnp.arange(tri_count, dtype=jnp.int32)
    occ_index = jnp.arange(occ_count, dtype=jnp.int32)
    offsets = jnp.cumsum(block_sizes) - block_sizes
    own_mask = roots == my_index
    own_size = jnp.sum(jnp.where(own_mask, block_sizes, 0))
    own_off = jnp.sum(jnp.where(own_mask, offsets, 0))
    chooser = triples[:, :, None] == blocks
    pair_root = jnp.sum(jnp.where(chooser, roots, 0), axis=2)
    pair_size = jnp.sum(jnp.where(chooser, block_sizes, 0), axis=2)
    pair_off = jnp.sum(jnp.where(chooser, offsets, 0), axis=2)
    row_ids = pair_root[:, :, None] * BMAX + slot_ids

    def energies(first_slot):
        clipped = jnp.minimum(first_slot, occ_count - 1)
        return jnp.sum(jnp.where(clipped[..., None] == occ_index, occ_gap, 0.0), axis=-1)

    pair_gaps = energies(pair_off[:, :, None] + slot_ids)
    own_gaps = energies(own_off + slot_ids)
    pair_live = slot_ids < pair_size[:, :, None]
    own_live = slot_ids < own_size
    everything = whole_of(amps, TRI, 0)
    chosen = jnp.take(everything, row_ids.reshape(-1), axis=0).reshape(
        pair_count, 2, BMAX, vir_local, vir_count
    )
    complete_integral_table = gather_directly(vvvo, "vir", 1)
    base_den = vir_gap[:, None, None] + own_gaps[None, :, None] + pair_gap[None, None, :]

    def pair_terms(picked_pair, left_proj, right_proj, gap_values, live_mask):
        full_den = (
            base_den[None, None]
            + gap_values[0][:, None, None, None, None]
            + gap_values[1][None, :, None, None, None]
        )
        all_live = (
            live_mask[0][:, None, None, None, None]
            & live_mask[1][None, :, None, None, None]
            & own_live[None, None, None, :, None]
        )
        weighted = jnp.where(all_live, left_proj[:, None] * right_proj[None] / full_den, 0.0)
        dens_term = jnp.sum(weighted * weighted, axis=(0, 1, 3))
        left_rows = picked_pair[0].astype(jnp.float32)
        grad_term = jnp.einsum(
            "rnw,rqnhe->hwe", left_rows, weighted, precision=lax.Precision.HIGHEST
        )
        return (dens_term, grad_term)

    start_state = (
        jnp.zeros((vir_local, pair_width), jnp.float32),
        jnp.zeros((BMAX, vir_count, pair_width), jnp.float32),
    )

    def accumulate(state, inputs):
        picked_pair, gap_values, live_mask = inputs
        left_proj = jnp.einsum(
            "flg,ugw->fluw",
            picked_pair[0],
            complete_integral_table,
            preferred_element_type=jnp.float32,
        )
        right_proj = jnp.einsum(
            "flg,ugw->fluw",
            picked_pair[1],
            complete_integral_table,
            preferred_element_type=jnp.float32,
        )
        dens_term, grad_term = pair_terms(picked_pair, left_proj, right_proj, gap_values, live_mask)
        return ((state[0] + dens_term, state[1] + grad_term), None)

    (density, grad_part), _ = lax.scan(accumulate, start_state, (chosen, pair_gaps, pair_live))
    grad_share = sent_and_summed(grad_part, "vir", 1)
    density_all = of_everyone(density, TRI) / float(tri_count * pair_count)
    return (density_all, grad_share)


def solution(mesh):
    finer = Mesh(mesh.devices.reshape(8, 4, mesh.shape["vir"]), ("tri_0", "tri_1", "vir"))
    return jax.shard_map(
        body,
        mesh=finer,
        in_specs=(
            P(TRI, "vir", None),
            P(TRI, "vir", None),
            P(),
            P("vir"),
            P(),
            P(),
            P(),
            P(TRI, None),
        ),
        out_specs=(P("vir", None), P(TRI, "vir", None)),
        check_vma=False,
    )
```

profile of v0, /device:TPU:6, one launch (start us, length us, event | category | flops | bytes accessed | tf_op | source)
XLA Modules:
  0.0 280.2 jit_solution(6250599871006523590)
XLA Ops:
  7.2 24.4 %all_gather.6 = bf16[12,48,768]{2,1,0:T(8,128)(2,1)} all-gather(bf16[3,48,768]{2,1,0:T(8,128)(2,1)} %param.10), channel_id=1, replica_groups=mesh['tri_0'=8,'tri_1'=4,'vir'=16] {'tri_1'}, dimensions={0}, use_global_device_ids=true | all-gather | bytes 1105920 | tf_op jit(solution)/shard_map/all_gather | solution.py:14
  31.6 1.7 broadcast_in_dim.98
  33.4 10.5 %all-to-all-start = ((bf16[16,3,48,128]{3,2,1,0:T(8,128)(2,1)}), bf16[16,3,48,128]{3,2,1,0:T(8,128)(2,1)S(1)}, u32[]{:S(2)}, u32[]{:S(2)}) async-start(bf16[16,3,48,128]{3,2,1,0:T(8,128)(2,1)} %broadcast_in_dim.98), calls=%async_computation | async-start | bytes 1179648 | tf_op jit(solution)/shard_map/all_to_all | solution.py:20
  45.6 1.4 fusion.15
  46.9 1.4 select_reduce_fusion
  52.1 6.8 %all-to-all-done = bf16[16,3,48,128]{3,2,1,0:T(8,128)(2,1)S(1)} async-done(((bf16[16,3,48,128]{3,2,1,0:T(8,128)(2,1)}), bf16[16,3,48,128]{3,2,1,0:T(8,128)(2,1)S(1)}, u32[]{:S(2)}, u32[]{:S(2)}) %all-to-all-start) | async-done | bytes 589856 | tf_op jit(solution)/shard_map/all_to_all | solution.py:20
  58.9 58.8 %all-gather.2.cloned.1.call-done = bf16[96,48,768]{2,1,0:T(8,128)(2,1)} async-done(((bf16[12,48,768]{2,1,0:T(8,128)(2,1)}), bf16[96,48,768]{2,1,0:T(8,128)(2,1)}) %all-gather.2.cloned.1.call-update) | async-done | bytes 7077904 | tf_op jit(solution)/shard_map/all_gather | solution.py:14
  117.7 8.9 %gather_fusion = bf16[72,48,768]{2,1,0:T(8,128)(2,1)} fusion(bf16[96,48,768]{2,1,0:T(8,128)(2,1)} %all-gather.2.cloned.1.call-done, s32[1024]{0:T(1024)S(1)} %pad_clamp_fusion), kind=kCustom, calls=%fused_computation | custom fusion | bytes 10617120 | tf_op jit(solution)/shard_map/jit(_take)/gather | solution.py:79
  126.6 5.4 %broadcast_select_fusion = bf16[12,2,3,48,768]{4,3,2,1,0:T(8,128)(2,1)} fusion(bf16[12,2,3,48,768]{4,3,2,1,0:T(8,128)(2,1)} %bitcast.64, pred[12,2,3]{2,1,0:T(4,128)(4,1)S(1)} %compare_and_fusion), kind=kLoop, calls=%fused_computation.29 | loop fusion | flops 2654208 | bytes 10616904 | tf_op jit(solution)/shard_map/jit(_take)/select_n | solution.py:79
  132.0 69.1 %while.13 = (s32[]{:T(128)}, f32[48,128]{1,0:T(8,128)S(1)}, f32[3,768,128]{1,2,0:T(8,128)S(1)}, pred[12,2,3]{2,1,0:T(4,128)(4,1)S(1)}, bf16[12,2,3,48,768]{4,3,2...) while((s32[]{:T(128)}, f32[48,128]{1,0:T(8,128)S(1)}, ...), condition=%wide.region_11.12_spmd.clone, body=%wide.region_8.11_spmd.clone.sunk | while | flops 681252928 | bytes 6220744 | solution.py:126
  132.8 1.2 fusion.28
  134.0 1.2 fusion.29
  135.7 2.0 fusion.31
  138.6 1.2 fusion.28
  139.8 1.2 fusion.29
  141.4 2.0 fusion.31
  144.3 1.2 fusion.28
  145.5 1.2 fusion.29
  147.2 2.0 fusion.31
  150.1 1.2 fusion.28
  151.3 1.2 fusion.29
  153.0 2.0 fusion.31
  155.8 1.2 fusion.28
  157.1 1.2 fusion.29
  158.7 2.0 fusion.31
  161.6 1.2 fusion.28
  162.8 1.2 fusion.29
  164.5 2.0 fusion.31
  167.4 1.2 fusion.28
  168.6 1.2 fusion.29
  170.3 2.0 fusion.31
  173.1 1.2 fusion.28
  174.3 1.2 fusion.29
  176.0 2.0 fusion.31
  178.9 1.2 fusion.28
  180.1 1.2 fusion.29
  181.8 2.0 fusion.31
  184.6 1.2 fusion.28
  185.9 1.2 fusion.29
  187.5 2.0 fusion.31
  191.6 1.2 fusion.29
  193.3 2.0 fusion.31
  197.4 1.2 fusion.29
  199.1 2.0 fusion.31
  202.1 8.1 %all-to-all-start.1 = ((f32[32,48,128]{2,1,0:T(8,128)}), f32[32,48,128]{2,1,0:T(8,128)S(1)}, u32[]{:S(2)}, u32[]{:S(2)}) async-start(f32[32,48,128]{2,1,0:T(8,128)} %broadcast_in_dim.104), calls=%async_computation.1 | async-start | bytes 1572864 | tf_op jit(solution)/shard_map/all_to_all | solution.py:20
  211.6 22.0 %all-to-all-done.1 = f32[32,48,128]{2,1,0:T(8,128)S(1)} async-done(((f32[32,48,128]{2,1,0:T(8,128)}), f32[32,48,128]{2,1,0:T(8,128)S(1)}, u32[]{:S(2)}, u32[]{:S(2)}) %all-to-all-start.1) | async-done | bytes 786464 | tf_op jit(solution)/shard_map/all_to_all | solution.py:20
  233.6 7.7 %all-to-all-start.2 = ((f32[16,3,48,128]{3,2,1,0:T(8,128)}), f32[16,3,48,128]{3,2,1,0:T(8,128)S(1)}, u32[]{:S(2)}, u32[]{:S(2)}) async-start(f32[16,3,48,128]{3,2,1,0:T(8,128)} %copy.42), calls=%async_computation.2 | async-start | bytes 2359296 | tf_op jit(solution)/shard_map/all_to_all | solution.py:41
  242.0 30.7 %all-to-all-done.2 = f32[16,3,48,128]{3,2,1,0:T(8,128)S(1)} async-done(((f32[16,3,48,128]{3,2,1,0:T(8,128)}), f32[16,3,48,128]{3,2,1,0:T(8,128)S(1)}, u32[]{:S(2)}, u32[]{:S(2)}) %all-to-all-start.2) | async-done | bytes 1179680 | tf_op jit(solution)/shard_map/all_to_all | solution.py:41
  (164 shorter events, 26.2 us)
Async XLA Ops:
  7.2 110.6 %all-gather.2.cloned.1.call-start = ((), (), s32[]{:S(2)}) async-start(), calls=%async_computation.3 | async-start | bytes 7962624 | tf_op jit(solution)/shard_map/all_gather | solution.py:14
  33.4 25.5 %all-to-all-start = ((bf16[16,3,48,128]{3,2,1,0:T(8,128)(2,1)}), bf16[16,3,48,128]{3,2,1,0:T(8,128)(2,1)S(1)}, u32[]{:S(2)}, u32[]{:S(2)}) async-start(bf16[16,3,48,128]{3,2,1,0:T(8,128)(2,1)} %broadcast_in_dim.98), calls=%async_computation | async-start | bytes 1179648 | tf_op jit(solution)/shard_map/all_to_all | solution.py:20
  126.6 5.4 %copy-start = (f32[128]{0:T(128)S(1)}, f32[128]{0:T(128)}, u32[]{:S(2)}) copy-start(f32[128]{0:T(128)} %param.14) | copy-start | bytes 1540
  202.1 31.6 %all-to-all-start.1 = ((f32[32,48,128]{2,1,0:T(8,128)}), f32[32,48,128]{2,1,0:T(8,128)S(1)}, u32[]{:S(2)}, u32[]{:S(2)}) async-start(f32[32,48,128]{2,1,0:T(8,128)} %broadcast_in_dim.104), calls=%async_computation.1 | async-start | bytes 1572864 | tf_op jit(solution)/shard_map/all_to_all | solution.py:20
  233.6 39.0 %all-to-all-start.2 = ((f32[16,3,48,128]{3,2,1,0:T(8,128)}), f32[16,3,48,128]{3,2,1,0:T(8,128)S(1)}, u32[]{:S(2)}, u32[]{:S(2)}) async-start(f32[16,3,48,128]{3,2,1,0:T(8,128)} %copy.42), calls=%async_computation.2 | async-start | bytes 2359296 | tf_op jit(solution)/shard_map/all_to_all | solution.py:41
Sparse Core Ops, SparseCore 0:
  31.8 85.9 all-gather.1
where the time goes:
time: 283 us; the launch traced here: 280 us
  waiting for transfers between devices  118 us (42%)
  matrix products  53.3 us (19%)
  other arithmetic  27.3 us (10%)
  starting transfers between devices  26.3 us (9%)
  blocking collectives  24.4 us (9%)
  local copies, waits for them, and re-layouts  15.2 us (5%)
  between operations  14.2 us (5%)
    all_gather x1, waiting for transfers between devices, whole_of(): nearer = lax.all_gather(x, axes[-1], axis=dim, tiled=True)  58.8 us
    all_to_all x1, waiting for transfers between devices, sent_and_summed(): lax.all_to_all(pieces, axis, split_axis=0, concat_axis=0, tiled=True)  30.7 us
    all_to_all x2, waiting for transfers between devices, from_everyone(): return lax.all_to_all(copies, axis, split_axis=0, concat_axis=0, tiled=True)  28.8 us
    all_gather x1, blocking collectives, whole_of(): nearer = lax.all_gather(x, axes[-1], axis=dim, tiled=True)  24.4 us
    dot_general x12, matrix products, pair_terms(): jnp.einsum('rnw,rqnhe->hwe', left_rows, weighted, precision=lax.Precision...  24.2 us
    all_to_all x2, starting transfers between devices, from_everyone(): return lax.all_to_all(copies, axis, split_axis=0, concat_axis=0, tiled=True)  18.6 us
    dot_general x12, matrix products, accumulate(): jnp.einsum('flg,ugw->fluw', picked_pair[0], complete_integral_table, pref...  14.6 us
    dot_general x12, matrix products, accumulate(): jnp.einsum('flg,ugw->fluw', picked_pair[1], complete_integral_table, pref...  14.5 us
  transfers between devices with their start and end apart: 4, of which 4 were waited for; matrix products, arithmetic and copies ran while one was open for 4% of the time, Pallas kernels for 0%

commit v1 on v0

v1 whole, which is shorter than its diff:
```python
import jax
import jax.numpy as jnp
from jax import lax
from jax.sharding import PartitionSpec as P

BMAX = 3


def body(amps, vvvo, occ_gap, vir_gap, pair_gap, block_sizes, roots, triples):
    tri_count = lax.axis_size("tri")
    me = lax.axis_index("tri")
    npair = triples.shape[0]
    nocc = occ_gap.shape[0]
    nrow = tri_count * BMAX
    f32, bf16 = jnp.float32, jnp.bfloat16
    slots = jnp.arange(BMAX, dtype=jnp.int32)
    offsets = (jnp.cumsum(block_sizes) - block_sizes).astype(jnp.int32)

    own = roots == me
    own_size = jnp.sum(jnp.where(own, block_sizes, 0))
    own_off = jnp.sum(jnp.where(own, offsets, 0))
    own_gap = occ_gap[jnp.minimum(own_off + slots, nocc - 1)]
    own_live = slots < own_size

    pair_root = roots[triples]
    pair_gap_occ = occ_gap[jnp.minimum(offsets[triples][..., None] + slots, nocc - 1)]
    pair_live = slots < block_sizes[triples][..., None]
    rows = pair_root[..., None] * BMAX + slots

    everything = lax.all_gather(amps, "tri", axis=0, tiled=True)
    table = lax.all_gather(vvvo, "vir", axis=1, tiled=True)

    pick = (rows.reshape(-1)[:, None] == jnp.arange(nrow, dtype=jnp.int32)).astype(bf16)
    picked = jnp.einsum("rb,bad->rad", pick, everything, preferred_element_type=bf16)
    proj = jnp.einsum("rad,kdm->rakm", picked, table, preferred_element_type=f32)
    nv, nk, nm = proj.shape[1], proj.shape[2], proj.shape[3]
    proj = proj.reshape(npair, 2, BMAX, nv, nk, nm)
    left, right = proj[:, 0], proj[:, 1]

    base = vir_gap[:, None, None] + own_gap[None, :, None] + pair_gap[None, None, :]
    den = (
        base[None, None, None]
        + pair_gap_occ[:, 0, :, None, None, None, None]
        + pair_gap_occ[:, 1, None, :, None, None, None]
    )
    live = (
        pair_live[:, 0, :, None, None, None, None]
        & pair_live[:, 1, None, :, None, None, None]
        & own_live[None, None, None, None, :, None]
    )
    weighted = jnp.where(live, left[:, :, None] * right[:, None] / den, 0.0)
    dens_part = jnp.sum(weighted * weighted, axis=(0, 1, 2, 4))
    summed = jnp.sum(weighted, axis=2)

    hi_f32 = lax.reduce_precision(summed, exponent_bits=8, mantissa_bits=7)
    hi = hi_f32.astype(bf16)
    lo = (summed - hi_f32).astype(bf16)
    left_rows = picked.reshape(npair, 2, BMAX, nv, -1)[:, 0]
    grad = jnp.einsum("qiad,qiakm->dkm", left_rows, hi, preferred_element_type=f32)
    grad = grad + jnp.einsum("qiad,qiakm->dkm", left_rows, lo, preferred_element_type=f32)
    grad = lax.psum_scatter(grad, "vir", scatter_dimension=0, tiled=True)
    grad = jnp.transpose(grad, (1, 0, 2))

    density = lax.psum(dens_part, "tri") / float(tri_count * npair)
    return density, grad


def solution(mesh):
    return jax.shard_map(
        body,
        mesh=mesh,
        in_specs=(
            P("tri", "vir", None),
            P("tri", "vir", None),
            P(),
            P("vir"),
            P(),
            P(),
            P(),
            P("tri", None),
        ),
        out_specs=(P("vir", None), P("tri", "vir", None)),
        check_vma=False,
    )
```

time: 283 us -> 374 us (1.32)
  blocking collectives: 24.4 us -> 205 us
  matrix products: 53.3 us -> 15.1 us
  starting transfers between devices: 26.3 us -> 0.08 us
  other arithmetic: 27.3 us -> 7.75 us
  local copies, waits for them, and re-layouts: 15.2 us -> 7.68 us
  waiting for transfers between devices: 118 us -> 123 us
    psum x0 -> x1, blocking collectives: none -> 151 us  [body(): density = lax.psum(dens_part, 'tri') / float(tri_count * npair)]
    all_gather x1, waiting for transfers between devices: 58.8 us -> 123 us  [body(): everything = lax.all_gather(amps, 'tri', axis=0, tiled=True)]
    all_to_all x3 -> x0, waiting for transfers between devices: 59.5 us -> none  [the longest x1 30.7 us: sent_and_summed(): lax.all_to_all(pieces, axis, split_axis=0, concat_axis=0, tiled=True)]
    dot_general x36 -> x4, matrix products: 53.3 us -> 15.1 us  [the longest x1 7.92 us: body(): jnp.einsum('rb,bad->rad', pick, everything, preferred_element_type=bf16)]
    all_gather x1, blocking collectives: 24.4 us -> 53.9 us  [body(): table = lax.all_gather(vvvo, 'vir', axis=1, tiled=True)]
    all_to_all x3 -> x0, starting transfers between devices: 26.3 us -> none  [the longest x2 18.6 us: from_everyone(): return lax.all_to_all(copies, axis, split_axis=0, concat_axis=0, tiled=True)]
    lt x13 -> x2, other arithmetic: 7.58 us -> 0.67 us  [the longest x1 0.66 us: body(): own_live = slots < own_size]
    gather x1 -> x9, local copies, waits for them, and re-layouts: 8.91 us -> 4.32 us  [the longest x2 1.33 us: body(): occ_gap[jnp.minimum(offsets[triples][..., None] + slots, nocc - 1)]]
  transfers between devices with their start and end apart: 4 -> 2, of which waited for: 4 -> 1; matrix products, arithmetic and copies ran while one was open for 4% -> 3% of each run, Pallas kernels for 0% -> 0%
where the time goes in v1:
time: 374 us; the launch traced here: 373 us
  blocking collectives  205 us (55%)
  waiting for transfers between devices  123 us (33%)
  matrix products  15.1 us (4%)
  between operations  14.3 us (4%)
  other arithmetic  7.75 us (2%)
  local copies, waits for them, and re-layouts  7.68 us (2%)
    psum x1, blocking collectives, body(): density = lax.psum(dens_part, 'tri') / float(tri_count * npair)  151 us
    all_gather x1, waiting for transfers between devices, body(): everything = lax.all_gather(amps, 'tri', axis=0, tiled=True)  123 us
    all_gather x1, blocking collectives, body(): table = lax.all_gather(vvvo, 'vir', axis=1, tiled=True)  53.9 us
    dot_general x1, matrix products, body(): jnp.einsum('rb,bad->rad', pick, everything, preferred_element_type=bf16)  7.92 us
  transfers between devices with their start and end apart: 2, of which 1 were waited for; matrix products, arithmetic and copies ran while one was open for 3% of the time, Pallas kernels for 0%

profile of v1, /device:TPU:6, one launch (start us, length us, event | category | flops | bytes accessed | tf_op | source)
XLA Modules:
  0.0 372.8 jit_solution(18367673848902578636)
XLA Ops:
  7.2 0.7 all-gather.2.cloned.1.call-update
  7.9 0.0 reduce-scatter.2.cloned.1.call-start
  8.0 0.7 copy.60
  8.7 0.1 reduce-window.9
  8.8 0.1 reduce
  8.9 0.7 compare_select_fusion.1
  9.6 0.1 copy.54
  9.7 0.1 reshape.160
  9.8 0.7 gather_fusion
  10.5 0.7 gather_fusion.1
  11.2 0.6 fusion.17
  11.8 0.7 gather_fusion.3
  12.5 0.1 reshape.183
  12.6 0.1 compare_select_fusion
  12.7 0.1 reshape.192
  12.9 1.2 gather_fusion.4
  14.1 0.1 reshape.191
  14.2 0.1 copy.63
  14.3 0.1 copy.64
  14.4 0.1 copy.61
  14.5 0.1 copy.62
  14.6 0.7 fusion.19
  15.3 0.6 gather_fusion.2
  15.9 0.1 reshape.206
  16.0 0.1 iota_add_fusion
  16.1 0.1 add.157
  16.2 0.1 reshape.159
  16.3 0.1 copy.55
  16.4 0.1 copy.57
  16.5 0.1 copy.56
  16.6 0.7 iota_compare_fusion.2
  17.3 0.1 broadcast_add_fusion.2
  17.4 0.1 broadcast_and_fusion.1
  17.5 0.1 broadcast_and_fusion
  17.6 0.1 broadcast_add_fusion.1
  17.7 53.9 %all_gather.7 = bf16[3,768,128]{2,1,0:T(8,128)(2,1)S(1)} all-gather(bf16[3,48,128]{2,1,0:T(8,128)(2,1)S(1)} %copy-done.3), channel_id=1, replica_groups=mesh['tri'=32,'vir'=16] {'vir'}, dimensions={1}, use_global_device_ids=true | all-gather | bytes 626688 | tf_op jit(solution)/shard_map/all_gather | solution.py:31
  71.5 0.2 broadcast_add_fusion
  71.8 122.6 %all-gather.2.cloned.1.call-done = bf16[96,48,768]{2,1,0:T(8,128)(2,1)} async-done(((bf16[3,48,768]{2,1,0:T(8,128)(2,1)}), bf16[96,48,768]{2,1,0:T(8,128)(2,1)}) %all-gather.2.cloned.1.call-update) | async-done | bytes 7077904 | tf_op jit(solution)/shard_map/all_gather | solution.py:30
  194.3 7.9 %fusion = bf16[72,48,768]{2,0,1:T(8,128)(2,1)S(1)} fusion(bf16[96,48,768]{2,1,0:T(8,128)(2,1)} %all-gather.2.cloned.1.call-done, s32[72]{0:T(128)S(1)} %add.157), kind=kOutput, calls=%fused_computation.7 | convolution fusion | flops 509614848 | bytes 12386592 | tf_op jit(solution)/shard_map/rb,bad->rad/dot_general | solution.py:34
  202.3 1.0 copy.65
  203.3 2.9 fusion.3
  206.3 0.5 slice_bitcast_fusion.1
  206.7 3.1 fusion.2
  209.9 0.4 fusion.5
  210.3 1.6 fusion.8
  211.9 2.7 fusion.10
  214.6 150.8 %psum.7 = f32[48,128]{1,0:T(8,128)S(1)} all-reduce(f32[48,128]{1,0:T(8,128)S(1)} %get-tuple-element.3), channel_id=1, replica_groups=mesh['tri'=32,'vir'=16] {'tri'}, use_global_device_ids=true, to_apply=%region_4.5 | all-reduce | flops 6144 | bytes 49152 | tf_op jit(solution)/shard_map/psum | solution.py:64
  365.4 0.6 broadcast_multiply_fusion
  (22 shorter events, 0.1 us)
Async XLA Ops:
  7.2 5.7 %copy-start = (f32[64]{0:T(128)S(1)}, f32[64]{0:T(128)}, u32[]{:S(2)}) copy-start(f32[64]{0:T(128)} %param.10) | copy-start | bytes 772
  7.2 2.6 copy-start.1
  7.2 187.1 %all-gather.2.cloned.1.call-start = ((), (), s32[]{:S(2)}) async-start(), calls=%async_computation.1 | async-start | bytes 7299072 | tf_op jit(solution)/shard_map/all_gather | solution.py:30
  7.9 358.1 %reduce-scatter.2.cloned.1.call-start = ((), (), s32[]{:S(2)}) async-start(), calls=%async_computation.2 | async-start | bytes 1253376 | tf_op jit(solution)/shard_map/reduce_scatter | solution.py:61
  9.8 0.7 copy-start.2
  12.8 4.5 %copy-start.5 = (f32[48]{0:T(128)S(1)}, f32[48]{0:T(128)}, u32[]{:S(2)}) copy-start(f32[48]{0:T(128)} %param.11) | copy-start | bytes 580
  12.9 4.7 %copy-start.4 = (f32[128]{0:T(128)S(1)}, f32[128]{0:T(128)}, u32[]{:S(2)}) copy-start(f32[128]{0:T(128)} %param.12) | copy-start | bytes 1540
  12.9 4.8 %copy-start.3 = (bf16[3,48,128]{2,1,0:T(8,128)(2,1)S(1)}, bf16[3,48,128]{2,1,0:T(8,128)(2,1)}, u32[]{:S(2)}) copy-start(bf16[3,48,128]{2,1,0:T(8,128)(2,1)} %param.9) | copy-start | bytes 110596
Sparse Core Ops, SparseCore 0:
  10.1 184.2 all-gather.1
  214.7 88.3 reduce-scatter.1

commit v2 on v1

--- a/solution.py
+++ b/solution.py
@@ -1,14 +1,51 @@
 import jax
 import jax.numpy as jnp
 from jax import lax
+from jax.sharding import Mesh
 from jax.sharding import PartitionSpec as P
 
 BMAX = 3
+TRI = ("tri_0", "tri_1")
+
+
+def whole_of(x, axes, dim):
+    if not axes:
+        return x
+    nearer = lax.all_gather(x, axes[-1], axis=dim, tiled=True)
+    return whole_of(nearer, axes[:-1], dim)
+
+
+def from_everyone(x, axis):
+    copies = jnp.broadcast_to(x, (lax.axis_size(axis), *x.shape))
+    return lax.all_to_all(copies, axis, split_axis=0, concat_axis=0, tiled=True)
+
+
+def joined_along(pieces, dim):
+    pieces = jnp.moveaxis(pieces, 0, dim)
+    lengths = pieces.shape
+    return pieces.reshape(*lengths[:dim], lengths[dim] * lengths[dim + 1], *lengths[dim + 2 :])
+
+
+def sent_and_summed(x, axis, dim):
+    before, after = (x.shape[:dim], x.shape[dim + 1 :])
+    pieces = jnp.moveaxis(x.reshape(*before, lax.axis_size(axis), -1, *after), dim, 0)
+    arrived = lax.all_to_all(pieces, axis, split_axis=0, concat_axis=0, tiled=True)
+    return arrived.sum(axis=0)
+
+
+def butterfly_sum(x, axes):
+    count = lax.axis_size(axes)
+    bit = 1
+    while bit < count:
+        perm = [(i, i ^ bit) for i in range(count)]
+        x = x + lax.ppermute(x, axes, perm)
+        bit *= 2
+    return x
 
 
 def body(amps, vvvo, occ_gap, vir_gap, pair_gap, block_sizes, roots, triples):
-    tri_count = lax.axis_size("tri")
-    me = lax.axis_index("tri")
+    tri_count = lax.axis_size(TRI)
+    me = lax.axis_index(TRI)
     npair = triples.shape[0]
     nocc = occ_gap.shape[0]
     nrow = tri_count * BMAX
@@ -27,8 +64,8 @@
     pair_live = slots < block_sizes[triples][..., None]
     rows = pair_root[..., None] * BMAX + slots
 
-    everything = lax.all_gather(amps, "tri", axis=0, tiled=True)
-    table = lax.all_gather(vvvo, "vir", axis=1, tiled=True)
+    everything = whole_of(amps, TRI, 0)
+    table = joined_along(from_everyone(vvvo, "vir"), 1)
 
     pick = (rows.reshape(-1)[:, None] == jnp.arange(nrow, dtype=jnp.int32)).astype(bf16)
     picked = jnp.einsum("rb,bad->rad", pick, everything, preferred_element_type=bf16)
@@ -58,27 +95,29 @@
     left_rows = picked.reshape(npair, 2, BMAX, nv, -1)[:, 0]
     grad = jnp.einsum("qiad,qiakm->dkm", left_rows, hi, preferred_element_type=f32)
     grad = grad + jnp.einsum("qiad,qiakm->dkm", left_rows, lo, preferred_element_type=f32)
-    grad = lax.psum_scatter(grad, "vir", scatter_dimension=0, tiled=True)
+    grad = sent_and_summed(grad, "vir", 0)
     grad = jnp.transpose(grad, (1, 0, 2))
 
-    density = lax.psum(dens_part, "tri") / float(tri_count * npair)
+    density = butterfly_sum(dens_part, TRI) / float(tri_count * npair)
     return density, grad
 
 
 def solution(mesh):
+    tri_hi = mesh.shape["tri"] // 4
+    finer = Mesh(mesh.devices.reshape(tri_hi, 4, mesh.shape["vir"]), ("tri_0", "tri_1", "vir"))
     return jax.shard_map(
         body,
-        mesh=mesh,
+        mesh=finer,
         in_specs=(
-            P("tri", "vir", None),
-            P("tri", "vir", None),
+            P(TRI, "vir", None),
+            P(TRI, "vir", None),
             P(),
             P("vir"),
             P(),
             P(),
             P(),
-            P("tri", None),
+            P(TRI, None),
         ),
-        out_specs=(P("vir", None), P("tri", "vir", None)),
+        out_specs=(P("vir", None), P(TRI, "vir", None)),
         check_vma=False,
     )

time: 374 us -> 214 us (0.57)
  blocking collectives: 205 us -> 24.4 us
  starting transfers between devices: 0.08 us -> 36.1 us
  waiting for transfers between devices: 123 us -> 105 us
    psum x1 -> x0, blocking collectives: 151 us -> none  [body(): density = lax.psum(dens_part, 'tri') / float(tri_count * npair)]
    all_gather x1, waiting for transfers between devices: 123 us -> 58 us  [whole_of(): nearer = lax.all_gather(x, axes[-1], axis=dim, tiled=True)]
    ppermute x0 -> x5, waiting for transfers between devices: none -> 41 us  [butterfly_sum(): x = x + lax.ppermute(x, axes, perm)]
    all_gather x1, blocking collectives: 53.9 us -> 24.4 us  [whole_of(): nearer = lax.all_gather(x, axes[-1], axis=dim, tiled=True)]
    all_to_all x0 -> x2, starting transfers between devices: none -> 20.9 us  [the longest x1 10.5 us: from_everyone(): return lax.all_to_all(copies, axis, split_axis=0, concat_axis=0, tiled=True)]
    ppermute x0 -> x5, starting transfers between devices: none -> 15.2 us  [butterfly_sum(): x = x + lax.ppermute(x, axes, perm)]
    all_to_all x0 -> x2, waiting for transfers between devices: none -> 6.4 us  [the longest x1 6.4 us: from_everyone(): return lax.all_to_all(copies, axis, split_axis=0, concat_axis=0, tiled=True)]
  transfers between devices with their start and end apart: 2 -> 8, of which waited for: 1 -> 7; matrix products, arithmetic and copies ran while one was open for 3% -> 5% of each run, Pallas kernels for 0% -> 0%
where the time goes in v2:
time: 214 us; the launch traced here: 213 us
  waiting for transfers between devices  105 us (49%)
  starting transfers between devices  36.1 us (17%)
  blocking collectives  24.4 us (11%)
  between operations  14.3 us (7%)
  matrix products  14.1 us (7%)
  local copies, waits for them, and re-layouts  10.7 us (5%)
  other arithmetic  7.79 us (4%)
    all_gather x1, waiting for transfers between devices, whole_of(): nearer = lax.all_gather(x, axes[-1], axis=dim, tiled=True)  58 us
    ppermute x5, waiting for transfers between devices, butterfly_sum(): x = x + lax.ppermute(x, axes, perm)  41 us
    all_gather x1, blocking collectives, whole_of(): nearer = lax.all_gather(x, axes[-1], axis=dim, tiled=True)  24.4 us
    ppermute x5, starting transfers between devices, butterfly_sum(): x = x + lax.ppermute(x, axes, perm)  15.2 us
    all_to_all x1, starting transfers between devices, from_everyone(): return lax.all_to_all(copies, axis, split_axis=0, concat_axis=0, tiled=True)  10.5 us
    all_to_all x1, starting transfers between devices, sent_and_summed(): lax.all_to_all(pieces, axis, split_axis=0, concat_axis=0, tiled=True)  10.4 us
    dot_general x1, matrix products, body(): jnp.einsum('rb,bad->rad', pick, everything, preferred_element_type=bf16)  7.92 us
    all_to_all x1, waiting for transfers between devices, from_everyone(): return lax.all_to_all(copies, axis, split_axis=0, concat_axis=0, tiled=True)  6.4 us
  transfers between devices with their start and end apart: 8, of which 7 were waited for; matrix products, arithmetic and copies ran while one was open for 5% of the time, Pallas kernels for 0%

profile of v2, /device:TPU:6, one launch (start us, length us, event | category | flops | bytes accessed | tf_op | source)
XLA Modules:
  0.0 212.9 jit_solution(5295340631605588599)
XLA Ops:
  7.2 24.4 %all_gather.6 = bf16[12,48,768]{2,1,0:T(8,128)(2,1)} all-gather(bf16[3,48,768]{2,1,0:T(8,128)(2,1)} %param.8), channel_id=1, replica_groups=mesh['tri_0'=8,'tri_1'=4,'vir'=16] {'tri_1'}, dimensions={0}, use_global_device_ids=true | all-gather | bytes 1105920 | tf_op jit(solution)/shard_map/all_gather | solution.py:14
  31.7 1.7 broadcast_in_dim.20
  33.4 10.5 %all-to-all-start = ((bf16[16,3,48,128]{3,2,1,0:T(8,128)(2,1)}), bf16[16,3,48,128]{3,2,1,0:T(8,128)(2,1)S(1)}, u32[]{:S(2)}, u32[]{:S(2)}) async-start(bf16[16,3,48,128]{3,2,1,0:T(8,128)(2,1)} %broadcast_in_dim.20), calls=%async_computation | async-start | bytes 1179648 | tf_op jit(solution)/shard_map/all_to_all | solution.py:20
  44.0 0.1 reduce
  44.2 0.1 copy.54
  44.4 0.7 gather_fusion
  45.1 0.7 gather_fusion.1
  45.8 0.6 fusion.14
  46.4 0.7 gather_fusion.3
  47.2 0.1 compare_select_fusion
  47.3 0.1 reshape.195
  47.5 1.2 gather_fusion.4
  48.7 0.1 reshape.194
  48.8 0.7 fusion.16
  49.5 0.6 gather_fusion.2
  50.7 0.1 copy.65
  50.9 0.1 copy.63
  51.0 0.1 add.172
  51.1 0.1 copy.57
  51.2 0.1 copy.56
  51.3 0.7 iota_compare_fusion.2
  52.0 0.1 broadcast_and_fusion
  52.2 0.2 broadcast_add_fusion
  52.5 6.4 %all-to-all-done = bf16[16,3,48,128]{3,2,1,0:T(8,128)(2,1)S(1)} async-done(((bf16[16,3,48,128]{3,2,1,0:T(8,128)(2,1)}), bf16[16,3,48,128]{3,2,1,0:T(8,128)(2,1)S(1)}, u32[]{:S(2)}, u32[]{:S(2)}) %all-to-all-start) | async-done | bytes 589856 | tf_op jit(solution)/shard_map/all_to_all | solution.py:20
  58.9 0.9 copy.60
  59.8 58.0 %all-gather.2.cloned.1.call-done = bf16[96,48,768]{2,1,0:T(8,128)(2,1)} async-done(((bf16[12,48,768]{2,1,0:T(8,128)(2,1)}), bf16[96,48,768]{2,1,0:T(8,128)(2,1)}) %all-gather.2.cloned.1.call-update) | async-done | bytes 7077904 | tf_op jit(solution)/shard_map/all_gather | solution.py:14
  117.8 7.9 %fusion = bf16[72,48,768]{2,0,1:T(8,128)(2,1)S(1)} fusion(bf16[96,48,768]{2,1,0:T(8,128)(2,1)} %all-gather.2.cloned.1.call-done, s32[72]{0:T(128)S(1)} %add.172), kind=kOutput, calls=%fused_computation.7 | convolution fusion | flops 509614848 | bytes 12386592 | tf_op jit(solution)/shard_map/rb,bad->rad/dot_general | solution.py:71
  125.7 1.0 copy.59
  126.8 2.9 %fusion.18 = f32[12,2,3,48,3,128]{5,3,4,2,1,0:T(8,128)S(1)} fusion(bf16[12,2,3,48,768,1]{4,3,5,2,1,0:T(8,128)(2,1)S(1)} %bitcast.57, bf16[3,768,128,1,1,1]{2,1,0,5,4,3:T(8,128)(2,1)S(1)} %bitcast.62), kind=kOutput, calls=%fused_computation.50 | convolution fusion | flops 2038431744 | bytes 11206656 | tf_op jit(solution)/shard_map/rad,kdm->rakm/dot_general | solution.py:72
  129.7 0.5 slice_bitcast_fusion.1
  130.1 3.1 %fusion.2 = (f32[12,3,48,3,128]{4,2,3,1,0:T(8,128)S(1)}, f32[48,128]{1,0:T(8,128)S(1)}) fusion(f32[12,3]{1,0:T(8,128)S(1)} %copy.65, f32[12,3,48,3,128]{4,2,3,1,0:T(8,128)S(1)} %broadcast_add_fusion, f32[12,3,48,3,128]{4,2,3,1,0:T(8,128)S(1)} %get-tuple-element.8, f32[12,3,48,3,128]{4,2,3,1,0:T(8,128)S(1)} %get-tuple-element.7, ...), kind=kLoop, calls=%fused_computation.9 | loop fusion | flops 13264896 | bytes 10641876 | tf_op jit(solution)/shard_map/reduce_sum | solution.py:90
  133.3 0.4 fusion.3
  133.7 1.6 fusion.6
  135.3 1.7 fusion.8
  137.0 1.1 copy.69
  138.1 10.4 %all-to-all-start.1 = ((f32[16,48,3,128]{3,1,2,0:T(8,128)}), f32[16,48,3,128]{3,1,2,0:T(8,128)S(1)}, u32[]{:S(2)}, u32[]{:S(2)}) async-start(f32[16,48,3,128]{3,1,2,0:T(8,128)} %copy.69), calls=%async_computation.1 | async-start | bytes 2359296 | tf_op jit(solution)/shard_map/all_to_all | solution.py:32
  148.5 2.6 %collective-permute-start = (f32[48,128]{1,0:T(8,128)S(1)}, f32[48,128]{1,0:T(8,128)S(1)}, u32[]{:S(2)}, u32[]{:S(2)}) collective-permute-start(f32[48,128]{1,0:T(8,128)S(1)} %get-tuple-element.3), channel_id=1, source_target_pairs={{0,16},{16,0},{32,48},{48,32},{64,80},{80,64},{96,112},{112,96},{1... | collective-permute-start | bytes 73736 | tf_op jit(solution)/shard_map/ppermute | solution.py:41
  151.1 25.1 %collective-permute-done = f32[48,128]{1,0:T(8,128)S(1)} collective-permute-done((f32[48,128]{1,0:T(8,128)S(1)}, f32[48,128]{1,0:T(8,128)S(1)}, u32[]{:S(2)}, u32[]{:S(2)}) %collective-permute-start) | collective-permute-done | bytes 24608 | tf_op jit(solution)/shard_map/ppermute | solution.py:41
  176.2 1.9 collective-permute-start.1
  178.1 4.7 %collective-permute-done.1 = f32[48,128]{1,0:T(8,128)S(1)} collective-permute-done((f32[48,128]{1,0:T(8,128)S(1)}, f32[48,128]{1,0:T(8,128)S(1)}, u32[]{:S(2)}, u32[]{:S(2)}) %collective-permute-start.1) | collective-permute-done | bytes 24608 | tf_op jit(solution)/shard_map/ppermute | solution.py:41
  182.8 2.0 collective-permute-start.2
  184.8 3.7 %collective-permute-done.2 = f32[48,128]{1,0:T(8,128)S(1)} collective-permute-done((f32[48,128]{1,0:T(8,128)S(1)}, f32[48,128]{1,0:T(8,128)S(1)}, u32[]{:S(2)}, u32[]{:S(2)}) %collective-permute-start.2) | collective-permute-done | bytes 24608 | tf_op jit(solution)/shard_map/ppermute | solution.py:41
  188.5 3.6 %collective-permute-start.3 = (f32[48,128]{1,0:T(8,128)S(1)}, f32[48,128]{1,0:T(8,128)S(1)}, u32[]{:S(2)}, u32[]{:S(2)}) collective-permute-start(f32[48,128]{1,0:T(8,128)S(1)} %add.196), channel_id=1, source_target_pairs={{0,128},{16,144},{32,160},{48,176},{64,192},{80,208},{96,224},{112... | collective-permute-start | bytes 73736 | tf_op jit(solution)/shard_map/ppermute | solution.py:41
  192.1 3.0 %collective-permute-done.3 = f32[48,128]{1,0:T(8,128)S(1)} collective-permute-done((f32[48,128]{1,0:T(8,128)S(1)}, f32[48,128]{1,0:T(8,128)S(1)}, u32[]{:S(2)}, u32[]{:S(2)}) %collective-permute-start.3) | collective-permute-done | bytes 24608 | tf_op jit(solution)/shard_map/ppermute | solution.py:41
  195.1 5.1 %collective-permute-start.4 = (f32[48,128]{1,0:T(8,128)S(1)}, f32[48,128]{1,0:T(8,128)S(1)}, u32[]{:S(2)}, u32[]{:S(2)}) collective-permute-start(f32[48,128]{1,0:T(8,128)S(1)} %add.197), channel_id=1, source_target_pairs={{0,256},{16,272},{32,288},{48,304},{64,320},{80,336},{96,352},{112... | collective-permute-start | bytes 73736 | tf_op jit(solution)/shard_map/ppermute | solution.py:41
  200.2 4.5 %collective-permute-done.4 = f32[48,128]{1,0:T(8,128)S(1)} collective-permute-done((f32[48,128]{1,0:T(8,128)S(1)}, f32[48,128]{1,0:T(8,128)S(1)}, u32[]{:S(2)}, u32[]{:S(2)}) %collective-permute-start.4) | collective-permute-done | bytes 24608 | tf_op jit(solution)/shard_map/ppermute | solution.py:41
  204.8 0.6 add_multiply_fusion
  205.4 0.7 reduce_sum.49
  (42 shorter events, 1.2 us)
Async XLA Ops:
  7.2 40.3 %copy-start = (f32[64]{0:T(128)S(1)}, f32[64]{0:T(128)}, u32[]{:S(2)}) copy-start(f32[64]{0:T(128)} %param.10) | copy-start | bytes 772
  7.2 36.7 %copy-start.1 = (s32[32]{0:T(128)S(1)}, s32[32]{0:T(128)}, u32[]{:S(2)}) copy-start(s32[32]{0:T(128)} %param.13) | copy-start | bytes 388
  7.2 37.0 %copy-start.4 = (s32[12,2]{0,1:T(2,128)S(1)}, s32[12,2]{0,1:T(2,128)}, u32[]{:S(2)}) copy-start(s32[12,2]{0,1:T(2,128)} %param.15) | copy-start | bytes 292
  7.2 110.6 %all-gather.2.cloned.1.call-start = ((), (), s32[]{:S(2)}) async-start(), calls=%async_computation.2 | async-start | bytes 7962624 | tf_op jit(solution)/shard_map/all_gather | solution.py:14
  33.4 25.5 %all-to-all-start = ((bf16[16,3,48,128]{3,2,1,0:T(8,128)(2,1)}), bf16[16,3,48,128]{3,2,1,0:T(8,128)(2,1)S(1)}, u32[]{:S(2)}, u32[]{:S(2)}) async-start(bf16[16,3,48,128]{3,2,1,0:T(8,128)(2,1)} %broadcast_in_dim.20), calls=%async_computation | async-start | bytes 1179648 | tf_op jit(solution)/shard_map/all_to_all | solution.py:20
  44.4 0.7 copy-start.2
  47.4 3.0 %copy-start.6 = (f32[48]{0:T(128)S(1)}, f32[48]{0:T(128)}, u32[]{:S(2)}) copy-start(f32[48]{0:T(128)} %param.11) | copy-start | bytes 580
  47.5 4.7 %copy-start.5 = (f32[128]{0:T(128)S(1)}, f32[128]{0:T(128)}, u32[]{:S(2)}) copy-start(f32[128]{0:T(128)} %param.12) | copy-start | bytes 1540
  125.7 1.1 copy-start.3
  138.1 67.3 %all-to-all-start.1 = ((f32[16,48,3,128]{3,1,2,0:T(8,128)}), f32[16,48,3,128]{3,1,2,0:T(8,128)S(1)}, u32[]{:S(2)}, u32[]{:S(2)}) async-start(f32[16,48,3,128]{3,1,2,0:T(8,128)} %copy.69), calls=%async_computation.1 | async-start | bytes 2359296 | tf_op jit(solution)/shard_map/all_to_all | solution.py:32
  148.5 27.7 %collective-permute-start = (f32[48,128]{1,0:T(8,128)S(1)}, f32[48,128]{1,0:T(8,128)S(1)}, u32[]{:S(2)}, u32[]{:S(2)}) collective-permute-start(f32[48,128]{1,0:T(8,128)S(1)} %get-tuple-element.3), channel_id=1, source_target_pairs={{0,16},{16,0},{32,48},{48,32},{64,80},{80,64},{96,112},{112,96},{1... | collective-permute-start | bytes 73736 | tf_op jit(solution)/shard_map/ppermute | solution.py:41
  176.2 6.6 %collective-permute-start.1 = (f32[48,128]{1,0:T(8,128)S(1)}, f32[48,128]{1,0:T(8,128)S(1)}, u32[]{:S(2)}, u32[]{:S(2)}) collective-permute-start(f32[48,128]{1,0:T(8,128)S(1)} %add.194), channel_id=1, source_target_pairs={{0,32},{16,48},{32,0},{48,16},{64,96},{80,112},{96,64},{112,80},{1... | collective-permute-start | bytes 73736 | tf_op jit(solution)/shard_map/ppermute | solution.py:41
  182.8 5.7 %collective-permute-start.2 = (f32[48,128]{1,0:T(8,128)S(1)}, f32[48,128]{1,0:T(8,128)S(1)}, u32[]{:S(2)}, u32[]{:S(2)}) collective-permute-start(f32[48,128]{1,0:T(8,128)S(1)} %add.195), channel_id=1, source_target_pairs={{0,64},{16,80},{32,96},{48,112},{64,0},{80,16},{96,32},{112,48},{1... | collective-permute-start | bytes 73736 | tf_op jit(solution)/shard_map/ppermute | solution.py:41
  188.5 6.6 %collective-permute-start.3 = (f32[48,128]{1,0:T(8,128)S(1)}, f32[48,128]{1,0:T(8,128)S(1)}, u32[]{:S(2)}, u32[]{:S(2)}) collective-permute-start(f32[48,128]{1,0:T(8,128)S(1)} %add.196), channel_id=1, source_target_pairs={{0,128},{16,144},{32,160},{48,176},{64,192},{80,208},{96,224},{112... | collective-permute-start | bytes 73736 | tf_op jit(solution)/shard_map/ppermute | solution.py:41
  195.1 9.6 %collective-permute-start.4 = (f32[48,128]{1,0:T(8,128)S(1)}, f32[48,128]{1,0:T(8,128)S(1)}, u32[]{:S(2)}, u32[]{:S(2)}) collective-permute-start(f32[48,128]{1,0:T(8,128)S(1)} %add.197), channel_id=1, source_target_pairs={{0,256},{16,272},{32,288},{48,304},{64,320},{80,336},{96,352},{112... | collective-permute-start | bytes 73736 | tf_op jit(solution)/shard_map/ppermute | solution.py:41
Sparse Core Ops, SparseCore 0:
  31.8 85.9 all-gather.1

commit v3 on v2

--- a/solution.py
+++ b/solution.py
@@ -31,6 +31,28 @@
     pieces = jnp.moveaxis(x.reshape(*before, lax.axis_size(axis), -1, *after), dim, 0)
     arrived = lax.all_to_all(pieces, axis, split_axis=0, concat_axis=0, tiled=True)
     return arrived.sum(axis=0)
+
+
+def reduce_tails(grad, dens, vir_bits, tri_bits):
+    vir_count = lax.axis_size("vir")
+    tri_count = lax.axis_size(TRI)
+    nbits = vir_count.bit_length() - 1
+    me = lax.axis_index("vir")
+    grad = grad.reshape((2,) * nbits + grad.shape[1:])
+    for r in range(max(len(vir_bits), len(tri_bits))):
+        if r < len(vir_bits):
+            bit = vir_bits[r]
+            dim = nbits - 1 - bit
+            mine = (me >> bit) & 1
+            keep = lax.dynamic_index_in_dim(grad, mine, axis=dim, keepdims=True)
+            send = lax.dynamic_index_in_dim(grad, 1 - mine, axis=dim, keepdims=True)
+            perm = [(i, i ^ (1 << bit)) for i in range(vir_count)]
+            grad = keep + lax.ppermute(send, "vir", perm)
+        if r < len(tri_bits):
+            bit = tri_bits[r]
+            perm = [(i, i ^ (1 << bit)) for i in range(tri_count)]
+            dens = dens + lax.ppermute(dens, TRI, perm)
+    return grad.reshape(grad.shape[nbits:]), dens
 
 
 def butterfly_sum(x, axes):
@@ -95,10 +117,11 @@
     left_rows = picked.reshape(npair, 2, BMAX, nv, -1)[:, 0]
     grad = jnp.einsum("qiad,qiakm->dkm", left_rows, hi, preferred_element_type=f32)
     grad = grad + jnp.einsum("qiad,qiakm->dkm", left_rows, lo, preferred_element_type=f32)
-    grad = sent_and_summed(grad, "vir", 0)
+    vir_count = lax.axis_size("vir")
+    grad = grad.reshape(vir_count, -1, grad.shape[1], grad.shape[2])
+    grad, density = reduce_tails(grad, dens_part, (0, 2, 3, 1), (0, 1, 2, 3, 4))
     grad = jnp.transpose(grad, (1, 0, 2))
-
-    density = butterfly_sum(dens_part, TRI) / float(tri_count * npair)
+    density = density / float(tri_count * npair)
     return density, grad
 
 

time: 214 us -> 206 us (0.963)
  waiting for transfers between devices: 105 us -> 87.4 us
  starting transfers between devices: 36.1 us -> 45.4 us
    ppermute x5 -> x9, starting transfers between devices: 15.2 us -> 34.9 us  [the longest x5 18.9 us: reduce_tails(): dens = dens + lax.ppermute(dens, TRI, perm)]
    ppermute x5 -> x9, waiting for transfers between devices: 41 us -> 23 us  [the longest x4 12.2 us: reduce_tails(): grad = keep + lax.ppermute(send, 'vir', perm)]
    all_to_all x1 -> x0, starting transfers between devices: 10.4 us -> none  [sent_and_summed(): lax.all_to_all(pieces, axis, split_axis=0, concat_axis=0, tiled=True)]
  transfers between devices with their start and end apart: 8 -> 11, of which waited for: 7 -> 9; matrix products, arithmetic and copies ran while one was open for 5% -> 6% of each run, Pallas kernels for 0% -> 0%
where the time goes in v3:
time: 206 us; the launch traced here: 204 us
  waiting for transfers between devices  87.4 us (42%)
  starting transfers between devices  45.4 us (22%)
  blocking collectives  24.5 us (12%)
  between operations  14.5 us (7%)
  matrix products  14.1 us (7%)
  local copies, waits for them, and re-layouts  9.82 us (5%)
  other arithmetic  7.85 us (4%)
    all_gather x1, waiting for transfers between devices, whole_of(): nearer = lax.all_gather(x, axes[-1], axis=dim, tiled=True)  58 us
    all_gather x1, blocking collectives, whole_of(): nearer = lax.all_gather(x, axes[-1], axis=dim, tiled=True)  24.5 us
    ppermute x5, starting transfers between devices, reduce_tails(): dens = dens + lax.ppermute(dens, TRI, perm)  18.9 us
    ppermute x4, starting transfers between devices, reduce_tails(): grad = keep + lax.ppermute(send, 'vir', perm)  16.1 us
    ppermute x4, waiting for transfers between devices, reduce_tails(): grad = keep + lax.ppermute(send, 'vir', perm)  12.2 us
    ppermute x5, waiting for transfers between devices, reduce_tails(): dens = dens + lax.ppermute(dens, TRI, perm)  10.8 us
    all_to_all x1, starting transfers between devices, from_everyone(): return lax.all_to_all(copies, axis, split_axis=0, concat_axis=0, tiled=True)  10.4 us
    dot_general x1, matrix products, body(): jnp.einsum('rb,bad->rad', pick, everything, preferred_element_type=bf16)  7.92 us
  transfers between devices with their start and end apart: 11, of which 9 were waited for; matrix products, arithmetic and copies ran while one was open for 6% of the time, Pallas kernels for 0%

profile of v3, /device:TPU:6, one launch (start us, length us, event | category | flops | bytes accessed | tf_op | source)
XLA Modules:
  0.0 203.5 jit_solution(12118059712926368234)
XLA Ops:
  7.2 24.5 %all_gather.6 = bf16[12,48,768]{2,1,0:T(8,128)(2,1)} all-gather(bf16[3,48,768]{2,1,0:T(8,128)(2,1)} %param.8), channel_id=1, replica_groups=mesh['tri_0'=8,'tri_1'=4,'vir'=16] {'tri_1'}, dimensions={0}, use_global_device_ids=true | all-gather | bytes 1105920 | tf_op jit(solution)/shard_map/all_gather | solution.py:14
  31.8 1.7 broadcast_in_dim.20
  33.5 10.4 %all-to-all-start = ((bf16[16,3,48,128]{3,2,1,0:T(8,128)(2,1)}), bf16[16,3,48,128]{3,2,1,0:T(8,128)(2,1)S(1)}, u32[]{:S(2)}, u32[]{:S(2)}) async-start(bf16[16,3,48,128]{3,2,1,0:T(8,128)(2,1)} %broadcast_in_dim.20), calls=%async_computation | async-start | bytes 1179648 | tf_op jit(solution)/shard_map/all_to_all | solution.py:20
  44.1 0.1 reduce
  44.4 0.7 gather_fusion
  45.1 0.7 gather_fusion.1
  45.8 0.6 fusion.14
  46.4 0.7 gather_fusion.3
  47.3 0.1 reshape.195
  47.5 1.2 gather_fusion.4
  48.7 0.1 reshape.194
  48.8 0.7 fusion.16
  49.5 0.6 gather_fusion.2
  51.0 0.1 add.216
  51.1 0.1 copy.62
  51.2 0.1 copy.61
  51.3 0.7 iota_compare_fusion.2
  52.1 0.1 broadcast_and_fusion
  52.3 0.2 broadcast_add_fusion
  52.5 6.4 %all-to-all-done = bf16[16,3,48,128]{3,2,1,0:T(8,128)(2,1)S(1)} async-done(((bf16[16,3,48,128]{3,2,1,0:T(8,128)(2,1)}), bf16[16,3,48,128]{3,2,1,0:T(8,128)(2,1)S(1)}, u32[]{:S(2)}, u32[]{:S(2)}) %all-to-all-start) | async-done | bytes 589856 | tf_op jit(solution)/shard_map/all_to_all | solution.py:20
  58.9 0.9 copy.65
  59.8 58.0 %all-gather.2.cloned.1.call-done = bf16[96,48,768]{2,1,0:T(8,128)(2,1)} async-done(((bf16[12,48,768]{2,1,0:T(8,128)(2,1)}), bf16[96,48,768]{2,1,0:T(8,128)(2,1)}) %all-gather.2.cloned.1.call-update) | async-done | bytes 7077904 | tf_op jit(solution)/shard_map/all_gather | solution.py:14
  117.8 7.9 %fusion = bf16[72,48,768]{2,0,1:T(8,128)(2,1)S(1)} fusion(bf16[96,48,768]{2,1,0:T(8,128)(2,1)} %all-gather.2.cloned.1.call-done, s32[72]{0:T(128)S(1)} %add.216), kind=kOutput, calls=%fused_computation.7 | convolution fusion | flops 509614848 | bytes 12386592 | tf_op jit(solution)/shard_map/rb,bad->rad/dot_general | solution.py:93
  125.7 1.0 copy.64
  126.8 2.9 %fusion.18 = f32[12,2,3,48,3,128]{5,3,4,2,1,0:T(8,128)S(1)} fusion(bf16[12,2,3,48,768,1]{4,3,5,2,1,0:T(8,128)(2,1)S(1)} %bitcast.60, bf16[3,768,128,1,1,1]{2,1,0,5,4,3:T(8,128)(2,1)S(1)} %bitcast.65), kind=kOutput, calls=%fused_computation.59 | convolution fusion | flops 2038431744 | bytes 11206656 | tf_op jit(solution)/shard_map/rad,kdm->rakm/dot_general | solution.py:94
  129.7 0.5 slice_bitcast_fusion.1
  130.2 3.1 %fusion.2 = (f32[12,3,48,3,128]{4,2,3,1,0:T(8,128)S(1)}, f32[48,128]{1,0:T(8,128)S(1)}) fusion(f32[12,3]{1,0:T(8,128)S(1)} %copy.70, f32[12,3,48,3,128]{4,2,3,1,0:T(8,128)S(1)} %broadcast_add_fusion, f32[12,3,48,3,128]{4,2,3,1,0:T(8,128)S(1)} %get-tuple-element.8, f32[12,3,48,3,128]{4,2,3,1,0:T(8,128)S(1)} %get-tuple-element.7, ...), kind=kLoop, calls=%fused_computation.9 | loop fusion | flops 13264896 | bytes 10641876 | tf_op jit(solution)/shard_map/reduce_sum | solution.py:112
  133.3 0.4 fusion.3
  133.7 1.6 fusion.6
  135.4 1.7 fusion.8
  137.2 1.9 collective-permute-start.5
  139.1 2.0 collective-permute-done.5
  141.2 2.8 %collective-permute-start.6 = (f32[2,1,2,1,48,3,128]{6,4,5,3,2,1,0:T(8,128)S(1)}, f32[2,1,2,1,48,3,128]{6,4,5,3,2,1,0:T(8,128)S(1)}, u32[]{:S(2)}, u32[]{:S(2)}) collective-permute-start(f32[2,1,2,1,48,3,128]{6,4,5,3,2,1,0:T(8,128)S(1)} %constant_dynamic-slice_fusion.2), channel_id=1, source_target_pairs={{0,4},{1,5},{2,6},{3,7},{4,0},{5,1},{6,2},{7,3},{8,12},{9,13},{10,... | collective-permute-start | bytes 884744 | tf_op jit(solution)/shard_map/ppermute | solution.py:50
  143.9 8.2 %collective-permute-done.6 = f32[2,1,2,1,48,3,128]{6,4,5,3,2,1,0:T(8,128)S(1)} collective-permute-done((f32[2,1,2,1,48,3,128]{6,4,5,3,2,1,0:T(8,128)S(1)}, f32[2,1,2,1,48,3,128]{6,4,5,3,2,1,0:T(8,128)S(1)}, u32[]{:S(2)}, u32[]{:S(2)}) %collective-permute-start.6) | collective-permute-done | bytes 294944 | tf_op jit(solution)/shard_map/ppermute | solution.py:50
  152.2 3.4 %collective-permute-start.7 = (f32[1,1,2,1,48,3,128]{6,4,5,3,2,1,0:T(8,128)S(1)}, f32[1,1,2,1,48,3,128]{6,4,5,3,2,1,0:T(8,128)S(1)}, u32[]{:S(2)}, u32[]{:S(2)}) collective-permute-start(f32[1,1,2,1,48,3,128]{6,4,5,3,2,1,0:T(8,128)S(1)} %constant_dynamic-slice_fusion.1), channel_id=1, source_target_pairs={{0,8},{1,9},{2,10},{3,11},{4,12},{5,13},{6,14},{7,15},{8,0},{9,1},... | collective-permute-start | bytes 442376 | tf_op jit(solution)/shard_map/ppermute | solution.py:50
  155.5 3.6 %collective-permute-start = (f32[48,128]{1,0:T(8,128)S(1)}, f32[48,128]{1,0:T(8,128)S(1)}, u32[]{:S(2)}, u32[]{:S(2)}) collective-permute-start(f32[48,128]{1,0:T(8,128)S(1)} %get-tuple-element.3), channel_id=1, source_target_pairs={{0,16},{16,0},{32,48},{48,32},{64,80},{80,64},{96,112},{112,96},{1... | collective-permute-start | bytes 73736 | tf_op jit(solution)/shard_map/ppermute | solution.py:54
  159.1 2.2 %collective-permute-done = f32[48,128]{1,0:T(8,128)S(1)} collective-permute-done((f32[48,128]{1,0:T(8,128)S(1)}, f32[48,128]{1,0:T(8,128)S(1)}, u32[]{:S(2)}, u32[]{:S(2)}) %collective-permute-start) | collective-permute-done | bytes 24608 | tf_op jit(solution)/shard_map/ppermute | solution.py:54
  161.3 4.6 %collective-permute-start.1 = (f32[48,128]{1,0:T(8,128)S(1)}, f32[48,128]{1,0:T(8,128)S(1)}, u32[]{:S(2)}, u32[]{:S(2)}) collective-permute-start(f32[48,128]{1,0:T(8,128)S(1)} %add.238), channel_id=1, source_target_pairs={{0,32},{16,48},{32,0},{48,16},{64,96},{80,112},{96,64},{112,80},{1... | collective-permute-start | bytes 73736 | tf_op jit(solution)/shard_map/ppermute | solution.py:54
  165.9 2.0 collective-permute-done.1
  167.9 2.0 collective-permute-start.2
  169.9 3.7 %collective-permute-done.2 = f32[48,128]{1,0:T(8,128)S(1)} collective-permute-done((f32[48,128]{1,0:T(8,128)S(1)}, f32[48,128]{1,0:T(8,128)S(1)}, u32[]{:S(2)}, u32[]{:S(2)}) %collective-permute-start.2) | collective-permute-done | bytes 24608 | tf_op jit(solution)/shard_map/ppermute | solution.py:54
  173.6 3.6 %collective-permute-start.3 = (f32[48,128]{1,0:T(8,128)S(1)}, f32[48,128]{1,0:T(8,128)S(1)}, u32[]{:S(2)}, u32[]{:S(2)}) collective-permute-start(f32[48,128]{1,0:T(8,128)S(1)} %add.240), channel_id=1, source_target_pairs={{0,128},{16,144},{32,160},{48,176},{64,192},{80,208},{96,224},{112... | collective-permute-start | bytes 73736 | tf_op jit(solution)/shard_map/ppermute | solution.py:54
  177.2 3.0 %collective-permute-done.3 = f32[48,128]{1,0:T(8,128)S(1)} collective-permute-done((f32[48,128]{1,0:T(8,128)S(1)}, f32[48,128]{1,0:T(8,128)S(1)}, u32[]{:S(2)}, u32[]{:S(2)}) %collective-permute-start.3) | collective-permute-done | bytes 24608 | tf_op jit(solution)/shard_map/ppermute | solution.py:54
  180.2 5.1 %collective-permute-start.4 = (f32[48,128]{1,0:T(8,128)S(1)}, f32[48,128]{1,0:T(8,128)S(1)}, u32[]{:S(2)}, u32[]{:S(2)}) collective-permute-start(f32[48,128]{1,0:T(8,128)S(1)} %add.241), channel_id=1, source_target_pairs={{0,256},{16,272},{32,288},{48,304},{64,320},{80,336},{96,352},{112... | collective-permute-start | bytes 73736 | tf_op jit(solution)/shard_map/ppermute | solution.py:54
  185.3 8.0 %collective-permute-start.8 = (f32[1,1,1,1,48,3,128]{6,4,5,3,2,1,0:T(8,128)S(1)}, f32[1,1,1,1,48,3,128]{6,4,5,3,2,1,0:T(8,128)S(1)}, u32[]{:S(2)}, u32[]{:S(2)}) collective-permute-start(f32[1,1,1,1,48,3,128]{6,4,5,3,2,1,0:T(8,128)S(1)} %constant_dynamic-slice_fusion), channel_id=1, source_target_pairs={{0,2},{1,3},{2,0},{3,1},{4,6},{5,7},{6,4},{7,5},{8,10},{9,11},{10,... | collective-permute-start | bytes 221192 | tf_op jit(solution)/shard_map/ppermute | solution.py:50
  193.4 0.6 add_multiply_fusion
  194.0 2.0 collective-permute-done.8
  196.0 0.6 add_bitcast_fusion
  (55 shorter events, 1.9 us)
Async XLA Ops:
  7.2 40.3 %copy-start = (f32[64]{0:T(128)S(1)}, f32[64]{0:T(128)}, u32[]{:S(2)}) copy-start(f32[64]{0:T(128)} %param.10) | copy-start | bytes 772
  7.2 36.7 %copy-start.1 = (s32[32]{0:T(128)S(1)}, s32[32]{0:T(128)}, u32[]{:S(2)}) copy-start(s32[32]{0:T(128)} %param.13) | copy-start | bytes 388
  7.2 37.0 %copy-start.4 = (s32[12,2]{0,1:T(2,128)S(1)}, s32[12,2]{0,1:T(2,128)}, u32[]{:S(2)}) copy-start(s32[12,2]{0,1:T(2,128)} %param.15) | copy-start | bytes 292
  7.2 110.6 %all-gather.2.cloned.1.call-start = ((), (), s32[]{:S(2)}) async-start(), calls=%async_computation.1 | async-start | bytes 7962624 | tf_op jit(solution)/shard_map/all_gather | solution.py:14
  33.5 25.4 %all-to-all-start = ((bf16[16,3,48,128]{3,2,1,0:T(8,128)(2,1)}), bf16[16,3,48,128]{3,2,1,0:T(8,128)(2,1)S(1)}, u32[]{:S(2)}, u32[]{:S(2)}) async-start(bf16[16,3,48,128]{3,2,1,0:T(8,128)(2,1)} %broadcast_in_dim.20), calls=%async_computation | async-start | bytes 1179648 | tf_op jit(solution)/shard_map/all_to_all | solution.py:20
  44.4 0.7 copy-start.2
  47.4 3.0 %copy-start.6 = (f32[48]{0:T(128)S(1)}, f32[48]{0:T(128)}, u32[]{:S(2)}) copy-start(f32[48]{0:T(128)} %param.11) | copy-start | bytes 580
  47.5 4.7 %copy-start.5 = (f32[128]{0:T(128)S(1)}, f32[128]{0:T(128)}, u32[]{:S(2)}) copy-start(f32[128]{0:T(128)} %param.12) | copy-start | bytes 1540
  125.7 1.1 copy-start.3
  137.2 3.9 %collective-permute-start.5 = (f32[2,2,2,1,48,3,128]{6,4,5,3,2,1,0:T(8,128)S(1)}, f32[2,2,2,1,48,3,128]{6,4,5,3,2,1,0:T(8,128)S(1)}, u32[]{:S(2)}, u32[]{:S(2)}) collective-permute-start(f32[2,2,2,1,48,3,128]{6,4,5,3,2,1,0:T(8,128)S(1)} %copy.83), channel_id=1, source_target_pairs={{0,1},{1,0},{2,3},{3,2},{4,5},{5,4},{6,7},{7,6},{8,9},{9,8},{10,11... | collective-permute-start | bytes 1769480 | tf_op jit(solution)/shard_map/ppermute | solution.py:50
  141.2 10.9 %collective-permute-start.6 = (f32[2,1,2,1,48,3,128]{6,4,5,3,2,1,0:T(8,128)S(1)}, f32[2,1,2,1,48,3,128]{6,4,5,3,2,1,0:T(8,128)S(1)}, u32[]{:S(2)}, u32[]{:S(2)}) collective-permute-start(f32[2,1,2,1,48,3,128]{6,4,5,3,2,1,0:T(8,128)S(1)} %constant_dynamic-slice_fusion.2), channel_id=1, source_target_pairs={{0,4},{1,5},{2,6},{3,7},{4,0},{5,1},{6,2},{7,3},{8,12},{9,13},{10,... | collective-permute-start | bytes 884744 | tf_op jit(solution)/shard_map/ppermute | solution.py:50
  152.2 33.1 %collective-permute-start.7 = (f32[1,1,2,1,48,3,128]{6,4,5,3,2,1,0:T(8,128)S(1)}, f32[1,1,2,1,48,3,128]{6,4,5,3,2,1,0:T(8,128)S(1)}, u32[]{:S(2)}, u32[]{:S(2)}) collective-permute-start(f32[1,1,2,1,48,3,128]{6,4,5,3,2,1,0:T(8,128)S(1)} %constant_dynamic-slice_fusion.1), channel_id=1, source_target_pairs={{0,8},{1,9},{2,10},{3,11},{4,12},{5,13},{6,14},{7,15},{8,0},{9,1},... | collective-permute-start | bytes 442376 | tf_op jit(solution)/shard_map/ppermute | solution.py:50
  155.5 5.7 %collective-permute-start = (f32[48,128]{1,0:T(8,128)S(1)}, f32[48,128]{1,0:T(8,128)S(1)}, u32[]{:S(2)}, u32[]{:S(2)}) collective-permute-start(f32[48,128]{1,0:T(8,128)S(1)} %get-tuple-element.3), channel_id=1, source_target_pairs={{0,16},{16,0},{32,48},{48,32},{64,80},{80,64},{96,112},{112,96},{1... | collective-permute-start | bytes 73736 | tf_op jit(solution)/shard_map/ppermute | solution.py:54
  161.3 6.6 %collective-permute-start.1 = (f32[48,128]{1,0:T(8,128)S(1)}, f32[48,128]{1,0:T(8,128)S(1)}, u32[]{:S(2)}, u32[]{:S(2)}) collective-permute-start(f32[48,128]{1,0:T(8,128)S(1)} %add.238), channel_id=1, source_target_pairs={{0,32},{16,48},{32,0},{48,16},{64,96},{80,112},{96,64},{112,80},{1... | collective-permute-start | bytes 73736 | tf_op jit(solution)/shard_map/ppermute | solution.py:54
  167.9 5.7 %collective-permute-start.2 = (f32[48,128]{1,0:T(8,128)S(1)}, f32[48,128]{1,0:T(8,128)S(1)}, u32[]{:S(2)}, u32[]{:S(2)}) collective-permute-start(f32[48,128]{1,0:T(8,128)S(1)} %add.239), channel_id=1, source_target_pairs={{0,64},{16,80},{32,96},{48,112},{64,0},{80,16},{96,32},{112,48},{1... | collective-permute-start | bytes 73736 | tf_op jit(solution)/shard_map/ppermute | solution.py:54
  173.6 6.6 %collective-permute-start.3 = (f32[48,128]{1,0:T(8,128)S(1)}, f32[48,128]{1,0:T(8,128)S(1)}, u32[]{:S(2)}, u32[]{:S(2)}) collective-permute-start(f32[48,128]{1,0:T(8,128)S(1)} %add.240), channel_id=1, source_target_pairs={{0,128},{16,144},{32,160},{48,176},{64,192},{80,208},{96,224},{112... | collective-permute-start | bytes 73736 | tf_op jit(solution)/shard_map/ppermute | solution.py:54
  180.2 13.2 %collective-permute-start.4 = (f32[48,128]{1,0:T(8,128)S(1)}, f32[48,128]{1,0:T(8,128)S(1)}, u32[]{:S(2)}, u32[]{:S(2)}) collective-permute-start(f32[48,128]{1,0:T(8,128)S(1)} %add.241), channel_id=1, source_target_pairs={{0,256},{16,272},{32,288},{48,304},{64,320},{80,336},{96,352},{112... | collective-permute-start | bytes 73736 | tf_op jit(solution)/shard_map/ppermute | solution.py:54
  185.3 10.7 %collective-permute-start.8 = (f32[1,1,1,1,48,3,128]{6,4,5,3,2,1,0:T(8,128)S(1)}, f32[1,1,1,1,48,3,128]{6,4,5,3,2,1,0:T(8,128)S(1)}, u32[]{:S(2)}, u32[]{:S(2)}) collective-permute-start(f32[1,1,1,1,48,3,128]{6,4,5,3,2,1,0:T(8,128)S(1)} %constant_dynamic-slice_fusion), channel_id=1, source_target_pairs={{0,2},{1,3},{2,0},{3,1},{4,6},{5,7},{6,4},{7,5},{8,10},{9,11},{10,... | collective-permute-start | bytes 221192 | tf_op jit(solution)/shard_map/ppermute | solution.py:50
Sparse Core Ops, SparseCore 0:
  31.9 85.8 all-gather.1

commit v4 on v3

--- a/solution.py
+++ b/solution.py
@@ -86,12 +86,25 @@
     pair_live = slots < block_sizes[triples][..., None]
     rows = pair_root[..., None] * BMAX + slots
 
-    everything = whole_of(amps, TRI, 0)
+    split = (amps.shape[2] * 2) // 3
+    first_half = whole_of(amps[:, :, :split], TRI, 0)
+    across = lax.all_gather(amps[:, :, split:], "tri_0", axis=0, tiled=True)
+    second_half = joined_along(from_everyone(across, "tri_1"), 0)
     table = joined_along(from_everyone(vvvo, "vir"), 1)
 
-    pick = (rows.reshape(-1)[:, None] == jnp.arange(nrow, dtype=jnp.int32)).astype(bf16)
-    picked = jnp.einsum("rb,bad->rad", pick, everything, preferred_element_type=bf16)
-    proj = jnp.einsum("rad,kdm->rakm", picked, table, preferred_element_type=f32)
+    tri_lo = lax.axis_size("tri_1")
+    tri_hi = lax.axis_size("tri_0")
+    flat_rows = rows.reshape(-1)
+    swapped_rows = (
+        (pair_root % tri_lo)[..., None] * (tri_hi * BMAX) + (pair_root // tri_lo)[..., None] * BMAX + slots
+    ).reshape(-1)
+    row_ids = jnp.arange(nrow, dtype=jnp.int32)
+    pick_a = (flat_rows[:, None] == row_ids).astype(bf16)
+    pick_b = (swapped_rows[:, None] == row_ids).astype(bf16)
+    picked_a = jnp.einsum("rb,bad->rad", pick_a, first_half, preferred_element_type=bf16)
+    picked_b = jnp.einsum("rb,bad->rad", pick_b, second_half, preferred_element_type=bf16)
+    proj = jnp.einsum("rad,kdm->rakm", picked_a, table[:, :split], preferred_element_type=f32)
+    proj = proj + jnp.einsum("rad,kdm->rakm", picked_b, table[:, split:], preferred_element_type=f32)
     nv, nk, nm = proj.shape[1], proj.shape[2], proj.shape[3]
     proj = proj.reshape(npair, 2, BMAX, nv, nk, nm)
     left, right = proj[:, 0], proj[:, 1]
@@ -114,9 +127,12 @@
     hi_f32 = lax.reduce_precision(summed, exponent_bits=8, mantissa_bits=7)
     hi = hi_f32.astype(bf16)
     lo = (summed - hi_f32).astype(bf16)
-    left_rows = picked.reshape(npair, 2, BMAX, nv, -1)[:, 0]
-    grad = jnp.einsum("qiad,qiakm->dkm", left_rows, hi, preferred_element_type=f32)
-    grad = grad + jnp.einsum("qiad,qiakm->dkm", left_rows, lo, preferred_element_type=f32)
+    def grad_of(picked):
+        left_rows = picked.reshape(npair, 2, BMAX, nv, -1)[:, 0]
+        g = jnp.einsum("qiad,qiakm->dkm", left_rows, hi, preferred_element_type=f32)
+        return g + jnp.einsum("qiad,qiakm->dkm", left_rows, lo, preferred_element_type=f32)
+
+    grad = jnp.concatenate([grad_of(picked_a), grad_of(picked_b)], axis=0)
     vir_count = lax.axis_size("vir")
     grad = grad.reshape(vir_count, -1, grad.shape[1], grad.shape[2])
     grad, density = reduce_tails(grad, dens_part, (0, 2, 3, 1), (0, 1, 2, 3, 4))

time: 206 us -> 221 us (1.073)
  blocking collectives: 24.5 us -> 49.1 us
  waiting for transfers between devices: 87.4 us -> 64.6 us
  local copies, waits for them, and re-layouts: 9.82 us -> 17.2 us
  starting transfers between devices: 45.4 us -> 48.5 us
    all_gather x1, waiting for transfers between devices: 58 us -> 0.01 us  [whole_of(): nearer = lax.all_gather(x, axes[-1], axis=dim, tiled=True)]
    all_to_all x1 -> x2, waiting for transfers between devices: 6.39 us -> 38.8 us  [from_everyone(): return lax.all_to_all(copies, axis, split_axis=0, concat_axis=0, tiled=True)]
    all_gather x0 -> x1, blocking collectives: none -> 29.7 us  [body(): across = lax.all_gather(amps[:, :, split:], 'tri_0', axis=0, tiled=True)]
    all_to_all x1 -> x2, starting transfers between devices: 10.4 us -> 15.9 us  [from_everyone(): return lax.all_to_all(copies, axis, split_axis=0, concat_axis=0, tiled=True)]
    all_gather x1, blocking collectives: 24.5 us -> 19.3 us  [whole_of(): nearer = lax.all_gather(x, axes[-1], axis=dim, tiled=True)]
    ppermute x5, waiting for transfers between devices: 10.8 us -> 13.9 us  [reduce_tails(): dens = dens + lax.ppermute(dens, TRI, perm)]
    dot_general x4 -> x8, matrix products: 14.1 us -> 15.6 us  [the longest x1 8.18 us: body(): jnp.einsum('rb,bad->rad', pick_a, first_half, preferred_element_type=bf16)]
  transfers between devices with their start and end apart: 11 -> 12, of which waited for: 9 -> 8; matrix products, arithmetic and copies ran while one was open for 6% -> 8% of each run, Pallas kernels for 0% -> 0%
where the time goes in v4:
time: 221 us; the launch traced here: 219 us
  waiting for transfers between devices  64.6 us (29%)
  blocking collectives  49.1 us (22%)
  starting transfers between devices  48.5 us (22%)
  local copies, waits for them, and re-layouts  17.2 us (8%)
  matrix products  15.6 us (7%)
  between operations  14.5 us (7%)
  other arithmetic  9.73 us (4%)
    all_to_all x2, waiting for transfers between devices, from_everyone(): return lax.all_to_all(copies, axis, split_axis=0, concat_axis=0, tiled=True)  38.8 us
    all_gather x1, blocking collectives, body(): across = lax.all_gather(amps[:, :, split:], 'tri_0', axis=0, tiled=True)  29.7 us
    all_gather x1, blocking collectives, whole_of(): nearer = lax.all_gather(x, axes[-1], axis=dim, tiled=True)  19.3 us
    ppermute x5, starting transfers between devices, reduce_tails(): dens = dens + lax.ppermute(dens, TRI, perm)  16.8 us
    all_to_all x2, starting transfers between devices, from_everyone(): return lax.all_to_all(copies, axis, split_axis=0, concat_axis=0, tiled=True)  15.9 us
    ppermute x4, starting transfers between devices, reduce_tails(): grad = keep + lax.ppermute(send, 'vir', perm)  15.7 us
    ppermute x5, waiting for transfers between devices, reduce_tails(): dens = dens + lax.ppermute(dens, TRI, perm)  13.9 us
    ppermute x4, waiting for transfers between devices, reduce_tails(): grad = keep + lax.ppermute(send, 'vir', perm)  11.9 us
  transfers between devices with their start and end apart: 12, of which 8 were waited for; matrix products, arithmetic and copies ran while one was open for 8% of the time, Pallas kernels for 0%

profile of v4, /device:TPU:6, one launch (start us, length us, event | category | flops | bytes accessed | tf_op | source)
XLA Modules:
  0.0 219.3 jit_solution(7311368988327687274)
XLA Ops:
  7.3 0.9 slice.38
  8.2 19.3 %all_gather.9 = bf16[12,48,512]{2,1,0:T(8,128)(2,1)} all-gather(bf16[3,48,512]{2,1,0:T(8,128)(2,1)S(1)} %slice.38), channel_id=1, replica_groups=mesh['tri_0'=8,'tri_1'=4,'vir'=16] {'tri_1'}, dimensions={0}, use_global_device_ids=true | all-gather | bytes 737280 | tf_op jit(solution)/shard_map/all_gather | solution.py:14
  27.5 1.7 broadcast_in_dim.22
  29.2 10.5 %all-to-all-start = ((bf16[16,3,48,128]{3,2,1,0:T(8,128)(2,1)}), bf16[16,3,48,128]{3,2,1,0:T(8,128)(2,1)S(1)}, u32[]{:S(2)}, u32[]{:S(2)}) async-start(bf16[16,3,48,128]{3,2,1,0:T(8,128)(2,1)} %broadcast_in_dim.22), calls=%async_computation | async-start | bytes 1179648 | tf_op jit(solution)/shard_map/all_to_all | solution.py:20
  40.2 29.7 %all_gather.11 = bf16[24,48,256]{2,1,0:T(8,128)(2,1)S(1)} all-gather(bf16[3,48,256]{2,1,0:T(8,128)(2,1)S(1)} %slice-done), channel_id=1, replica_groups=mesh['tri_0'=8,'tri_1'=4,'vir'=16] {'tri_0'}, dimensions={0}, use_global_device_ids=true | all-gather | bytes 663552 | tf_op jit(solution)/shard_map/all_gather | solution.py:91
  70.2 1.6 broadcast_in_dim.23
  71.8 5.4 %all-to-all-start.1 = ((bf16[4,24,48,256]{3,1,2,0:T(8,128)(2,1)}), bf16[4,24,48,256]{3,1,2,0:T(8,128)(2,1)S(1)}, u32[]{:S(2)}, u32[]{:S(2)}) async-start(bf16[4,24,48,256]{3,1,2,0:T(8,128)(2,1)} %broadcast_in_dim.23), calls=%async_computation.1 | async-start | bytes 4718592 | tf_op jit(solution)/shard_map/all_to_all | solution.py:20
  77.2 0.7 gather_fusion
  77.9 0.7 gather_fusion.1
  78.6 0.6 fusion.26
  79.2 0.7 gather_fusion.3
  80.3 1.4 gather_fusion.4
  82.2 0.7 fusion.28
  85.2 0.7 iota_compare_fusion.3
  86.0 0.7 broadcast_and_fusion
  86.8 1.8 broadcast_add_fusion
  88.7 38.8 %all-to-all-done.1 = bf16[4,24,48,256]{3,1,2,0:T(8,128)(2,1)S(1)} async-done(((bf16[4,24,48,256]{3,1,2,0:T(8,128)(2,1)}), bf16[4,24,48,256]{3,1,2,0:T(8,128)(2,1)S(1)}, u32[]{:S(2)}, u32[]{:S(2)}) %all-to-all-start.1) | async-done | bytes 2359328 | tf_op jit(solution)/shard_map/all_to_all | solution.py:20
  127.8 0.7 fusion.20
  128.5 1.6 copy.140
  130.1 8.2 %fusion.1 = bf16[72,48,512]{2,0,1:T(8,128)(2,1)S(1)} fusion(bf16[96,48,512]{2,1,0:T(8,128)(2,1)} %all-gather.2.cloned.1.call-done, s32[72]{0:T(128)S(1)} %add.263), kind=kOutput, calls=%fused_computation.8 | convolution fusion | flops 339745536 | bytes 8257824 | tf_op jit(solution)/shard_map/rb,bad->rad/dot_general | solution.py:104
  138.3 1.2 copy.136
  139.5 2.0 fusion.3
  141.5 1.1 convolution_add_fusion
  142.6 0.7 slice_bitcast_fusion.1
  143.3 1.1 copy-done.3
  144.4 2.7 %fusion = (f32[12,3,48,3,128]{4,2,3,1,0:T(8,128)S(1)}, f32[48,128]{1,0:T(8,128)S(1)}) fusion(f32[12,3]{1,0:T(8,128)S(1)} %copy.135, f32[12,3,48,3,128]{4,2,3,1,0:T(8,128)S(1)} %copy-done.3, f32[12,3,48,3,128]{4,2,3,1,0:T(8,128)S(1)} %get-tuple-element.8, f32[12,3,48,3,128]{4,2,3,1,0:T(8,128)S(1)} %get-tuple-element.7, pred[12,3,3,3]{3,2,1,0:T(4,128)(4,1)S(1)} %copy-done.5), kind=kLoop, calls=%fused_computation.7 | loop fusion | flops 13264896 | bytes 10641876 | tf_op jit(solution)/shard_map/reduce_sum | solution.py:125
  147.5 1.0 copy-done.4
  148.6 0.7 convolution_bitcast_fusion
  149.2 0.7 fusion.12
  149.9 1.1 fusion.9
  151.1 1.2 fusion.11
  152.5 1.9 collective-permute-start.5
  154.4 2.0 collective-permute-done.5
  156.5 2.7 %collective-permute-start.6 = (f32[2,1,2,1,48,3,128]{6,4,5,3,2,1,0:T(8,128)S(1)}, f32[2,1,2,1,48,3,128]{6,4,5,3,2,1,0:T(8,128)S(1)}, u32[]{:S(2)}, u32[]{:S(2)}) collective-permute-start(f32[2,1,2,1,48,3,128]{6,4,5,3,2,1,0:T(8,128)S(1)} %constant_dynamic-slice_fusion.2), channel_id=1, source_target_pairs={{0,4},{1,5},{2,6},{3,7},{4,0},{5,1},{6,2},{7,3},{8,12},{9,13},{10,... | collective-permute-start | bytes 884744 | tf_op jit(solution)/shard_map/ppermute | solution.py:50
  159.2 8.2 %collective-permute-done.6 = f32[2,1,2,1,48,3,128]{6,4,5,3,2,1,0:T(8,128)S(1)} collective-permute-done((f32[2,1,2,1,48,3,128]{6,4,5,3,2,1,0:T(8,128)S(1)}, f32[2,1,2,1,48,3,128]{6,4,5,3,2,1,0:T(8,128)S(1)}, u32[]{:S(2)}, u32[]{:S(2)}) %collective-permute-start.6) | collective-permute-done | bytes 294944 | tf_op jit(solution)/shard_map/ppermute | solution.py:50
  167.5 3.2 %collective-permute-start.7 = (f32[1,1,2,1,48,3,128]{6,4,5,3,2,1,0:T(8,128)S(1)}, f32[1,1,2,1,48,3,128]{6,4,5,3,2,1,0:T(8,128)S(1)}, u32[]{:S(2)}, u32[]{:S(2)}) collective-permute-start(f32[1,1,2,1,48,3,128]{6,4,5,3,2,1,0:T(8,128)S(1)} %constant_dynamic-slice_fusion.1), channel_id=1, source_target_pairs={{0,8},{1,9},{2,10},{3,11},{4,12},{5,13},{6,14},{7,15},{8,0},{9,1},... | collective-permute-start | bytes 442376 | tf_op jit(solution)/shard_map/ppermute | solution.py:50
  170.7 1.9 collective-permute-start
  172.6 3.8 %collective-permute-done = f32[48,128]{1,0:T(8,128)S(1)} collective-permute-done((f32[48,128]{1,0:T(8,128)S(1)}, f32[48,128]{1,0:T(8,128)S(1)}, u32[]{:S(2)}, u32[]{:S(2)}) %collective-permute-start) | collective-permute-done | bytes 24608 | tf_op jit(solution)/shard_map/ppermute | solution.py:54
  176.4 1.9 collective-permute-start.1
  178.3 4.7 %collective-permute-done.1 = f32[48,128]{1,0:T(8,128)S(1)} collective-permute-done((f32[48,128]{1,0:T(8,128)S(1)}, f32[48,128]{1,0:T(8,128)S(1)}, u32[]{:S(2)}, u32[]{:S(2)}) %collective-permute-start.1) | collective-permute-done | bytes 24608 | tf_op jit(solution)/shard_map/ppermute | solution.py:54
  183.0 2.9 %collective-permute-start.2 = (f32[48,128]{1,0:T(8,128)S(1)}, f32[48,128]{1,0:T(8,128)S(1)}, u32[]{:S(2)}, u32[]{:S(2)}) collective-permute-start(f32[48,128]{1,0:T(8,128)S(1)} %add.292), channel_id=1, source_target_pairs={{0,64},{16,80},{32,96},{48,112},{64,0},{80,16},{96,32},{112,48},{1... | collective-permute-start | bytes 73736 | tf_op jit(solution)/shard_map/ppermute | solution.py:54
  185.9 2.8 %collective-permute-done.2 = f32[48,128]{1,0:T(8,128)S(1)} collective-permute-done((f32[48,128]{1,0:T(8,128)S(1)}, f32[48,128]{1,0:T(8,128)S(1)}, u32[]{:S(2)}, u32[]{:S(2)}) %collective-permute-start.2) | collective-permute-done | bytes 24608 | tf_op jit(solution)/shard_map/ppermute | solution.py:54
  188.7 4.0 %collective-permute-start.3 = (f32[48,128]{1,0:T(8,128)S(1)}, f32[48,128]{1,0:T(8,128)S(1)}, u32[]{:S(2)}, u32[]{:S(2)}) collective-permute-start(f32[48,128]{1,0:T(8,128)S(1)} %add.293), channel_id=1, source_target_pairs={{0,128},{16,144},{32,160},{48,176},{64,192},{80,208},{96,224},{112... | collective-permute-start | bytes 73736 | tf_op jit(solution)/shard_map/ppermute | solution.py:54
  192.7 2.6 %collective-permute-done.3 = f32[48,128]{1,0:T(8,128)S(1)} collective-permute-done((f32[48,128]{1,0:T(8,128)S(1)}, f32[48,128]{1,0:T(8,128)S(1)}, u32[]{:S(2)}, u32[]{:S(2)}) %collective-permute-start.3) | collective-permute-done | bytes 24608 | tf_op jit(solution)/shard_map/ppermute | solution.py:54
  195.4 6.1 %collective-permute-start.4 = (f32[48,128]{1,0:T(8,128)S(1)}, f32[48,128]{1,0:T(8,128)S(1)}, u32[]{:S(2)}, u32[]{:S(2)}) collective-permute-start(f32[48,128]{1,0:T(8,128)S(1)} %add.294), channel_id=1, source_target_pairs={{0,256},{16,272},{32,288},{48,304},{64,320},{80,336},{96,352},{112... | collective-permute-start | bytes 73736 | tf_op jit(solution)/shard_map/ppermute | solution.py:54
  201.5 7.9 %collective-permute-start.8 = (f32[1,1,1,1,48,3,128]{6,4,5,3,2,1,0:T(8,128)S(1)}, f32[1,1,1,1,48,3,128]{6,4,5,3,2,1,0:T(8,128)S(1)}, u32[]{:S(2)}, u32[]{:S(2)}) collective-permute-start(f32[1,1,1,1,48,3,128]{6,4,5,3,2,1,0:T(8,128)S(1)} %constant_dynamic-slice_fusion), channel_id=1, source_target_pairs={{0,2},{1,3},{2,0},{3,1},{4,6},{5,7},{6,4},{7,5},{8,10},{9,11},{10,... | collective-permute-start | bytes 221192 | tf_op jit(solution)/shard_map/ppermute | solution.py:50
  210.1 1.7 collective-permute-done.8
  211.8 0.6 add_bitcast_fusion
  (81 shorter events, 5.9 us)
Async XLA Ops:
  7.2 73.1 %copy-start = (f32[64]{0:T(128)S(1)}, f32[64]{0:T(128)}, u32[]{:S(2)}) copy-start(f32[64]{0:T(128)} %param.10) | copy-start | bytes 772
  7.2 33.0 %slice-start = ((bf16[3,48,768]{2,1,0:T(8,128)(2,1)}), bf16[3,48,256]{2,1,0:T(8,128)(2,1)S(1)}, s32[]{:S(2)}) async-start(bf16[3,48,768]{2,1,0:T(8,128)(2,1)} %param.8), calls=%async_computation.3 | async-start | bytes 147456 | tf_op jit(solution)/shard_map/slice | solution.py:91
  7.2 32.6 %copy-start.1 = (s32[32]{0:T(128)S(1)}, s32[32]{0:T(128)}, u32[]{:S(2)}) copy-start(s32[32]{0:T(128)} %param.13) | copy-start | bytes 388
  7.2 32.8 %copy-start.7 = (s32[12,2]{0,1:T(2,128)S(1)}, s32[12,2]{0,1:T(2,128)}, u32[]{:S(2)}) copy-start(s32[12,2]{0,1:T(2,128)} %param.15) | copy-start | bytes 292
  7.2 122.9 %all-gather.2.cloned.1.call-start = ((), (), s32[]{:S(2)}) async-start(), calls=%async_computation.2 | async-start | bytes 5308416 | tf_op jit(solution)/shard_map/all_gather | solution.py:14
  29.2 40.9 %all-to-all-start = ((bf16[16,3,48,128]{3,2,1,0:T(8,128)(2,1)}), bf16[16,3,48,128]{3,2,1,0:T(8,128)(2,1)S(1)}, u32[]{:S(2)}, u32[]{:S(2)}) async-start(bf16[16,3,48,128]{3,2,1,0:T(8,128)(2,1)} %broadcast_in_dim.22), calls=%async_computation | async-start | bytes 1179648 | tf_op jit(solution)/shard_map/all_to_all | solution.py:20
  71.8 55.7 %all-to-all-start.1 = ((bf16[4,24,48,256]{3,1,2,0:T(8,128)(2,1)}), bf16[4,24,48,256]{3,1,2,0:T(8,128)(2,1)S(1)}, u32[]{:S(2)}, u32[]{:S(2)}) async-start(bf16[4,24,48,256]{3,1,2,0:T(8,128)(2,1)} %broadcast_in_dim.23), calls=%async_computation.1 | async-start | bytes 4718592 | tf_op jit(solution)/shard_map/all_to_all | solution.py:20
  77.2 0.7 copy-start.2
  80.2 5.6 %copy-start.9 = (f32[48]{0:T(128)S(1)}, f32[48]{0:T(128)}, u32[]{:S(2)}) copy-start(f32[48]{0:T(128)} %param.11) | copy-start | bytes 580
  80.3 6.5 %copy-start.8 = (f32[128]{0:T(128)S(1)}, f32[128]{0:T(128)}, u32[]{:S(2)}) copy-start(f32[128]{0:T(128)} %param.12) | copy-start | bytes 1540
  88.7 39.2 %copy-start.6 = (s32[72]{0:T(128)S(1)}, s32[72]{0:T(128)}, u32[]{:S(2)}) copy-start(s32[72]{0:T(128)} %add.268) | copy-start | bytes 868
  142.6 1.8 copy-start.3
  142.6 1.7 copy-start.5
  147.1 1.5 copy-start.4
  152.5 3.9 %collective-permute-start.5 = (f32[2,2,2,1,48,3,128]{6,4,5,3,2,1,0:T(8,128)S(1)}, f32[2,2,2,1,48,3,128]{6,4,5,3,2,1,0:T(8,128)S(1)}, u32[]{:S(2)}, u32[]{:S(2)}) collective-permute-start(f32[2,2,2,1,48,3,128]{6,4,5,3,2,1,0:T(8,128)S(1)} %copy.161), channel_id=1, source_target_pairs={{0,1},{1,0},{2,3},{3,2},{4,5},{5,4},{6,7},{7,6},{8,9},{9,8},{10,11... | collective-permute-start | bytes 1769480 | tf_op jit(solution)/shard_map/ppermute | solution.py:50
  156.5 10.9 %collective-permute-start.6 = (f32[2,1,2,1,48,3,128]{6,4,5,3,2,1,0:T(8,128)S(1)}, f32[2,1,2,1,48,3,128]{6,4,5,3,2,1,0:T(8,128)S(1)}, u32[]{:S(2)}, u32[]{:S(2)}) collective-permute-start(f32[2,1,2,1,48,3,128]{6,4,5,3,2,1,0:T(8,128)S(1)} %constant_dynamic-slice_fusion.2), channel_id=1, source_target_pairs={{0,4},{1,5},{2,6},{3,7},{4,0},{5,1},{6,2},{7,3},{8,12},{9,13},{10,... | collective-permute-start | bytes 884744 | tf_op jit(solution)/shard_map/ppermute | solution.py:50
  167.5 34.0 %collective-permute-start.7 = (f32[1,1,2,1,48,3,128]{6,4,5,3,2,1,0:T(8,128)S(1)}, f32[1,1,2,1,48,3,128]{6,4,5,3,2,1,0:T(8,128)S(1)}, u32[]{:S(2)}, u32[]{:S(2)}) collective-permute-start(f32[1,1,2,1,48,3,128]{6,4,5,3,2,1,0:T(8,128)S(1)} %constant_dynamic-slice_fusion.1), channel_id=1, source_target_pairs={{0,8},{1,9},{2,10},{3,11},{4,12},{5,13},{6,14},{7,15},{8,0},{9,1},... | collective-permute-start | bytes 442376 | tf_op jit(solution)/shard_map/ppermute | solution.py:50
  170.7 5.7 %collective-permute-start = (f32[48,128]{1,0:T(8,128)S(1)}, f32[48,128]{1,0:T(8,128)S(1)}, u32[]{:S(2)}, u32[]{:S(2)}) collective-permute-start(f32[48,128]{1,0:T(8,128)S(1)} %get-tuple-element.3), channel_id=1, source_target_pairs={{0,16},{16,0},{32,48},{48,32},{64,80},{80,64},{96,112},{112,96},{1... | collective-permute-start | bytes 73736 | tf_op jit(solution)/shard_map/ppermute | solution.py:54
  176.4 6.6 %collective-permute-start.1 = (f32[48,128]{1,0:T(8,128)S(1)}, f32[48,128]{1,0:T(8,128)S(1)}, u32[]{:S(2)}, u32[]{:S(2)}) collective-permute-start(f32[48,128]{1,0:T(8,128)S(1)} %add.291), channel_id=1, source_target_pairs={{0,32},{16,48},{32,0},{48,16},{64,96},{80,112},{96,64},{112,80},{1... | collective-permute-start | bytes 73736 | tf_op jit(solution)/shard_map/ppermute | solution.py:54
  183.0 5.7 %collective-permute-start.2 = (f32[48,128]{1,0:T(8,128)S(1)}, f32[48,128]{1,0:T(8,128)S(1)}, u32[]{:S(2)}, u32[]{:S(2)}) collective-permute-start(f32[48,128]{1,0:T(8,128)S(1)} %add.292), channel_id=1, source_target_pairs={{0,64},{16,80},{32,96},{48,112},{64,0},{80,16},{96,32},{112,48},{1... | collective-permute-start | bytes 73736 | tf_op jit(solution)/shard_map/ppermute | solution.py:54
  188.7 6.6 %collective-permute-start.3 = (f32[48,128]{1,0:T(8,128)S(1)}, f32[48,128]{1,0:T(8,128)S(1)}, u32[]{:S(2)}, u32[]{:S(2)}) collective-permute-start(f32[48,128]{1,0:T(8,128)S(1)} %add.293), channel_id=1, source_target_pairs={{0,128},{16,144},{32,160},{48,176},{64,192},{80,208},{96,224},{112... | collective-permute-start | bytes 73736 | tf_op jit(solution)/shard_map/ppermute | solution.py:54
  195.4 14.1 %collective-permute-start.4 = (f32[48,128]{1,0:T(8,128)S(1)}, f32[48,128]{1,0:T(8,128)S(1)}, u32[]{:S(2)}, u32[]{:S(2)}) collective-permute-start(f32[48,128]{1,0:T(8,128)S(1)} %add.294), channel_id=1, source_target_pairs={{0,256},{16,272},{32,288},{48,304},{64,320},{80,336},{96,352},{112... | collective-permute-start | bytes 73736 | tf_op jit(solution)/shard_map/ppermute | solution.py:54
  201.5 10.2 %collective-permute-start.8 = (f32[1,1,1,1,48,3,128]{6,4,5,3,2,1,0:T(8,128)S(1)}, f32[1,1,1,1,48,3,128]{6,4,5,3,2,1,0:T(8,128)S(1)}, u32[]{:S(2)}, u32[]{:S(2)}) collective-permute-start(f32[1,1,1,1,48,3,128]{6,4,5,3,2,1,0:T(8,128)S(1)} %constant_dynamic-slice_fusion), channel_id=1, source_target_pairs={{0,2},{1,3},{2,0},{3,1},{4,6},{5,7},{6,4},{7,5},{8,10},{9,11},{10,... | collective-permute-start | bytes 221192 | tf_op jit(solution)/shard_map/ppermute | solution.py:50
Sparse Core Ops, SparseCore 0:
  27.7 69.4 all-gather.1

commit v5 on v3

--- a/solution.py
+++ b/solution.py
@@ -86,12 +86,16 @@
     pair_live = slots < block_sizes[triples][..., None]
     rows = pair_root[..., None] * BMAX + slots
 
-    everything = whole_of(amps, TRI, 0)
+    split = amps.shape[2] // 2
+    first_half = whole_of(amps[:, :, :split], TRI, 0)
+    second_half = whole_of(amps[:, :, split:], TRI, 0)
     table = joined_along(from_everyone(vvvo, "vir"), 1)
 
     pick = (rows.reshape(-1)[:, None] == jnp.arange(nrow, dtype=jnp.int32)).astype(bf16)
-    picked = jnp.einsum("rb,bad->rad", pick, everything, preferred_element_type=bf16)
-    proj = jnp.einsum("rad,kdm->rakm", picked, table, preferred_element_type=f32)
+    picked_a = jnp.einsum("rb,bad->rad", pick, first_half, preferred_element_type=bf16)
+    picked_b = jnp.einsum("rb,bad->rad", pick, second_half, preferred_element_type=bf16)
+    proj = jnp.einsum("rad,kdm->rakm", picked_a, table[:, :split], preferred_element_type=f32)
+    proj = proj + jnp.einsum("rad,kdm->rakm", picked_b, table[:, split:], preferred_element_type=f32)
     nv, nk, nm = proj.shape[1], proj.shape[2], proj.shape[3]
     proj = proj.reshape(npair, 2, BMAX, nv, nk, nm)
     left, right = proj[:, 0], proj[:, 1]
@@ -114,9 +118,12 @@
     hi_f32 = lax.reduce_precision(summed, exponent_bits=8, mantissa_bits=7)
     hi = hi_f32.astype(bf16)
     lo = (summed - hi_f32).astype(bf16)
-    left_rows = picked.reshape(npair, 2, BMAX, nv, -1)[:, 0]
-    grad = jnp.einsum("qiad,qiakm->dkm", left_rows, hi, preferred_element_type=f32)
-    grad = grad + jnp.einsum("qiad,qiakm->dkm", left_rows, lo, preferred_element_type=f32)
+    def grad_of(picked):
+        left_rows = picked.reshape(npair, 2, BMAX, nv, -1)[:, 0]
+        g = jnp.einsum("qiad,qiakm->dkm", left_rows, hi, preferred_element_type=f32)
+        return g + jnp.einsum("qiad,qiakm->dkm", left_rows, lo, preferred_element_type=f32)
+
+    grad = jnp.concatenate([grad_of(picked_a), grad_of(picked_b)], axis=0)
     vir_count = lax.axis_size("vir")
     grad = grad.reshape(vir_count, -1, grad.shape[1], grad.shape[2])
     grad, density = reduce_tails(grad, dens_part, (0, 2, 3, 1), (0, 1, 2, 3, 4))

time: 206 us -> 218 us (1.058)
  blocking collectives: 24.5 us -> 34.7 us
  local copies, waits for them, and re-layouts: 9.82 us -> 13.6 us
  waiting for transfers between devices: 87.4 us -> 84.8 us
    all_gather x1 -> x2, blocking collectives: 24.5 us -> 34.7 us  [whole_of(): nearer = lax.all_gather(x, axes[-1], axis=dim, tiled=True)]
    unnamed x15 -> x17, local copies, waits for them, and re-layouts: 0.1 us -> 2.68 us
    dot_general x4 -> x8, matrix products: 14.1 us -> 13.2 us  [the longest x1 2.95 us: body(): jnp.einsum('rb,bad->rad', pick, second_half, preferred_element_type=bf16)]
    all_gather x1 -> x2, waiting for transfers between devices: 58 us -> 57.2 us  [whole_of(): nearer = lax.all_gather(x, axes[-1], axis=dim, tiled=True)]
  transfers between devices with their start and end apart: 11 -> 12, of which waited for: 9 -> 10; matrix products, arithmetic and copies ran while one was open for 6% -> 8% of each run, Pallas kernels for 0% -> 0%
where the time goes in v5:
time: 218 us; the launch traced here: 216 us
  waiting for transfers between devices  84.8 us (39%)
  starting transfers between devices  45.7 us (21%)
  blocking collectives  34.7 us (16%)
  between operations  14.5 us (7%)
  local copies, waits for them, and re-layouts  13.6 us (6%)
  matrix products  13.2 us (6%)
  other arithmetic  9.25 us (4%)
    all_gather x2, waiting for transfers between devices, whole_of(): nearer = lax.all_gather(x, axes[-1], axis=dim, tiled=True)  57.2 us
    all_gather x2, blocking collectives, whole_of(): nearer = lax.all_gather(x, axes[-1], axis=dim, tiled=True)  34.7 us
    ppermute x5, starting transfers between devices, reduce_tails(): dens = dens + lax.ppermute(dens, TRI, perm)  19.3 us
    ppermute x4, starting transfers between devices, reduce_tails(): grad = keep + lax.ppermute(send, 'vir', perm)  16.1 us
    ppermute x4, waiting for transfers between devices, reduce_tails(): grad = keep + lax.ppermute(send, 'vir', perm)  12.2 us
    ppermute x5, waiting for transfers between devices, reduce_tails(): dens = dens + lax.ppermute(dens, TRI, perm)  10.4 us
    all_to_all x1, starting transfers between devices, from_everyone(): return lax.all_to_all(copies, axis, split_axis=0, concat_axis=0, tiled=True)  10.3 us
    all_to_all x1, waiting for transfers between devices, from_everyone(): return lax.all_to_all(copies, axis, split_axis=0, concat_axis=0, tiled=True)  4.98 us
  transfers between devices with their start and end apart: 12, of which 10 were waited for; matrix products, arithmetic and copies ran while one was open for 8% of the time, Pallas kernels for 0%

profile of v5, /device:TPU:6, one launch (start us, length us, event | category | flops | bytes accessed | tf_op | source)
XLA Modules:
  0.0 215.8 jit_solution(398400715844222919)
XLA Ops:
  7.2 1.0 fusion.27
  8.2 18.1 %all_gather.12 = bf16[12,48,384]{2,1,0:T(8,128)(2,1)} all-gather(bf16[3,48,384]{2,1,0:T(8,128)(2,1)S(1)} %get-tuple-element.13), channel_id=1, replica_groups=mesh['tri_0'=8,'tri_1'=4,'vir'=16] {'tri_1'}, dimensions={0}, use_global_device_ids=true | all-gather | bytes 552960 | tf_op jit(solution)/shard_map/all_gather | solution.py:14
  26.4 16.6 %all_gather.14 = bf16[12,48,384]{2,1,0:T(8,128)(2,1)} all-gather(bf16[3,48,384]{2,1,0:T(8,128)(2,1)S(1)} %get-tuple-element.14), channel_id=1, replica_groups=mesh['tri_0'=8,'tri_1'=4,'vir'=16] {'tri_1'}, dimensions={0}, use_global_device_ids=true | all-gather | bytes 552960 | tf_op jit(solution)/shard_map/all_gather | solution.py:14
  43.1 1.6 broadcast_in_dim.20
  44.7 10.3 %all-to-all-start = ((bf16[16,3,48,128]{3,2,1,0:T(8,128)(2,1)}), bf16[16,3,48,128]{3,2,1,0:T(8,128)(2,1)S(1)}, u32[]{:S(2)}, u32[]{:S(2)}) async-start(bf16[16,3,48,128]{3,2,1,0:T(8,128)(2,1)} %broadcast_in_dim.20), calls=%async_computation | async-start | bytes 1179648 | tf_op jit(solution)/shard_map/all_to_all | solution.py:20
  55.5 0.7 gather_fusion
  56.2 0.7 gather_fusion.1
  56.9 0.6 fusion.24
  57.5 0.7 gather_fusion.3
  58.6 1.2 gather_fusion.4
  59.9 0.7 fusion.26
  60.6 0.6 gather_fusion.2
  62.4 0.7 iota_compare_fusion.2
  63.4 1.8 broadcast_add_fusion
  65.2 5.0 %all-to-all-done = bf16[16,3,48,128]{3,2,1,0:T(8,128)(2,1)S(1)} async-done(((bf16[16,3,48,128]{3,2,1,0:T(8,128)(2,1)}), bf16[16,3,48,128]{3,2,1,0:T(8,128)(2,1)S(1)}, u32[]{:S(2)}, u32[]{:S(2)}) %all-to-all-start) | async-done | bytes 589856 | tf_op jit(solution)/shard_map/all_to_all | solution.py:20
  70.2 10.0 %all-gather.3.cloned.1.call-done = bf16[96,48,384]{2,1,0:T(8,128)(2,1)} async-done(((bf16[12,48,384]{2,1,0:T(8,128)(2,1)}), bf16[96,48,384]{2,1,0:T(8,128)(2,1)}) %all-gather.3.cloned.1.call-update) | async-done | bytes 3538960 | tf_op jit(solution)/shard_map/all_gather | solution.py:14
  80.2 2.9 %fusion.3 = bf16[72,48,384]{2,0,1:T(8,128)(2,1)S(1)} fusion(bf16[96,48,384]{2,1,0:T(8,128)(2,1)} %all-gather.3.cloned.1.call-done, s32[72]{0:T(128)S(1)} %add.222), kind=kOutput, calls=%fused_computation.12 | convolution fusion | flops 254810880 | bytes 6193440 | tf_op jit(solution)/shard_map/rb,bad->rad/dot_general | solution.py:95
  83.1 1.8 copy.86
  85.0 47.3 %all-gather.5.cloned.1.call-done = bf16[96,48,384]{2,1,0:T(8,128)(2,1)} async-done(((bf16[12,48,384]{2,1,0:T(8,128)(2,1)}), bf16[96,48,384]{2,1,0:T(8,128)(2,1)}) %all-gather.5.cloned.1.call-update) | async-done | bytes 3538960 | tf_op jit(solution)/shard_map/all_gather | solution.py:14
  132.2 2.9 %fusion.1 = bf16[72,48,384]{2,0,1:T(8,128)(2,1)S(1)} fusion(bf16[96,48,384]{2,1,0:T(8,128)(2,1)} %all-gather.5.cloned.1.call-done, s32[72]{0:T(128)S(1)} %add.222), kind=kOutput, calls=%fused_computation.10 | convolution fusion | flops 254810880 | bytes 6193440 | tf_op jit(solution)/shard_map/rb,bad->rad/dot_general | solution.py:96
  135.5 1.8 fusion.6
  137.3 1.9 fusion.10
  139.2 0.5 slice_bitcast_fusion.1
  139.7 1.3 copy-done.3
  141.0 2.9 %fusion = (f32[12,3,48,3,128]{4,2,3,1,0:T(8,128)S(1)}, f32[48,128]{1,0:T(8,128)S(1)}) fusion(f32[12,3]{1,0:T(8,128)S(1)} %copy.85, f32[12,3,48,3,128]{4,2,3,1,0:T(8,128)S(1)} %copy-done.3, f32[12,3,48,3,128]{4,2,3,1,0:T(8,128)S(1)} %get-tuple-element.8, f32[12,3,48,3,128]{4,2,3,1,0:T(8,128)S(1)} %get-tuple-element.7, ...), kind=kLoop, calls=%fused_computation.7 | loop fusion | flops 13264896 | bytes 10641876 | tf_op jit(solution)/shard_map/reduce_sum | solution.py:116
  144.3 1.3 copy-done.4
  145.6 0.9 convolution_bitcast_fusion.2
  146.5 0.9 convolution_bitcast_fusion
  147.4 0.9 fusion.13
  148.3 0.9 fusion.14
  149.5 1.9 collective-permute-start.5
  151.4 2.0 collective-permute-done.5
  153.5 2.8 %collective-permute-start.6 = (f32[2,1,2,1,48,3,128]{6,4,5,3,2,1,0:T(8,128)S(1)}, f32[2,1,2,1,48,3,128]{6,4,5,3,2,1,0:T(8,128)S(1)}, u32[]{:S(2)}, u32[]{:S(2)}) collective-permute-start(f32[2,1,2,1,48,3,128]{6,4,5,3,2,1,0:T(8,128)S(1)} %constant_dynamic-slice_fusion.2), channel_id=1, source_target_pairs={{0,4},{1,5},{2,6},{3,7},{4,0},{5,1},{6,2},{7,3},{8,12},{9,13},{10,... | collective-permute-start | bytes 884744 | tf_op jit(solution)/shard_map/ppermute | solution.py:50
  156.3 8.2 %collective-permute-done.6 = f32[2,1,2,1,48,3,128]{6,4,5,3,2,1,0:T(8,128)S(1)} collective-permute-done((f32[2,1,2,1,48,3,128]{6,4,5,3,2,1,0:T(8,128)S(1)}, f32[2,1,2,1,48,3,128]{6,4,5,3,2,1,0:T(8,128)S(1)}, u32[]{:S(2)}, u32[]{:S(2)}) %collective-permute-start.6) | collective-permute-done | bytes 294944 | tf_op jit(solution)/shard_map/ppermute | solution.py:50
  164.5 3.4 %collective-permute-start.7 = (f32[1,1,2,1,48,3,128]{6,4,5,3,2,1,0:T(8,128)S(1)}, f32[1,1,2,1,48,3,128]{6,4,5,3,2,1,0:T(8,128)S(1)}, u32[]{:S(2)}, u32[]{:S(2)}) collective-permute-start(f32[1,1,2,1,48,3,128]{6,4,5,3,2,1,0:T(8,128)S(1)} %constant_dynamic-slice_fusion.1), channel_id=1, source_target_pairs={{0,8},{1,9},{2,10},{3,11},{4,12},{5,13},{6,14},{7,15},{8,0},{9,1},... | collective-permute-start | bytes 442376 | tf_op jit(solution)/shard_map/ppermute | solution.py:50
  167.9 3.6 %collective-permute-start = (f32[48,128]{1,0:T(8,128)S(1)}, f32[48,128]{1,0:T(8,128)S(1)}, u32[]{:S(2)}, u32[]{:S(2)}) collective-permute-start(f32[48,128]{1,0:T(8,128)S(1)} %get-tuple-element.3), channel_id=1, source_target_pairs={{0,16},{16,0},{32,48},{48,32},{64,80},{80,64},{96,112},{112,96},{1... | collective-permute-start | bytes 73736 | tf_op jit(solution)/shard_map/ppermute | solution.py:54
  171.4 2.2 %collective-permute-done = f32[48,128]{1,0:T(8,128)S(1)} collective-permute-done((f32[48,128]{1,0:T(8,128)S(1)}, f32[48,128]{1,0:T(8,128)S(1)}, u32[]{:S(2)}, u32[]{:S(2)}) %collective-permute-start) | collective-permute-done | bytes 24608 | tf_op jit(solution)/shard_map/ppermute | solution.py:54
  173.6 4.6 %collective-permute-start.1 = (f32[48,128]{1,0:T(8,128)S(1)}, f32[48,128]{1,0:T(8,128)S(1)}, u32[]{:S(2)}, u32[]{:S(2)}) collective-permute-start(f32[48,128]{1,0:T(8,128)S(1)} %add.245), channel_id=1, source_target_pairs={{0,32},{16,48},{32,0},{48,16},{64,96},{80,112},{96,64},{112,80},{1... | collective-permute-start | bytes 73736 | tf_op jit(solution)/shard_map/ppermute | solution.py:54
  178.2 2.0 collective-permute-done.1
  180.2 2.4 %collective-permute-start.2 = (f32[48,128]{1,0:T(8,128)S(1)}, f32[48,128]{1,0:T(8,128)S(1)}, u32[]{:S(2)}, u32[]{:S(2)}) collective-permute-start(f32[48,128]{1,0:T(8,128)S(1)} %add.246), channel_id=1, source_target_pairs={{0,64},{16,80},{32,96},{48,112},{64,0},{80,16},{96,32},{112,48},{1... | collective-permute-start | bytes 73736 | tf_op jit(solution)/shard_map/ppermute | solution.py:54
  182.6 3.3 %collective-permute-done.2 = f32[48,128]{1,0:T(8,128)S(1)} collective-permute-done((f32[48,128]{1,0:T(8,128)S(1)}, f32[48,128]{1,0:T(8,128)S(1)}, u32[]{:S(2)}, u32[]{:S(2)}) %collective-permute-start.2) | collective-permute-done | bytes 24608 | tf_op jit(solution)/shard_map/ppermute | solution.py:54
  185.9 3.6 %collective-permute-start.3 = (f32[48,128]{1,0:T(8,128)S(1)}, f32[48,128]{1,0:T(8,128)S(1)}, u32[]{:S(2)}, u32[]{:S(2)}) collective-permute-start(f32[48,128]{1,0:T(8,128)S(1)} %add.247), channel_id=1, source_target_pairs={{0,128},{16,144},{32,160},{48,176},{64,192},{80,208},{96,224},{112... | collective-permute-start | bytes 73736 | tf_op jit(solution)/shard_map/ppermute | solution.py:54
  189.6 3.0 %collective-permute-done.3 = f32[48,128]{1,0:T(8,128)S(1)} collective-permute-done((f32[48,128]{1,0:T(8,128)S(1)}, f32[48,128]{1,0:T(8,128)S(1)}, u32[]{:S(2)}, u32[]{:S(2)}) %collective-permute-start.3) | collective-permute-done | bytes 24608 | tf_op jit(solution)/shard_map/ppermute | solution.py:54
  192.6 5.1 %collective-permute-start.4 = (f32[48,128]{1,0:T(8,128)S(1)}, f32[48,128]{1,0:T(8,128)S(1)}, u32[]{:S(2)}, u32[]{:S(2)}) collective-permute-start(f32[48,128]{1,0:T(8,128)S(1)} %add.248), channel_id=1, source_target_pairs={{0,256},{16,272},{32,288},{48,304},{64,320},{80,336},{96,352},{112... | collective-permute-start | bytes 73736 | tf_op jit(solution)/shard_map/ppermute | solution.py:54
  197.7 8.0 %collective-permute-start.8 = (f32[1,1,1,1,48,3,128]{6,4,5,3,2,1,0:T(8,128)S(1)}, f32[1,1,1,1,48,3,128]{6,4,5,3,2,1,0:T(8,128)S(1)}, u32[]{:S(2)}, u32[]{:S(2)}) collective-permute-start(f32[1,1,1,1,48,3,128]{6,4,5,3,2,1,0:T(8,128)S(1)} %constant_dynamic-slice_fusion), channel_id=1, source_target_pairs={{0,2},{1,3},{2,0},{3,1},{4,6},{5,7},{6,4},{7,5},{8,10},{9,11},{10,... | collective-permute-start | bytes 221192 | tf_op jit(solution)/shard_map/ppermute | solution.py:50
  205.7 0.6 add_multiply_fusion
  206.3 2.0 collective-permute-done.8
  208.4 0.6 add_bitcast_fusion
  (68 shorter events, 3.6 us)
Async XLA Ops:
  7.2 51.4 %copy-start = (f32[64]{0:T(128)S(1)}, f32[64]{0:T(128)}, u32[]{:S(2)}) copy-start(f32[64]{0:T(128)} %param.10) | copy-start | bytes 772
  7.2 47.8 %copy-start.1 = (s32[32]{0:T(128)S(1)}, s32[32]{0:T(128)}, u32[]{:S(2)}) copy-start(s32[32]{0:T(128)} %param.13) | copy-start | bytes 388
  7.2 48.1 %copy-start.5 = (s32[12,2]{0,1:T(2,128)S(1)}, s32[12,2]{0,1:T(2,128)}, u32[]{:S(2)}) copy-start(s32[12,2]{0,1:T(2,128)} %param.15) | copy-start | bytes 292
  7.2 73.0 %all-gather.3.cloned.1.call-start = ((), (), s32[]{:S(2)}) async-start(), calls=%async_computation.1 | async-start | bytes 3981312 | tf_op jit(solution)/shard_map/all_gather | solution.py:14
  26.3 105.9 %all-gather.5.cloned.1.call-start = ((), (), s32[]{:S(2)}) async-start(), calls=%async_computation.2 | async-start | bytes 3981312 | tf_op jit(solution)/shard_map/all_gather | solution.py:14
  44.7 25.4 %all-to-all-start = ((bf16[16,3,48,128]{3,2,1,0:T(8,128)(2,1)}), bf16[16,3,48,128]{3,2,1,0:T(8,128)(2,1)S(1)}, u32[]{:S(2)}, u32[]{:S(2)}) async-start(bf16[16,3,48,128]{3,2,1,0:T(8,128)(2,1)} %broadcast_in_dim.20), calls=%async_computation | async-start | bytes 1179648 | tf_op jit(solution)/shard_map/all_to_all | solution.py:20
  55.5 0.7 copy-start.2
  58.6 3.0 %copy-start.7 = (f32[48]{0:T(128)S(1)}, f32[48]{0:T(128)}, u32[]{:S(2)}) copy-start(f32[48]{0:T(128)} %param.11) | copy-start | bytes 580
  58.6 4.7 %copy-start.6 = (f32[128]{0:T(128)S(1)}, f32[128]{0:T(128)}, u32[]{:S(2)}) copy-start(f32[128]{0:T(128)} %param.12) | copy-start | bytes 1540
  139.2 1.8 copy-start.3
  143.9 1.8 copy-start.4
  149.5 3.9 %collective-permute-start.5 = (f32[2,2,2,1,48,3,128]{6,4,5,3,2,1,0:T(8,128)S(1)}, f32[2,2,2,1,48,3,128]{6,4,5,3,2,1,0:T(8,128)S(1)}, u32[]{:S(2)}, u32[]{:S(2)}) collective-permute-start(f32[2,2,2,1,48,3,128]{6,4,5,3,2,1,0:T(8,128)S(1)} %copy.111), channel_id=1, source_target_pairs={{0,1},{1,0},{2,3},{3,2},{4,5},{5,4},{6,7},{7,6},{8,9},{9,8},{10,11... | collective-permute-start | bytes 1769480 | tf_op jit(solution)/shard_map/ppermute | solution.py:50
  153.5 10.9 %collective-permute-start.6 = (f32[2,1,2,1,48,3,128]{6,4,5,3,2,1,0:T(8,128)S(1)}, f32[2,1,2,1,48,3,128]{6,4,5,3,2,1,0:T(8,128)S(1)}, u32[]{:S(2)}, u32[]{:S(2)}) collective-permute-start(f32[2,1,2,1,48,3,128]{6,4,5,3,2,1,0:T(8,128)S(1)} %constant_dynamic-slice_fusion.2), channel_id=1, source_target_pairs={{0,4},{1,5},{2,6},{3,7},{4,0},{5,1},{6,2},{7,3},{8,12},{9,13},{10,... | collective-permute-start | bytes 884744 | tf_op jit(solution)/shard_map/ppermute | solution.py:50
  164.5 33.1 %collective-permute-start.7 = (f32[1,1,2,1,48,3,128]{6,4,5,3,2,1,0:T(8,128)S(1)}, f32[1,1,2,1,48,3,128]{6,4,5,3,2,1,0:T(8,128)S(1)}, u32[]{:S(2)}, u32[]{:S(2)}) collective-permute-start(f32[1,1,2,1,48,3,128]{6,4,5,3,2,1,0:T(8,128)S(1)} %constant_dynamic-slice_fusion.1), channel_id=1, source_target_pairs={{0,8},{1,9},{2,10},{3,11},{4,12},{5,13},{6,14},{7,15},{8,0},{9,1},... | collective-permute-start | bytes 442376 | tf_op jit(solution)/shard_map/ppermute | solution.py:50
  167.9 5.7 %collective-permute-start = (f32[48,128]{1,0:T(8,128)S(1)}, f32[48,128]{1,0:T(8,128)S(1)}, u32[]{:S(2)}, u32[]{:S(2)}) collective-permute-start(f32[48,128]{1,0:T(8,128)S(1)} %get-tuple-element.3), channel_id=1, source_target_pairs={{0,16},{16,0},{32,48},{48,32},{64,80},{80,64},{96,112},{112,96},{1... | collective-permute-start | bytes 73736 | tf_op jit(solution)/shard_map/ppermute | solution.py:54
  173.6 6.6 %collective-permute-start.1 = (f32[48,128]{1,0:T(8,128)S(1)}, f32[48,128]{1,0:T(8,128)S(1)}, u32[]{:S(2)}, u32[]{:S(2)}) collective-permute-start(f32[48,128]{1,0:T(8,128)S(1)} %add.245), channel_id=1, source_target_pairs={{0,32},{16,48},{32,0},{48,16},{64,96},{80,112},{96,64},{112,80},{1... | collective-permute-start | bytes 73736 | tf_op jit(solution)/shard_map/ppermute | solution.py:54
  180.2 5.7 %collective-permute-start.2 = (f32[48,128]{1,0:T(8,128)S(1)}, f32[48,128]{1,0:T(8,128)S(1)}, u32[]{:S(2)}, u32[]{:S(2)}) collective-permute-start(f32[48,128]{1,0:T(8,128)S(1)} %add.246), channel_id=1, source_target_pairs={{0,64},{16,80},{32,96},{48,112},{64,0},{80,16},{96,32},{112,48},{1... | collective-permute-start | bytes 73736 | tf_op jit(solution)/shard_map/ppermute | solution.py:54
  185.9 6.6 %collective-permute-start.3 = (f32[48,128]{1,0:T(8,128)S(1)}, f32[48,128]{1,0:T(8,128)S(1)}, u32[]{:S(2)}, u32[]{:S(2)}) collective-permute-start(f32[48,128]{1,0:T(8,128)S(1)} %add.247), channel_id=1, source_target_pairs={{0,128},{16,144},{32,160},{48,176},{64,192},{80,208},{96,224},{112... | collective-permute-start | bytes 73736 | tf_op jit(solution)/shard_map/ppermute | solution.py:54
  192.6 13.2 %collective-permute-start.4 = (f32[48,128]{1,0:T(8,128)S(1)}, f32[48,128]{1,0:T(8,128)S(1)}, u32[]{:S(2)}, u32[]{:S(2)}) collective-permute-start(f32[48,128]{1,0:T(8,128)S(1)} %add.248), channel_id=1, source_target_pairs={{0,256},{16,272},{32,288},{48,304},{64,320},{80,336},{96,352},{112... | collective-permute-start | bytes 73736 | tf_op jit(solution)/shard_map/ppermute | solution.py:54
  197.7 10.7 %collective-permute-start.8 = (f32[1,1,1,1,48,3,128]{6,4,5,3,2,1,0:T(8,128)S(1)}, f32[1,1,1,1,48,3,128]{6,4,5,3,2,1,0:T(8,128)S(1)}, u32[]{:S(2)}, u32[]{:S(2)}) collective-permute-start(f32[1,1,1,1,48,3,128]{6,4,5,3,2,1,0:T(8,128)S(1)} %constant_dynamic-slice_fusion), channel_id=1, source_target_pairs={{0,2},{1,3},{2,0},{3,1},{4,6},{5,7},{6,4},{7,5},{8,10},{9,11},{10,... | collective-permute-start | bytes 221192 | tf_op jit(solution)/shard_map/ppermute | solution.py:50
Sparse Core Ops, SparseCore 0:
  26.5 53.6 all-gather.2
  82.2 49.9 all-gather.4

commit v6 on v2

--- a/solution.py
+++ b/solution.py
@@ -6,6 +6,7 @@
 
 BMAX = 3
 TRI = ("tri_0", "tri_1")
+VIR = ("vx", "vz", "vc")
 
 
 def whole_of(x, axes, dim):
@@ -31,6 +32,25 @@
     pieces = jnp.moveaxis(x.reshape(*before, lax.axis_size(axis), -1, *after), dim, 0)
     arrived = lax.all_to_all(pieces, axis, split_axis=0, concat_axis=0, tiled=True)
     return arrived.sum(axis=0)
+
+
+def halve(x, axis, dim):
+    mine = lax.axis_index(axis)
+    keep = lax.dynamic_index_in_dim(x, mine, axis=dim, keepdims=False)
+    send = lax.dynamic_index_in_dim(x, 1 - mine, axis=dim, keepdims=False)
+    return keep + lax.ppermute(send, axis, [(0, 1), (1, 0)])
+
+
+def reduce_tails(grad, dens, tri_bits):
+    tri_count = lax.axis_size(TRI)
+    grad = halve(grad, "vc", 2)
+    for r, bit in enumerate(tri_bits):
+        perm = [(i, i ^ (1 << bit)) for i in range(tri_count)]
+        dens = dens + lax.ppermute(dens, TRI, perm)
+        if r == 0:
+            grad = lax.psum_scatter(grad, "vx", scatter_dimension=0, tiled=True)
+    grad = halve(grad[0], "vz", 0)
+    return grad, dens
 
 
 def butterfly_sum(x, axes):
@@ -65,7 +85,7 @@
     rows = pair_root[..., None] * BMAX + slots
 
     everything = whole_of(amps, TRI, 0)
-    table = joined_along(from_everyone(vvvo, "vir"), 1)
+    table = joined_along(from_everyone(vvvo, VIR), 1)
 
     pick = (rows.reshape(-1)[:, None] == jnp.arange(nrow, dtype=jnp.int32)).astype(bf16)
     picked = jnp.einsum("rb,bad->rad", pick, everything, preferred_element_type=bf16)
@@ -95,29 +115,30 @@
     left_rows = picked.reshape(npair, 2, BMAX, nv, -1)[:, 0]
     grad = jnp.einsum("qiad,qiakm->dkm", left_rows, hi, preferred_element_type=f32)
     grad = grad + jnp.einsum("qiad,qiakm->dkm", left_rows, lo, preferred_element_type=f32)
-    grad = sent_and_summed(grad, "vir", 0)
+    grad = grad.reshape(lax.axis_size("vx"), lax.axis_size("vz"), lax.axis_size("vc"), -1, grad.shape[1], grad.shape[2])
+    grad, density = reduce_tails(grad, dens_part, (0, 1, 2, 3, 4))
     grad = jnp.transpose(grad, (1, 0, 2))
-
-    density = butterfly_sum(dens_part, TRI) / float(tri_count * npair)
+    density = density / float(tri_count * npair)
     return density, grad
 
 
 def solution(mesh):
     tri_hi = mesh.shape["tri"] // 4
-    finer = Mesh(mesh.devices.reshape(tri_hi, 4, mesh.shape["vir"]), ("tri_0", "tri_1", "vir"))
+    vir_hi = mesh.shape["vir"] // 4
+    finer = Mesh(mesh.devices.reshape(tri_hi, 4, vir_hi, 2, 2), TRI + VIR)
     return jax.shard_map(
         body,
         mesh=finer,
         in_specs=(
-            P(TRI, "vir", None),
-            P(TRI, "vir", None),
+            P(TRI, VIR, None),
+            P(TRI, VIR, None),
             P(),
-            P("vir"),
+            P(VIR),
             P(),
             P(),
             P(),
             P(TRI, None),
         ),
-        out_specs=(P("vir", None), P(TRI, "vir", None)),
+        out_specs=(P(VIR, None), P(TRI, VIR, None)),
         check_vma=False,
     )

time: 214 us -> 193 us (0.902)
  waiting for transfers between devices: 105 us -> 79.1 us
  starting transfers between devices: 36.1 us -> 39.7 us
    ppermute x5 -> x7, waiting for transfers between devices: 41 us -> 14.7 us  [the longest x5 10.8 us: reduce_tails(): dens = dens + lax.ppermute(dens, TRI, perm)]
    ppermute x5 -> x7, starting transfers between devices: 15.2 us -> 29.1 us  [the longest x5 18.9 us: reduce_tails(): dens = dens + lax.ppermute(dens, TRI, perm)]
    all_to_all x1 -> x0, starting transfers between devices: 10.4 us -> none  [sent_and_summed(): lax.all_to_all(pieces, axis, split_axis=0, concat_axis=0, tiled=True)]
  transfers between devices with their start and end apart: 8 -> 10, of which waited for: 7 -> 8; matrix products, arithmetic and copies ran while one was open for 5% -> 7% of each run, Pallas kernels for 0% -> 0%
where the time goes in v6:
time: 193 us; the launch traced here: 192 us
  waiting for transfers between devices  79.1 us (41%)
  starting transfers between devices  39.7 us (21%)
  blocking collectives  24.4 us (13%)
  between operations  14.4 us (7%)
  matrix products  14.1 us (7%)
  local copies, waits for them, and re-layouts  10.7 us (6%)
  other arithmetic  9.5 us (5%)
    all_gather x1, waiting for transfers between devices, whole_of(): nearer = lax.all_gather(x, axes[-1], axis=dim, tiled=True)  58 us
    all_gather x1, blocking collectives, whole_of(): nearer = lax.all_gather(x, axes[-1], axis=dim, tiled=True)  24.4 us
    ppermute x5, starting transfers between devices, reduce_tails(): dens = dens + lax.ppermute(dens, TRI, perm)  18.9 us
    ppermute x5, waiting for transfers between devices, reduce_tails(): dens = dens + lax.ppermute(dens, TRI, perm)  10.8 us
    all_to_all x1, starting transfers between devices, from_everyone(): return lax.all_to_all(copies, axis, split_axis=0, concat_axis=0, tiled=True)  10.5 us
    ppermute x2, starting transfers between devices, halve(): return keep + lax.ppermute(send, axis, [(0, 1), (1, 0)])  10.2 us
    dot_general x1, matrix products, body(): jnp.einsum('rb,bad->rad', pick, everything, preferred_element_type=bf16)  7.92 us
    all_to_all x1, waiting for transfers between devices, from_everyone(): return lax.all_to_all(copies, axis, split_axis=0, concat_axis=0, tiled=True)  6.34 us
  transfers between devices with their start and end apart: 10, of which 8 were waited for; matrix products, arithmetic and copies ran while one was open for 7% of the time, Pallas kernels for 0%

profile of v6, /device:TPU:6, one launch (start us, length us, event | category | flops | bytes accessed | tf_op | source)
XLA Modules:
  0.0 191.8 jit_solution(7029826415322953633)
XLA Ops:
  7.2 24.4 %all_gather.6 = bf16[12,48,768]{2,1,0:T(8,128)(2,1)} all-gather(bf16[3,48,768]{2,1,0:T(8,128)(2,1)} %param.8), channel_id=1, replica_groups=mesh['tri_0'=8,'tri_1'=4,'vx'=4,'vz'=2,'vc'=2] {'tri_1'}, dimensions={0}, use_global_device_ids=true | all-gather | bytes 1105920 | tf_op jit(solution)/shard_map/all_gather | solution.py:15
  31.7 1.7 broadcast_in_dim.20
  33.4 10.5 %all-to-all-start = ((bf16[16,3,48,128]{3,2,1,0:T(8,128)(2,1)}), bf16[16,3,48,128]{3,2,1,0:T(8,128)(2,1)S(1)}, u32[]{:S(2)}, u32[]{:S(2)}) async-start(bf16[16,3,48,128]{3,2,1,0:T(8,128)(2,1)} %broadcast_in_dim.20), calls=%async_computation | async-start | bytes 1179648 | tf_op jit(solution)/shard_map/all_to_all | solution.py:21
  44.1 0.1 reduce
  44.5 0.7 gather_fusion
  45.2 0.7 gather_fusion.1
  45.9 0.6 fusion.16
  46.5 0.7 gather_fusion.3
  47.4 0.1 reshape.199
  47.5 1.2 gather_fusion.4
  48.8 0.1 reshape.198
  48.9 0.7 fusion.18
  49.6 0.6 gather_fusion.2
  50.7 0.1 copy.68
  51.0 0.1 add.196
  51.1 0.1 copy.60
  51.2 0.1 copy.59
  51.4 0.7 iota_compare_fusion.2
  52.1 0.1 broadcast_and_fusion
  52.3 0.2 broadcast_add_fusion
  52.6 6.3 %all-to-all-done = bf16[16,3,48,128]{3,2,1,0:T(8,128)(2,1)S(1)} async-done(((bf16[16,3,48,128]{3,2,1,0:T(8,128)(2,1)}), bf16[16,3,48,128]{3,2,1,0:T(8,128)(2,1)S(1)}, u32[]{:S(2)}, u32[]{:S(2)}) %all-to-all-start) | async-done | bytes 589856 | tf_op jit(solution)/shard_map/all_to_all | solution.py:21
  58.9 0.9 copy.63
  59.8 58.0 %all-gather.2.cloned.1.call-done = bf16[96,48,768]{2,1,0:T(8,128)(2,1)} async-done(((bf16[12,48,768]{2,1,0:T(8,128)(2,1)}), bf16[96,48,768]{2,1,0:T(8,128)(2,1)}) %all-gather.2.cloned.1.call-update) | async-done | bytes 7077904 | tf_op jit(solution)/shard_map/all_gather | solution.py:15
  117.8 7.9 %fusion = bf16[72,48,768]{2,0,1:T(8,128)(2,1)S(1)} fusion(bf16[96,48,768]{2,1,0:T(8,128)(2,1)} %all-gather.2.cloned.1.call-done, s32[72]{0:T(128)S(1)} %add.196), kind=kOutput, calls=%fused_computation.7 | convolution fusion | flops 509614848 | bytes 12386592 | tf_op jit(solution)/shard_map/rb,bad->rad/dot_general | solution.py:91
  125.7 1.0 copy.62
  126.8 2.9 %fusion.20 = f32[12,2,3,48,3,128]{5,3,4,2,1,0:T(8,128)S(1)} fusion(bf16[12,2,3,48,768,1]{4,3,5,2,1,0:T(8,128)(2,1)S(1)} %bitcast.71, bf16[3,768,128,1,1,1]{2,1,0,5,4,3:T(8,128)(2,1)S(1)} %bitcast.76), kind=kOutput, calls=%fused_computation.58 | convolution fusion | flops 2038431744 | bytes 11206656 | tf_op jit(solution)/shard_map/rad,kdm->rakm/dot_general | solution.py:92
  129.7 0.5 slice_bitcast_fusion.1
  130.2 3.1 %fusion.2 = (f32[12,3,48,3,128]{4,2,3,1,0:T(8,128)S(1)}, f32[48,128]{1,0:T(8,128)S(1)}) fusion(f32[12,3]{1,0:T(8,128)S(1)} %copy.68, f32[12,3,48,3,128]{4,2,3,1,0:T(8,128)S(1)} %broadcast_add_fusion, f32[12,3,48,3,128]{4,2,3,1,0:T(8,128)S(1)} %get-tuple-element.8, f32[12,3,48,3,128]{4,2,3,1,0:T(8,128)S(1)} %get-tuple-element.7, ...), kind=kLoop, calls=%fused_computation.9 | loop fusion | flops 13264896 | bytes 10641876 | tf_op jit(solution)/shard_map/reduce_sum | solution.py:110
  133.3 0.4 fusion.3
  133.7 1.6 fusion.6
  135.3 1.7 fusion.8
  137.2 1.9 %collective-permute-start.5 = (f32[4,2,48,3,128]{4,2,3,1,0:T(8,128)S(1)}, f32[4,2,48,3,128]{4,2,3,1,0:T(8,128)S(1)}, u32[]{:S(2)}, u32[]{:S(2)}) collective-permute-start(f32[4,2,48,3,128]{4,2,3,1,0:T(8,128)S(1)} %bitcast.77), channel_id=1, source_target_pairs={{0,1},{1,0},{2,3},{3,2},{4,5},{5,4},{6,7},{7,6},{8,9},{9,8},{10,11... | collective-permute-start | bytes 1769480 | tf_op jit(solution)/shard_map/ppermute | solution.py:41
  139.1 2.0 %collective-permute-done.5 = f32[4,2,48,3,128]{4,2,3,1,0:T(8,128)S(1)} collective-permute-done((f32[4,2,48,3,128]{4,2,3,1,0:T(8,128)S(1)}, f32[4,2,48,3,128]{4,2,3,1,0:T(8,128)S(1)}, u32[]{:S(2)}, u32[]{:S(2)}) %collective-permute-start.5) | collective-permute-done | bytes 589856 | tf_op jit(solution)/shard_map/ppermute | solution.py:41
  141.1 0.9 fusion.11
  142.0 3.6 %collective-permute-start = (f32[48,128]{1,0:T(8,128)S(1)}, f32[48,128]{1,0:T(8,128)S(1)}, u32[]{:S(2)}, u32[]{:S(2)}) collective-permute-start(f32[48,128]{1,0:T(8,128)S(1)} %get-tuple-element.3), channel_id=1, source_target_pairs={{0,16},{16,0},{32,48},{48,32},{64,80},{80,64},{96,112},{112,96},{1... | collective-permute-start | bytes 73736 | tf_op jit(solution)/shard_map/ppermute | solution.py:49
  145.5 2.2 %collective-permute-done = f32[48,128]{1,0:T(8,128)S(1)} collective-permute-done((f32[48,128]{1,0:T(8,128)S(1)}, f32[48,128]{1,0:T(8,128)S(1)}, u32[]{:S(2)}, u32[]{:S(2)}) %collective-permute-start) | collective-permute-done | bytes 24608 | tf_op jit(solution)/shard_map/ppermute | solution.py:49
  147.7 4.6 %collective-permute-start.1 = (f32[48,128]{1,0:T(8,128)S(1)}, f32[48,128]{1,0:T(8,128)S(1)}, u32[]{:S(2)}, u32[]{:S(2)}) collective-permute-start(f32[48,128]{1,0:T(8,128)S(1)} %add.218), channel_id=1, source_target_pairs={{0,32},{16,48},{32,0},{48,16},{64,96},{80,112},{96,64},{112,80},{1... | collective-permute-start | bytes 73736 | tf_op jit(solution)/shard_map/ppermute | solution.py:49
  152.3 2.0 %collective-permute-done.1 = f32[48,128]{1,0:T(8,128)S(1)} collective-permute-done((f32[48,128]{1,0:T(8,128)S(1)}, f32[48,128]{1,0:T(8,128)S(1)}, u32[]{:S(2)}, u32[]{:S(2)}) %collective-permute-start.1) | collective-permute-done | bytes 24608 | tf_op jit(solution)/shard_map/ppermute | solution.py:49
  154.3 2.0 %collective-permute-start.2 = (f32[48,128]{1,0:T(8,128)S(1)}, f32[48,128]{1,0:T(8,128)S(1)}, u32[]{:S(2)}, u32[]{:S(2)}) collective-permute-start(f32[48,128]{1,0:T(8,128)S(1)} %add.219), channel_id=1, source_target_pairs={{0,64},{16,80},{32,96},{48,112},{64,0},{80,16},{96,32},{112,48},{1... | collective-permute-start | bytes 73736 | tf_op jit(solution)/shard_map/ppermute | solution.py:49
  156.3 3.7 %collective-permute-done.2 = f32[48,128]{1,0:T(8,128)S(1)} collective-permute-done((f32[48,128]{1,0:T(8,128)S(1)}, f32[48,128]{1,0:T(8,128)S(1)}, u32[]{:S(2)}, u32[]{:S(2)}) %collective-permute-start.2) | collective-permute-done | bytes 24608 | tf_op jit(solution)/shard_map/ppermute | solution.py:49
  160.0 3.6 %collective-permute-start.3 = (f32[48,128]{1,0:T(8,128)S(1)}, f32[48,128]{1,0:T(8,128)S(1)}, u32[]{:S(2)}, u32[]{:S(2)}) collective-permute-start(f32[48,128]{1,0:T(8,128)S(1)} %add.220), channel_id=1, source_target_pairs={{0,128},{16,144},{32,160},{48,176},{64,192},{80,208},{96,224},{112... | collective-permute-start | bytes 73736 | tf_op jit(solution)/shard_map/ppermute | solution.py:49
  163.6 3.0 %collective-permute-done.3 = f32[48,128]{1,0:T(8,128)S(1)} collective-permute-done((f32[48,128]{1,0:T(8,128)S(1)}, f32[48,128]{1,0:T(8,128)S(1)}, u32[]{:S(2)}, u32[]{:S(2)}) %collective-permute-start.3) | collective-permute-done | bytes 24608 | tf_op jit(solution)/shard_map/ppermute | solution.py:49
  166.6 5.1 %collective-permute-start.4 = (f32[48,128]{1,0:T(8,128)S(1)}, f32[48,128]{1,0:T(8,128)S(1)}, u32[]{:S(2)}, u32[]{:S(2)}) collective-permute-start(f32[48,128]{1,0:T(8,128)S(1)} %add.221), channel_id=1, source_target_pairs={{0,256},{16,272},{32,288},{48,304},{64,320},{80,336},{96,352},{112... | collective-permute-start | bytes 73736 | tf_op jit(solution)/shard_map/ppermute | solution.py:49
  171.8 0.9 dynamic-slice_bitcast_fusion
  172.7 8.3 %collective-permute-start.6 = (f32[48,3,128]{2,0,1:T(8,128)S(1)}, f32[48,3,128]{2,0,1:T(8,128)S(1)}, u32[]{:S(2)}, u32[]{:S(2)}) collective-permute-start(f32[48,3,128]{2,0,1:T(8,128)S(1)} %dynamic-slice_bitcast_fusion), channel_id=1, source_target_pairs={{0,2},{2,0},{1,3},{3,1},{4,6},{6,4},{5,7},{7,5},{8,10},{10,8},{9,1... | collective-permute-start | bytes 221192 | tf_op jit(solution)/shard_map/ppermute | solution.py:41
  181.0 0.6 add_multiply_fusion
  181.6 1.9 collective-permute-done.6
  183.5 1.5 fusion.12
  (50 shorter events, 1.7 us)
Async XLA Ops:
  7.2 40.3 %copy-start = (f32[64]{0:T(128)S(1)}, f32[64]{0:T(128)}, u32[]{:S(2)}) copy-start(f32[64]{0:T(128)} %param.10) | copy-start | bytes 772
  7.2 36.8 %copy-start.1 = (s32[32]{0:T(128)S(1)}, s32[32]{0:T(128)}, u32[]{:S(2)}) copy-start(s32[32]{0:T(128)} %param.13) | copy-start | bytes 388
  7.2 37.0 %copy-start.4 = (s32[12,2]{0,1:T(2,128)S(1)}, s32[12,2]{0,1:T(2,128)}, u32[]{:S(2)}) copy-start(s32[12,2]{0,1:T(2,128)} %param.15) | copy-start | bytes 292
  7.2 110.6 %all-gather.2.cloned.1.call-start = ((), (), s32[]{:S(2)}) async-start(), calls=%async_computation.2 | async-start | bytes 7962624 | tf_op jit(solution)/shard_map/all_gather | solution.py:15
  33.4 25.5 %all-to-all-start = ((bf16[16,3,48,128]{3,2,1,0:T(8,128)(2,1)}), bf16[16,3,48,128]{3,2,1,0:T(8,128)(2,1)S(1)}, u32[]{:S(2)}, u32[]{:S(2)}) async-start(bf16[16,3,48,128]{3,2,1,0:T(8,128)(2,1)} %broadcast_in_dim.20), calls=%async_computation | async-start | bytes 1179648 | tf_op jit(solution)/shard_map/all_to_all | solution.py:21
  43.9 127.8 %reduce-scatter.2.cloned.1.call-start = ((), (), s32[]{:S(2)}) async-start(), calls=%async_computation.3 | async-start | bytes 737280 | tf_op jit(solution)/shard_map/reduce_scatter | solution.py:51
  44.4 0.7 copy-start.2
  47.5 3.0 %copy-start.6 = (f32[48]{0:T(128)S(1)}, f32[48]{0:T(128)}, u32[]{:S(2)}) copy-start(f32[48]{0:T(128)} %param.11) | copy-start | bytes 580
  47.5 4.7 %copy-start.5 = (f32[128]{0:T(128)S(1)}, f32[128]{0:T(128)}, u32[]{:S(2)}) copy-start(f32[128]{0:T(128)} %param.12) | copy-start | bytes 1540
  125.7 1.1 copy-start.3
  137.2 3.9 %collective-permute-start.5 = (f32[4,2,48,3,128]{4,2,3,1,0:T(8,128)S(1)}, f32[4,2,48,3,128]{4,2,3,1,0:T(8,128)S(1)}, u32[]{:S(2)}, u32[]{:S(2)}) collective-permute-start(f32[4,2,48,3,128]{4,2,3,1,0:T(8,128)S(1)} %bitcast.77), channel_id=1, source_target_pairs={{0,1},{1,0},{2,3},{3,2},{4,5},{5,4},{6,7},{7,6},{8,9},{9,8},{10,11... | collective-permute-start | bytes 1769480 | tf_op jit(solution)/shard_map/ppermute | solution.py:41
  142.0 5.7 %collective-permute-start = (f32[48,128]{1,0:T(8,128)S(1)}, f32[48,128]{1,0:T(8,128)S(1)}, u32[]{:S(2)}, u32[]{:S(2)}) collective-permute-start(f32[48,128]{1,0:T(8,128)S(1)} %get-tuple-element.3), channel_id=1, source_target_pairs={{0,16},{16,0},{32,48},{48,32},{64,80},{80,64},{96,112},{112,96},{1... | collective-permute-start | bytes 73736 | tf_op jit(solution)/shard_map/ppermute | solution.py:49
  147.7 6.6 %collective-permute-start.1 = (f32[48,128]{1,0:T(8,128)S(1)}, f32[48,128]{1,0:T(8,128)S(1)}, u32[]{:S(2)}, u32[]{:S(2)}) collective-permute-start(f32[48,128]{1,0:T(8,128)S(1)} %add.218), channel_id=1, source_target_pairs={{0,32},{16,48},{32,0},{48,16},{64,96},{80,112},{96,64},{112,80},{1... | collective-permute-start | bytes 73736 | tf_op jit(solution)/shard_map/ppermute | solution.py:49
  154.3 5.7 %collective-permute-start.2 = (f32[48,128]{1,0:T(8,128)S(1)}, f32[48,128]{1,0:T(8,128)S(1)}, u32[]{:S(2)}, u32[]{:S(2)}) collective-permute-start(f32[48,128]{1,0:T(8,128)S(1)} %add.219), channel_id=1, source_target_pairs={{0,64},{16,80},{32,96},{48,112},{64,0},{80,16},{96,32},{112,48},{1... | collective-permute-start | bytes 73736 | tf_op jit(solution)/shard_map/ppermute | solution.py:49
  160.0 6.6 %collective-permute-start.3 = (f32[48,128]{1,0:T(8,128)S(1)}, f32[48,128]{1,0:T(8,128)S(1)}, u32[]{:S(2)}, u32[]{:S(2)}) collective-permute-start(f32[48,128]{1,0:T(8,128)S(1)} %add.220), channel_id=1, source_target_pairs={{0,128},{16,144},{32,160},{48,176},{64,192},{80,208},{96,224},{112... | collective-permute-start | bytes 73736 | tf_op jit(solution)/shard_map/ppermute | solution.py:49
  166.6 14.3 %collective-permute-start.4 = (f32[48,128]{1,0:T(8,128)S(1)}, f32[48,128]{1,0:T(8,128)S(1)}, u32[]{:S(2)}, u32[]{:S(2)}) collective-permute-start(f32[48,128]{1,0:T(8,128)S(1)} %add.221), channel_id=1, source_target_pairs={{0,256},{16,272},{32,288},{48,304},{64,320},{80,336},{96,352},{112... | collective-permute-start | bytes 73736 | tf_op jit(solution)/shard_map/ppermute | solution.py:49
  172.7 10.8 %collective-permute-start.6 = (f32[48,3,128]{2,0,1:T(8,128)S(1)}, f32[48,3,128]{2,0,1:T(8,128)S(1)}, u32[]{:S(2)}, u32[]{:S(2)}) collective-permute-start(f32[48,3,128]{2,0,1:T(8,128)S(1)} %dynamic-slice_bitcast_fusion), channel_id=1, source_target_pairs={{0,2},{2,0},{1,3},{3,1},{4,6},{6,4},{5,7},{7,5},{8,10},{10,8},{9,1... | collective-permute-start | bytes 221192 | tf_op jit(solution)/shard_map/ppermute | solution.py:41
Sparse Core Ops, SparseCore 0:
  31.8 85.9 all-gather.1
  142.1 24.6 reduce-scatter.1

commit v7 on v6

--- a/solution.py
+++ b/solution.py
@@ -48,9 +48,8 @@
         perm = [(i, i ^ (1 << bit)) for i in range(tri_count)]
         dens = dens + lax.ppermute(dens, TRI, perm)
         if r == 0:
-            grad = lax.psum_scatter(grad, "vx", scatter_dimension=0, tiled=True)
-    grad = halve(grad[0], "vz", 0)
-    return grad, dens
+            grad = lax.psum_scatter(grad.reshape(-1, *grad.shape[2:]), ("vx", "vz"), scatter_dimension=0, tiled=True)
+    return grad[0], dens
 
 
 def butterfly_sum(x, axes):

time: 193 us -> 241 us (1.25)
  waiting for transfers between devices: 79.1 us -> 138 us
  starting transfers between devices: 39.7 us -> 31.4 us
    reduce_scatter x1, waiting for transfers between devices: 0.02 us -> 56.1 us  [reduce_tails(): lax.psum_scatter(grad.reshape(-1, *grad.shape[2:]), ('vx', 'vz'), scatter...]
    ppermute x2 -> x1, starting transfers between devices: 10.2 us -> 1.92 us  [halve(): return keep + lax.ppermute(send, axis, [(0, 1), (1, 0)])]
    ppermute x5, waiting for transfers between devices: 10.8 us -> 15.4 us  [reduce_tails(): dens = dens + lax.ppermute(dens, TRI, perm)]
  transfers between devices with their start and end apart: 10 -> 9, of which waited for: 8 -> 9; matrix products, arithmetic and copies ran while one was open for 7% -> 5% of each run, Pallas kernels for 0% -> 0%
where the time goes in v7:
time: 241 us; the launch traced here: 240 us
  waiting for transfers between devices  138 us (57%)
  starting transfers between devices  31.4 us (13%)
  blocking collectives  24.4 us (10%)
  between operations  14.4 us (6%)
  matrix products  14.1 us (6%)
  local copies, waits for them, and re-layouts  9.79 us (4%)
  other arithmetic  7.96 us (3%)
    all_gather x1, waiting for transfers between devices, whole_of(): nearer = lax.all_gather(x, axes[-1], axis=dim, tiled=True)  58 us
    reduce_scatter x1, waiting for transfers between devices, reduce_tails(): lax.psum_scatter(grad.reshape(-1, *grad.shape[2:]), ('vx', 'vz'), scatter...  56.1 us
    all_gather x1, blocking collectives, whole_of(): nearer = lax.all_gather(x, axes[-1], axis=dim, tiled=True)  24.4 us
    ppermute x5, starting transfers between devices, reduce_tails(): dens = dens + lax.ppermute(dens, TRI, perm)  18.9 us
    ppermute x5, waiting for transfers between devices, reduce_tails(): dens = dens + lax.ppermute(dens, TRI, perm)  15.4 us
    all_to_all x1, starting transfers between devices, from_everyone(): return lax.all_to_all(copies, axis, split_axis=0, concat_axis=0, tiled=True)  10.5 us
    dot_general x1, matrix products, body(): jnp.einsum('rb,bad->rad', pick, everything, preferred_element_type=bf16)  7.92 us
    all_to_all x1, waiting for transfers between devices, from_everyone(): return lax.all_to_all(copies, axis, split_axis=0, concat_axis=0, tiled=True)  6.34 us
  transfers between devices with their start and end apart: 9, of which 9 were waited for; matrix products, arithmetic and copies ran while one was open for 5% of the time, Pallas kernels for 0%

profile of v7, /device:TPU:6, one launch (start us, length us, event | category | flops | bytes accessed | tf_op | source)
XLA Modules:
  0.0 239.7 jit_solution(4727791420066266879)
XLA Ops:
  7.2 24.4 %all_gather.6 = bf16[12,48,768]{2,1,0:T(8,128)(2,1)} all-gather(bf16[3,48,768]{2,1,0:T(8,128)(2,1)} %param.8), channel_id=1, replica_groups=mesh['tri_0'=8,'tri_1'=4,'vx'=4,'vz'=2,'vc'=2] {'tri_1'}, dimensions={0}, use_global_device_ids=true | all-gather | bytes 1105920 | tf_op jit(solution)/shard_map/all_gather | solution.py:15
  31.7 1.7 broadcast_in_dim.20
  33.4 10.5 %all-to-all-start = ((bf16[16,3,48,128]{3,2,1,0:T(8,128)(2,1)}), bf16[16,3,48,128]{3,2,1,0:T(8,128)(2,1)S(1)}, u32[]{:S(2)}, u32[]{:S(2)}) async-start(bf16[16,3,48,128]{3,2,1,0:T(8,128)(2,1)} %broadcast_in_dim.20), calls=%async_computation | async-start | bytes 1179648 | tf_op jit(solution)/shard_map/all_to_all | solution.py:21
  44.1 0.1 reduce
  44.4 0.7 gather_fusion
  45.1 0.7 gather_fusion.1
  45.9 0.6 fusion.15
  46.5 0.7 gather_fusion.3
  47.3 0.1 compare_select_fusion
  47.4 0.1 reshape.199
  47.5 1.2 gather_fusion.4
  48.8 0.1 reshape.198
  48.9 0.7 fusion.17
  49.5 0.6 gather_fusion.2
  50.7 0.1 copy.68
  50.9 0.1 copy.66
  51.0 0.1 add.185
  51.1 0.1 copy.60
  51.2 0.1 copy.59
  51.4 0.7 iota_compare_fusion.2
  52.1 0.1 broadcast_and_fusion
  52.3 0.2 broadcast_add_fusion
  52.6 6.3 %all-to-all-done = bf16[16,3,48,128]{3,2,1,0:T(8,128)(2,1)S(1)} async-done(((bf16[16,3,48,128]{3,2,1,0:T(8,128)(2,1)}), bf16[16,3,48,128]{3,2,1,0:T(8,128)(2,1)S(1)}, u32[]{:S(2)}, u32[]{:S(2)}) %all-to-all-start) | async-done | bytes 589856 | tf_op jit(solution)/shard_map/all_to_all | solution.py:21
  58.9 0.9 copy.63
  59.8 58.0 %all-gather.2.cloned.1.call-done = bf16[96,48,768]{2,1,0:T(8,128)(2,1)} async-done(((bf16[12,48,768]{2,1,0:T(8,128)(2,1)}), bf16[96,48,768]{2,1,0:T(8,128)(2,1)}) %all-gather.2.cloned.1.call-update) | async-done | bytes 7077904 | tf_op jit(solution)/shard_map/all_gather | solution.py:15
  117.8 7.9 %fusion = bf16[72,48,768]{2,0,1:T(8,128)(2,1)S(1)} fusion(bf16[96,48,768]{2,1,0:T(8,128)(2,1)} %all-gather.2.cloned.1.call-done, s32[72]{0:T(128)S(1)} %add.185), kind=kOutput, calls=%fused_computation.7 | convolution fusion | flops 509614848 | bytes 12386592 | tf_op jit(solution)/shard_map/rb,bad->rad/dot_general | solution.py:90
  125.7 1.0 copy.62
  126.8 2.9 %fusion.19 = f32[12,2,3,48,3,128]{5,3,4,2,1,0:T(8,128)S(1)} fusion(bf16[12,2,3,48,768,1]{4,3,5,2,1,0:T(8,128)(2,1)S(1)} %bitcast.67, bf16[3,768,128,1,1,1]{2,1,0,5,4,3:T(8,128)(2,1)S(1)} %bitcast.73), kind=kOutput, calls=%fused_computation.55 | convolution fusion | flops 2038431744 | bytes 11206656 | tf_op jit(solution)/shard_map/rad,kdm->rakm/dot_general | solution.py:91
  129.7 0.5 slice_bitcast_fusion.1
  130.1 3.1 %fusion.2 = (f32[12,3,48,3,128]{4,2,3,1,0:T(8,128)S(1)}, f32[48,128]{1,0:T(8,128)S(1)}) fusion(f32[12,3]{1,0:T(8,128)S(1)} %copy.68, f32[12,3,48,3,128]{4,2,3,1,0:T(8,128)S(1)} %broadcast_add_fusion, f32[12,3,48,3,128]{4,2,3,1,0:T(8,128)S(1)} %get-tuple-element.8, f32[12,3,48,3,128]{4,2,3,1,0:T(8,128)S(1)} %get-tuple-element.7, ...), kind=kLoop, calls=%fused_computation.9 | loop fusion | flops 13264896 | bytes 10641876 | tf_op jit(solution)/shard_map/reduce_sum | solution.py:109
  133.3 0.4 fusion.3
  133.7 1.6 fusion.6
  135.3 1.7 fusion.8
  137.1 1.9 collective-permute-start.5
  139.1 2.0 collective-permute-done.5
  141.0 0.9 fusion.11
  141.9 3.6 %collective-permute-start = (f32[48,128]{1,0:T(8,128)S(1)}, f32[48,128]{1,0:T(8,128)S(1)}, u32[]{:S(2)}, u32[]{:S(2)}) collective-permute-start(f32[48,128]{1,0:T(8,128)S(1)} %get-tuple-element.3), channel_id=1, source_target_pairs={{0,16},{16,0},{32,48},{48,32},{64,80},{80,64},{96,112},{112,96},{1... | collective-permute-start | bytes 73736 | tf_op jit(solution)/shard_map/ppermute | solution.py:49
  145.5 2.2 collective-permute-done
  147.7 4.6 %collective-permute-start.1 = (f32[48,128]{1,0:T(8,128)S(1)}, f32[48,128]{1,0:T(8,128)S(1)}, u32[]{:S(2)}, u32[]{:S(2)}) collective-permute-start(f32[48,128]{1,0:T(8,128)S(1)} %add.207), channel_id=1, source_target_pairs={{0,32},{16,48},{32,0},{48,16},{64,96},{80,112},{96,64},{112,80},{1... | collective-permute-start | bytes 73736 | tf_op jit(solution)/shard_map/ppermute | solution.py:49
  152.3 2.0 collective-permute-done.1
  154.3 2.0 collective-permute-start.2
  156.3 3.7 %collective-permute-done.2 = f32[48,128]{1,0:T(8,128)S(1)} collective-permute-done((f32[48,128]{1,0:T(8,128)S(1)}, f32[48,128]{1,0:T(8,128)S(1)}, u32[]{:S(2)}, u32[]{:S(2)}) %collective-permute-start.2) | collective-permute-done | bytes 24608 | tf_op jit(solution)/shard_map/ppermute | solution.py:49
  160.0 3.6 %collective-permute-start.3 = (f32[48,128]{1,0:T(8,128)S(1)}, f32[48,128]{1,0:T(8,128)S(1)}, u32[]{:S(2)}, u32[]{:S(2)}) collective-permute-start(f32[48,128]{1,0:T(8,128)S(1)} %add.209), channel_id=1, source_target_pairs={{0,128},{16,144},{32,160},{48,176},{64,192},{80,208},{96,224},{112... | collective-permute-start | bytes 73736 | tf_op jit(solution)/shard_map/ppermute | solution.py:49
  163.6 3.0 %collective-permute-done.3 = f32[48,128]{1,0:T(8,128)S(1)} collective-permute-done((f32[48,128]{1,0:T(8,128)S(1)}, f32[48,128]{1,0:T(8,128)S(1)}, u32[]{:S(2)}, u32[]{:S(2)}) %collective-permute-start.3) | collective-permute-done | bytes 24608 | tf_op jit(solution)/shard_map/ppermute | solution.py:49
  166.6 5.1 %collective-permute-start.4 = (f32[48,128]{1,0:T(8,128)S(1)}, f32[48,128]{1,0:T(8,128)S(1)}, u32[]{:S(2)}, u32[]{:S(2)}) collective-permute-start(f32[48,128]{1,0:T(8,128)S(1)} %add.210), channel_id=1, source_target_pairs={{0,256},{16,272},{32,288},{48,304},{64,320},{80,336},{96,352},{112... | collective-permute-start | bytes 73736 | tf_op jit(solution)/shard_map/ppermute | solution.py:49
  171.7 4.5 %collective-permute-done.4 = f32[48,128]{1,0:T(8,128)S(1)} collective-permute-done((f32[48,128]{1,0:T(8,128)S(1)}, f32[48,128]{1,0:T(8,128)S(1)}, u32[]{:S(2)}, u32[]{:S(2)}) %collective-permute-start.4) | collective-permute-done | bytes 24608 | tf_op jit(solution)/shard_map/ppermute | solution.py:49
  176.2 0.6 add_multiply_fusion
  176.8 56.1 %reduce-scatter.2.cloned.1.call-done = f32[1,48,3,128]{3,1,2,0:T(8,128)} async-done(((f32[8,48,3,128]{3,1,2,0:T(8,128)}), f32[1,48,3,128]{3,1,2,0:T(8,128)}) %reduce-scatter.2.cloned.1.call-update) | async-done | bytes 73744 | tf_op jit(solution)/shard_map/reduce_scatter | solution.py:51
  (46 shorter events, 1.5 us)
Async XLA Ops:
  7.2 40.3 %copy-start = (f32[64]{0:T(128)S(1)}, f32[64]{0:T(128)}, u32[]{:S(2)}) copy-start(f32[64]{0:T(128)} %param.10) | copy-start | bytes 772
  7.2 36.8 %copy-start.1 = (s32[32]{0:T(128)S(1)}, s32[32]{0:T(128)}, u32[]{:S(2)}) copy-start(s32[32]{0:T(128)} %param.13) | copy-start | bytes 388
  7.2 37.0 %copy-start.4 = (s32[12,2]{0,1:T(2,128)S(1)}, s32[12,2]{0,1:T(2,128)}, u32[]{:S(2)}) copy-start(s32[12,2]{0,1:T(2,128)} %param.15) | copy-start | bytes 292
  7.2 110.6 %all-gather.2.cloned.1.call-start = ((), (), s32[]{:S(2)}) async-start(), calls=%async_computation.2 | async-start | bytes 7962624 | tf_op jit(solution)/shard_map/all_gather | solution.py:15
  33.4 25.5 %all-to-all-start = ((bf16[16,3,48,128]{3,2,1,0:T(8,128)(2,1)}), bf16[16,3,48,128]{3,2,1,0:T(8,128)(2,1)S(1)}, u32[]{:S(2)}, u32[]{:S(2)}) async-start(bf16[16,3,48,128]{3,2,1,0:T(8,128)(2,1)} %broadcast_in_dim.20), calls=%async_computation | async-start | bytes 1179648 | tf_op jit(solution)/shard_map/all_to_all | solution.py:21
  43.9 189.0 %reduce-scatter.2.cloned.1.call-start = ((), (), s32[]{:S(2)}) async-start(), calls=%async_computation.3 | async-start | bytes 663552 | tf_op jit(solution)/shard_map/reduce_scatter | solution.py:51
  44.4 0.7 copy-start.2
  47.5 3.0 %copy-start.6 = (f32[48]{0:T(128)S(1)}, f32[48]{0:T(128)}, u32[]{:S(2)}) copy-start(f32[48]{0:T(128)} %param.11) | copy-start | bytes 580
  47.5 4.7 %copy-start.5 = (f32[128]{0:T(128)S(1)}, f32[128]{0:T(128)}, u32[]{:S(2)}) copy-start(f32[128]{0:T(128)} %param.12) | copy-start | bytes 1540
  125.7 1.1 copy-start.3
  137.1 3.9 %collective-permute-start.5 = (f32[4,2,48,3,128]{4,2,3,1,0:T(8,128)S(1)}, f32[4,2,48,3,128]{4,2,3,1,0:T(8,128)S(1)}, u32[]{:S(2)}, u32[]{:S(2)}) collective-permute-start(f32[4,2,48,3,128]{4,2,3,1,0:T(8,128)S(1)} %bitcast.74), channel_id=1, source_target_pairs={{0,1},{1,0},{2,3},{3,2},{4,5},{5,4},{6,7},{7,6},{8,9},{9,8},{10,11... | collective-permute-start | bytes 1769480 | tf_op jit(solution)/shard_map/ppermute | solution.py:41
  141.9 5.7 %collective-permute-start = (f32[48,128]{1,0:T(8,128)S(1)}, f32[48,128]{1,0:T(8,128)S(1)}, u32[]{:S(2)}, u32[]{:S(2)}) collective-permute-start(f32[48,128]{1,0:T(8,128)S(1)} %get-tuple-element.3), channel_id=1, source_target_pairs={{0,16},{16,0},{32,48},{48,32},{64,80},{80,64},{96,112},{112,96},{1... | collective-permute-start | bytes 73736 | tf_op jit(solution)/shard_map/ppermute | solution.py:49
  147.7 6.6 %collective-permute-start.1 = (f32[48,128]{1,0:T(8,128)S(1)}, f32[48,128]{1,0:T(8,128)S(1)}, u32[]{:S(2)}, u32[]{:S(2)}) collective-permute-start(f32[48,128]{1,0:T(8,128)S(1)} %add.207), channel_id=1, source_target_pairs={{0,32},{16,48},{32,0},{48,16},{64,96},{80,112},{96,64},{112,80},{1... | collective-permute-start | bytes 73736 | tf_op jit(solution)/shard_map/ppermute | solution.py:49
  154.3 5.7 %collective-permute-start.2 = (f32[48,128]{1,0:T(8,128)S(1)}, f32[48,128]{1,0:T(8,128)S(1)}, u32[]{:S(2)}, u32[]{:S(2)}) collective-permute-start(f32[48,128]{1,0:T(8,128)S(1)} %add.208), channel_id=1, source_target_pairs={{0,64},{16,80},{32,96},{48,112},{64,0},{80,16},{96,32},{112,48},{1... | collective-permute-start | bytes 73736 | tf_op jit(solution)/shard_map/ppermute | solution.py:49
  160.0 6.6 %collective-permute-start.3 = (f32[48,128]{1,0:T(8,128)S(1)}, f32[48,128]{1,0:T(8,128)S(1)}, u32[]{:S(2)}, u32[]{:S(2)}) collective-permute-start(f32[48,128]{1,0:T(8,128)S(1)} %add.209), channel_id=1, source_target_pairs={{0,128},{16,144},{32,160},{48,176},{64,192},{80,208},{96,224},{112... | collective-permute-start | bytes 73736 | tf_op jit(solution)/shard_map/ppermute | solution.py:49
  166.6 9.6 %collective-permute-start.4 = (f32[48,128]{1,0:T(8,128)S(1)}, f32[48,128]{1,0:T(8,128)S(1)}, u32[]{:S(2)}, u32[]{:S(2)}) collective-permute-start(f32[48,128]{1,0:T(8,128)S(1)} %add.210), channel_id=1, source_target_pairs={{0,256},{16,272},{32,288},{48,304},{64,320},{80,336},{96,352},{112... | collective-permute-start | bytes 73736 | tf_op jit(solution)/shard_map/ppermute | solution.py:49
Sparse Core Ops, SparseCore 0:
  31.8 85.9 all-gather.1
  142.1 90.7 reduce-scatter.1

commit v8 on v6

--- a/solution.py
+++ b/solution.py
@@ -1,6 +1,8 @@
 import jax
 import jax.numpy as jnp
 from jax import lax
+from jax.experimental import pallas as pl
+from jax.experimental.pallas import tpu as pltpu
 from jax.sharding import Mesh
 from jax.sharding import PartitionSpec as P
 
@@ -32,6 +34,39 @@
     pieces = jnp.moveaxis(x.reshape(*before, lax.axis_size(axis), -1, *after), dim, 0)
     arrived = lax.all_to_all(pieces, axis, split_axis=0, concat_axis=0, tiled=True)
     return arrived.sum(axis=0)
+
+
+def pick_blocks(starts, table, width):
+    count = starts.shape[0]
+
+    def kernel(starts_ref, src_ref, out_ref, sems):
+        def issue(p, c):
+            pltpu.make_async_copy(
+                src_ref.at[pl.ds(starts_ref[p], width)], out_ref.at[pl.ds(p * width, width)], sems.at[p]
+            ).start()
+            return c
+
+        lax.fori_loop(0, count, issue, 0)
+
+        def finish(p, c):
+            pltpu.make_async_copy(
+                src_ref.at[pl.ds(0, width)], out_ref.at[pl.ds(p * width, width)], sems.at[p]
+            ).wait()
+            return c
+
+        lax.fori_loop(0, count, finish, 0)
+
+    return pl.pallas_call(
+        kernel,
+        grid_spec=pltpu.PrefetchScalarGridSpec(
+            num_scalar_prefetch=1,
+            grid=(1,),
+            in_specs=[pl.BlockSpec(memory_space=pl.ANY)],
+            out_specs=pl.BlockSpec(memory_space=pl.ANY),
+            scratch_shapes=[pltpu.SemaphoreType.DMA((count,))],
+        ),
+        out_shape=jax.ShapeDtypeStruct((count * width,) + table.shape[1:], table.dtype),
+    )(starts, table)
 
 
 def halve(x, axis, dim):
@@ -87,8 +122,7 @@
     everything = whole_of(amps, TRI, 0)
     table = joined_along(from_everyone(vvvo, VIR), 1)
 
-    pick = (rows.reshape(-1)[:, None] == jnp.arange(nrow, dtype=jnp.int32)).astype(bf16)
-    picked = jnp.einsum("rb,bad->rad", pick, everything, preferred_element_type=bf16)
+    picked = pick_blocks((pair_root * BMAX).reshape(-1).astype(jnp.int32), everything, BMAX)
     proj = jnp.einsum("rad,kdm->rakm", picked, table, preferred_element_type=f32)
     nv, nk, nm = proj.shape[1], proj.shape[2], proj.shape[3]
     proj = proj.reshape(npair, 2, BMAX, nv, nk, nm)

time: 193 us -> 348 us (1.80)
  Pallas kernels: 0 us -> 163 us
  matrix products: 14.1 us -> 8.16 us
    pallas_call x0 -> x1, Pallas kernels: none -> 163 us  [pick_blocks(): pl.pallas_call(kernel, grid_spec=pltpu.PrefetchScalarGridSpec(num_scalar_...]
    dot_general x1 -> x0, matrix products: 7.92 us -> none  [body(): jnp.einsum('rb,bad->rad', pick, everything, preferred_element_type=bf16)]
  transfers between devices with their start and end apart: 10 -> 10, of which waited for: 8 -> 8; matrix products, arithmetic and copies ran while one was open for 7% -> 4% of each run, Pallas kernels for 0% -> 0%
where the time goes in v8:
time: 348 us; the launch traced here: 347 us
  Pallas kernels  163 us (47%)
  waiting for transfers between devices  78.8 us (23%)
  starting transfers between devices  39.7 us (11%)
  blocking collectives  24.4 us (7%)
  between operations  14.4 us (4%)
  other arithmetic  9.69 us (3%)
  local copies, waits for them, and re-layouts  9.41 us (3%)
  matrix products  8.16 us (2%)
    pallas_call x1, Pallas kernels, pick_blocks(): pl.pallas_call(kernel, grid_spec=pltpu.PrefetchScalarGridSpec(num_scalar_...  163 us
    all_gather x1, waiting for transfers between devices, whole_of(): nearer = lax.all_gather(x, axes[-1], axis=dim, tiled=True)  58 us
    all_gather x1, blocking collectives, whole_of(): nearer = lax.all_gather(x, axes[-1], axis=dim, tiled=True)  24.4 us
    ppermute x5, starting transfers between devices, reduce_tails(): dens = dens + lax.ppermute(dens, TRI, perm)  18.9 us
    ppermute x5, waiting for transfers between devices, reduce_tails(): dens = dens + lax.ppermute(dens, TRI, perm)  10.8 us
    all_to_all x1, starting transfers between devices, from_everyone(): return lax.all_to_all(copies, axis, split_axis=0, concat_axis=0, tiled=True)  10.5 us
    ppermute x2, starting transfers between devices, halve(): return keep + lax.ppermute(send, axis, [(0, 1), (1, 0)])  10.2 us
  transfers between devices with their start and end apart: 10, of which 8 were waited for; matrix products, arithmetic and copies ran while one was open for 4% of the time, Pallas kernels for 0%

profile of v8, /device:TPU:6, one launch (start us, length us, event | category | flops | bytes accessed | tf_op | source)
XLA Modules:
  0.0 347.4 jit_solution(6824094413336966268)
XLA Ops:
  7.2 24.4 %all_gather.6 = bf16[12,48,768]{2,1,0:T(8,128)(2,1)} all-gather(bf16[3,48,768]{2,1,0:T(8,128)(2,1)} %param.8), channel_id=1, replica_groups=mesh['tri_0'=8,'tri_1'=4,'vx'=4,'vz'=2,'vc'=2] {'tri_1'}, dimensions={0}, use_global_device_ids=true | all-gather | bytes 1105920 | tf_op jit(solution)/shard_map/all_gather | solution.py:17
  31.7 1.7 broadcast_in_dim.20
  33.4 10.5 %all-to-all-start = ((bf16[16,3,48,128]{3,2,1,0:T(8,128)(2,1)}), bf16[16,3,48,128]{3,2,1,0:T(8,128)(2,1)S(1)}, u32[]{:S(2)}, u32[]{:S(2)}) async-start(bf16[16,3,48,128]{3,2,1,0:T(8,128)(2,1)} %broadcast_in_dim.20), calls=%async_computation | async-start | bytes 1179648 | tf_op jit(solution)/shard_map/all_to_all | solution.py:23
  44.1 0.1 reduce
  44.5 0.7 gather_fusion
  45.2 0.7 gather_fusion.1
  45.9 0.6 fusion.11
  46.5 0.7 gather_fusion.3
  47.4 0.1 reshape.185
  47.5 1.2 gather_fusion.4
  48.8 0.1 reshape.184
  48.9 0.7 fusion.13
  49.6 0.6 gather_fusion.2
  50.5 0.5 broadcast_multiply_fusion.starts_ref
  51.1 0.1 copy.60
  51.3 0.1 copy.58
  51.4 0.1 copy.54
  51.5 0.1 copy.53
  51.6 0.6 iota_compare_fusion.1
  52.3 0.1 broadcast_and_fusion
  52.6 0.2 broadcast_add_fusion
  52.8 6.1 %all-to-all-done = bf16[16,3,48,128]{3,2,1,0:T(8,128)(2,1)S(1)} async-done(((bf16[16,3,48,128]{3,2,1,0:T(8,128)(2,1)}), bf16[16,3,48,128]{3,2,1,0:T(8,128)(2,1)S(1)}, u32[]{:S(2)}, u32[]{:S(2)}) %all-to-all-start) | async-done | bytes 589856 | tf_op jit(solution)/shard_map/all_to_all | solution.py:23
  58.9 0.9 copy.55
  59.8 58.0 %all-gather.2.cloned.1.call-done.src_ref = bf16[96,48,768]{2,1,0:T(8,128)(2,1)} async-done(((bf16[12,48,768]{2,1,0:T(8,128)(2,1)}), bf16[96,48,768]{2,1,0:T(8,128)(2,1)}) %all-gather.2.cloned.1.call-update) | async-done | bytes 7077904 | tf_op jit(solution)/shard_map/all_gather | solution.py:17
  117.8 162.8 %shard_map.95 = bf16[72,48,768]{2,1,0:T(8,128)(2,1)} custom-call(s32[24]{0:T(128)} %broadcast_multiply_fusion.starts_ref, bf16[96,48,768]{2,1,0:T(8,128)(2,1)} %all-gather.2.cloned.1.call-done.src_ref), custom_call_target="tpu_custom_call" | custom-call | tf_op jit(solution)/shard_map/pallas_call | solution.py:59
  280.6 4.9 %fusion.15 = f32[12,2,3,48,3,128]{5,3,4,2,1,0:T(8,128)S(1)} fusion(bf16[12,2,3,48,768,1]{4,3,5,2,1,0:T(8,128)(2,1)} %bitcast.68, bf16[3,768,128,1,1,1]{2,1,0,5,4,3:T(8,128)(2,1)S(1)} %bitcast.75), kind=kOutput, calls=%fused_computation.52 | convolution fusion | flops 2038431744 | bytes 11206656 | tf_op jit(solution)/shard_map/rad,kdm->rakm/dot_general | solution.py:126
  285.5 0.5 slice_bitcast_fusion.1
  286.0 2.9 fusion
  288.9 0.4 fusion.1
  289.3 1.6 fusion.4
  290.9 1.7 fusion.6
  292.8 1.9 collective-permute-start.5
  294.7 2.0 collective-permute-done.5
  296.7 0.9 fusion.9
  297.6 3.6 %collective-permute-start = (f32[48,128]{1,0:T(8,128)S(1)}, f32[48,128]{1,0:T(8,128)S(1)}, u32[]{:S(2)}, u32[]{:S(2)}) collective-permute-start(f32[48,128]{1,0:T(8,128)S(1)} %get-tuple-element.3), channel_id=1, source_target_pairs={{0,16},{16,0},{32,48},{48,32},{64,80},{80,64},{96,112},{112,96},{1... | collective-permute-start | bytes 73736 | tf_op jit(solution)/shard_map/ppermute | solution.py:84
  301.1 2.2 collective-permute-done
  303.3 4.6 %collective-permute-start.1 = (f32[48,128]{1,0:T(8,128)S(1)}, f32[48,128]{1,0:T(8,128)S(1)}, u32[]{:S(2)}, u32[]{:S(2)}) collective-permute-start(f32[48,128]{1,0:T(8,128)S(1)} %add.197), channel_id=1, source_target_pairs={{0,32},{16,48},{32,0},{48,16},{64,96},{80,112},{96,64},{112,80},{1... | collective-permute-start | bytes 73736 | tf_op jit(solution)/shard_map/ppermute | solution.py:84
  307.9 2.0 collective-permute-done.1
  309.9 2.0 collective-permute-start.2
  311.9 3.7 %collective-permute-done.2 = f32[48,128]{1,0:T(8,128)S(1)} collective-permute-done((f32[48,128]{1,0:T(8,128)S(1)}, f32[48,128]{1,0:T(8,128)S(1)}, u32[]{:S(2)}, u32[]{:S(2)}) %collective-permute-start.2) | collective-permute-done | bytes 24608 | tf_op jit(solution)/shard_map/ppermute | solution.py:84
  315.6 3.6 %collective-permute-start.3 = (f32[48,128]{1,0:T(8,128)S(1)}, f32[48,128]{1,0:T(8,128)S(1)}, u32[]{:S(2)}, u32[]{:S(2)}) collective-permute-start(f32[48,128]{1,0:T(8,128)S(1)} %add.199), channel_id=1, source_target_pairs={{0,128},{16,144},{32,160},{48,176},{64,192},{80,208},{96,224},{112... | collective-permute-start | bytes 73736 | tf_op jit(solution)/shard_map/ppermute | solution.py:84
  319.2 3.0 collective-permute-done.3
  322.2 5.1 %collective-permute-start.4 = (f32[48,128]{1,0:T(8,128)S(1)}, f32[48,128]{1,0:T(8,128)S(1)}, u32[]{:S(2)}, u32[]{:S(2)}) collective-permute-start(f32[48,128]{1,0:T(8,128)S(1)} %add.200), channel_id=1, source_target_pairs={{0,256},{16,272},{32,288},{48,304},{64,320},{80,336},{96,352},{112... | collective-permute-start | bytes 73736 | tf_op jit(solution)/shard_map/ppermute | solution.py:84
  327.4 0.9 dynamic-slice_bitcast_fusion
  328.2 8.3 %collective-permute-start.6 = (f32[48,3,128]{2,0,1:T(8,128)S(1)}, f32[48,3,128]{2,0,1:T(8,128)S(1)}, u32[]{:S(2)}, u32[]{:S(2)}) collective-permute-start(f32[48,3,128]{2,0,1:T(8,128)S(1)} %dynamic-slice_bitcast_fusion), channel_id=1, source_target_pairs={{0,2},{2,0},{1,3},{3,1},{4,6},{6,4},{5,7},{7,5},{8,10},{10,8},{9,1... | collective-permute-start | bytes 221192 | tf_op jit(solution)/shard_map/ppermute | solution.py:76
  336.6 0.6 add_multiply_fusion
  337.2 1.9 collective-permute-done.6
  339.1 1.5 fusion.10
  (51 shorter events, 1.5 us)
Async XLA Ops:
  7.2 40.4 %copy-start = (f32[64]{0:T(128)S(1)}, f32[64]{0:T(128)}, u32[]{:S(2)}) copy-start(f32[64]{0:T(128)} %param.10) | copy-start | bytes 772
  7.2 36.8 %copy-start.1 = (s32[32]{0:T(128)S(1)}, s32[32]{0:T(128)}, u32[]{:S(2)}) copy-start(s32[32]{0:T(128)} %param.13) | copy-start | bytes 388
  7.2 37.1 %copy-start.4 = (s32[12,2]{0,1:T(2,128)S(1)}, s32[12,2]{0,1:T(2,128)}, u32[]{:S(2)}) copy-start(s32[12,2]{0,1:T(2,128)} %param.15) | copy-start | bytes 292
  7.2 110.6 %all-gather.2.cloned.1.call-start = ((), (), s32[]{:S(2)}) async-start(), calls=%async_computation.2 | async-start | bytes 7962624 | tf_op jit(solution)/shard_map/all_gather | solution.py:17
  33.4 25.5 %all-to-all-start = ((bf16[16,3,48,128]{3,2,1,0:T(8,128)(2,1)}), bf16[16,3,48,128]{3,2,1,0:T(8,128)(2,1)S(1)}, u32[]{:S(2)}, u32[]{:S(2)}) async-start(bf16[16,3,48,128]{3,2,1,0:T(8,128)(2,1)} %broadcast_in_dim.20), calls=%async_computation | async-start | bytes 1179648 | tf_op jit(solution)/shard_map/all_to_all | solution.py:23
  43.9 283.4 %reduce-scatter.2.cloned.1.call-start = ((), (), s32[]{:S(2)}) async-start(), calls=%async_computation.3 | async-start | bytes 737280 | tf_op jit(solution)/shard_map/reduce_scatter | solution.py:86
  44.5 0.7 copy-start.2
  47.5 2.9 copy-start.6
  47.5 4.9 %copy-start.5 = (f32[128]{0:T(128)S(1)}, f32[128]{0:T(128)}, u32[]{:S(2)}) copy-start(f32[128]{0:T(128)} %param.12) | copy-start | bytes 1540
  59.8 220.8 %copy-start.3 = (bf16[3,16,48,128]{3,2,1,0:T(8,128)(2,1)S(1)}, bf16[3,16,48,128]{3,2,1,0:T(8,128)(2,1)}, u32[]{:S(2)}) copy-start(bf16[3,16,48,128]{3,2,1,0:T(8,128)(2,1)} %copy.55) | copy-start | bytes 1769476
  285.5 3.8 %slice-start = ((s8[5308416]{0:T(1024)(128)(4,1)}), s8[1114112]{0:T(1024)(128)(4,1)S(1)}, s32[]{:S(2)}) async-start(s8[5308416]{0:T(1024)(128)(4,1)} %bitcast.69), calls=%async_computation.4 | async-start | bytes 2228224
  285.9 3.3 slice-start.1
  292.8 3.9 %collective-permute-start.5 = (f32[4,2,48,3,128]{4,2,3,1,0:T(8,128)S(1)}, f32[4,2,48,3,128]{4,2,3,1,0:T(8,128)S(1)}, u32[]{:S(2)}, u32[]{:S(2)}) collective-permute-start(f32[4,2,48,3,128]{4,2,3,1,0:T(8,128)S(1)} %bitcast.76), channel_id=1, source_target_pairs={{0,1},{1,0},{2,3},{3,2},{4,5},{5,4},{6,7},{7,6},{8,9},{9,8},{10,11... | collective-permute-start | bytes 1769480 | tf_op jit(solution)/shard_map/ppermute | solution.py:76
  297.6 5.7 %collective-permute-start = (f32[48,128]{1,0:T(8,128)S(1)}, f32[48,128]{1,0:T(8,128)S(1)}, u32[]{:S(2)}, u32[]{:S(2)}) collective-permute-start(f32[48,128]{1,0:T(8,128)S(1)} %get-tuple-element.3), channel_id=1, source_target_pairs={{0,16},{16,0},{32,48},{48,32},{64,80},{80,64},{96,112},{112,96},{1... | collective-permute-start | bytes 73736 | tf_op jit(solution)/shard_map/ppermute | solution.py:84
  303.3 6.6 %collective-permute-start.1 = (f32[48,128]{1,0:T(8,128)S(1)}, f32[48,128]{1,0:T(8,128)S(1)}, u32[]{:S(2)}, u32[]{:S(2)}) collective-permute-start(f32[48,128]{1,0:T(8,128)S(1)} %add.197), channel_id=1, source_target_pairs={{0,32},{16,48},{32,0},{48,16},{64,96},{80,112},{96,64},{112,80},{1... | collective-permute-start | bytes 73736 | tf_op jit(solution)/shard_map/ppermute | solution.py:84
  309.9 5.7 %collective-permute-start.2 = (f32[48,128]{1,0:T(8,128)S(1)}, f32[48,128]{1,0:T(8,128)S(1)}, u32[]{:S(2)}, u32[]{:S(2)}) collective-permute-start(f32[48,128]{1,0:T(8,128)S(1)} %add.198), channel_id=1, source_target_pairs={{0,64},{16,80},{32,96},{48,112},{64,0},{80,16},{96,32},{112,48},{1... | collective-permute-start | bytes 73736 | tf_op jit(solution)/shard_map/ppermute | solution.py:84
  315.6 6.6 %collective-permute-start.3 = (f32[48,128]{1,0:T(8,128)S(1)}, f32[48,128]{1,0:T(8,128)S(1)}, u32[]{:S(2)}, u32[]{:S(2)}) collective-permute-start(f32[48,128]{1,0:T(8,128)S(1)} %add.199), channel_id=1, source_target_pairs={{0,128},{16,144},{32,160},{48,176},{64,192},{80,208},{96,224},{112... | collective-permute-start | bytes 73736 | tf_op jit(solution)/shard_map/ppermute | solution.py:84
  322.2 14.3 %collective-permute-start.4 = (f32[48,128]{1,0:T(8,128)S(1)}, f32[48,128]{1,0:T(8,128)S(1)}, u32[]{:S(2)}, u32[]{:S(2)}) collective-permute-start(f32[48,128]{1,0:T(8,128)S(1)} %add.200), channel_id=1, source_target_pairs={{0,256},{16,272},{32,288},{48,304},{64,320},{80,336},{96,352},{112... | collective-permute-start | bytes 73736 | tf_op jit(solution)/shard_map/ppermute | solution.py:84
  328.2 10.8 %collective-permute-start.6 = (f32[48,3,128]{2,0,1:T(8,128)S(1)}, f32[48,3,128]{2,0,1:T(8,128)S(1)}, u32[]{:S(2)}, u32[]{:S(2)}) collective-permute-start(f32[48,3,128]{2,0,1:T(8,128)S(1)} %dynamic-slice_bitcast_fusion), channel_id=1, source_target_pairs={{0,2},{2,0},{1,3},{3,1},{4,6},{6,4},{5,7},{7,5},{8,10},{10,8},{9,1... | collective-permute-start | bytes 221192 | tf_op jit(solution)/shard_map/ppermute | solution.py:76
Sparse Core Ops, SparseCore 0:
  31.8 85.9 all-gather.1
  297.7 24.5 reduce-scatter.1

commit v9 on v6

--- a/solution.py
+++ b/solution.py
@@ -43,12 +43,12 @@
 
 def reduce_tails(grad, dens, tri_bits):
     tri_count = lax.axis_size(TRI)
-    grad = halve(grad, "vc", 2)
-    for r, bit in enumerate(tri_bits):
+    grad = jnp.moveaxis(grad, 1, 2)
+    grad = grad.reshape(-1, *grad.shape[2:])
+    grad = lax.psum_scatter(grad, ("vx", "vc"), scatter_dimension=0, tiled=True)
+    for bit in tri_bits:
         perm = [(i, i ^ (1 << bit)) for i in range(tri_count)]
         dens = dens + lax.ppermute(dens, TRI, perm)
-        if r == 0:
-            grad = lax.psum_scatter(grad, "vx", scatter_dimension=0, tiled=True)
     grad = halve(grad[0], "vz", 0)
     return grad, dens
 

time: 193 us -> 196 us (1.016)
  the two profiles are of different devices: /device:TPU:6 before, /device:TPU:8 now
where the time goes in v9:
time: 196 us; the launch traced here: 195 us
  waiting for transfers between devices  80.8 us (41%)
  starting transfers between devices  41.4 us (21%)
  blocking collectives  24.4 us (12%)
  between operations  14.4 us (7%)
  matrix products  14.1 us (7%)
  local copies, waits for them, and re-layouts  11.7 us (6%)
  other arithmetic  8.62 us (4%)
    all_gather x1, waiting for transfers between devices, whole_of(): nearer = lax.all_gather(x, axes[-1], axis=dim, tiled=True)  54.6 us
    all_gather x1, blocking collectives, whole_of(): nearer = lax.all_gather(x, axes[-1], axis=dim, tiled=True)  24.4 us
    ppermute x5, starting transfers between devices, reduce_tails(): dens = dens + lax.ppermute(dens, TRI, perm)  23.2 us
    all_to_all x1, starting transfers between devices, from_everyone(): return lax.all_to_all(copies, axis, split_axis=0, concat_axis=0, tiled=True)  10.1 us
    all_to_all x1, waiting for transfers between devices, from_everyone(): return lax.all_to_all(copies, axis, split_axis=0, concat_axis=0, tiled=True)  8.62 us
    ppermute x1, starting transfers between devices, halve(): return keep + lax.ppermute(send, axis, [(0, 1), (1, 0)])  8 us
    dot_general x1, matrix products, body(): jnp.einsum('rb,bad->rad', pick, everything, preferred_element_type=bf16)  7.92 us
    ppermute x5, waiting for transfers between devices, reduce_tails(): dens = dens + lax.ppermute(dens, TRI, perm)  7.82 us
  transfers between devices with their start and end apart: 9, of which 8 were waited for; matrix products, arithmetic and copies ran while one was open for 6% of the time, Pallas kernels for 0%

profile of v9, /device:TPU:8, one launch (start us, length us, event | category | flops | bytes accessed | tf_op | source)
XLA Modules:
  0.0 195.5 jit_solution(14219096022701107446)
XLA Ops:
  7.2 24.4 %all_gather.6 = bf16[12,48,768]{2,1,0:T(8,128)(2,1)} all-gather(bf16[3,48,768]{2,1,0:T(8,128)(2,1)} %param.8), channel_id=1, replica_groups=mesh['tri_0'=8,'tri_1'=4,'vx'=4,'vz'=2,'vc'=2] {'tri_1'}, dimensions={0}, use_global_device_ids=true | all-gather | bytes 1105920 | tf_op jit(solution)/shard_map/all_gather | solution.py:15
  31.7 1.7 broadcast_in_dim.20
  33.4 10.1 %all-to-all-start = ((bf16[16,3,48,128]{3,2,1,0:T(8,128)(2,1)}), bf16[16,3,48,128]{3,2,1,0:T(8,128)(2,1)S(1)}, u32[]{:S(2)}, u32[]{:S(2)}) async-start(bf16[16,3,48,128]{3,2,1,0:T(8,128)(2,1)} %broadcast_in_dim.20), calls=%async_computation | async-start | bytes 1179648 | tf_op jit(solution)/shard_map/all_to_all | solution.py:21
  43.8 0.1 reduce
  44.1 0.7 gather_fusion
  44.8 0.7 gather_fusion.1
  45.5 0.6 fusion.15
  46.1 0.7 gather_fusion.3
  47.0 0.1 reshape.203
  47.2 1.2 gather_fusion.4
  48.4 0.1 reshape.202
  48.5 0.7 fusion.17
  49.2 0.6 gather_fusion.2
  50.4 0.1 copy.66
  50.6 0.1 copy.64
  50.7 0.1 add.185
  50.8 0.1 copy.58
  50.9 0.1 copy.57
  51.0 0.7 iota_compare_fusion.2
  51.8 0.1 broadcast_and_fusion
  52.0 0.2 broadcast_add_fusion
  52.2 8.6 %all-to-all-done = bf16[16,3,48,128]{3,2,1,0:T(8,128)(2,1)S(1)} async-done(((bf16[16,3,48,128]{3,2,1,0:T(8,128)(2,1)}), bf16[16,3,48,128]{3,2,1,0:T(8,128)(2,1)S(1)}, u32[]{:S(2)}, u32[]{:S(2)}) %all-to-all-start) | async-done | bytes 589856 | tf_op jit(solution)/shard_map/all_to_all | solution.py:21
  60.8 0.9 copy.61
  61.8 54.6 %all-gather.2.cloned.1.call-done = bf16[96,48,768]{2,1,0:T(8,128)(2,1)} async-done(((bf16[12,48,768]{2,1,0:T(8,128)(2,1)}), bf16[96,48,768]{2,1,0:T(8,128)(2,1)}) %all-gather.2.cloned.1.call-update) | async-done | bytes 7077904 | tf_op jit(solution)/shard_map/all_gather | solution.py:15
  116.4 7.9 %fusion = bf16[72,48,768]{2,0,1:T(8,128)(2,1)S(1)} fusion(bf16[96,48,768]{2,1,0:T(8,128)(2,1)} %all-gather.2.cloned.1.call-done, s32[72]{0:T(128)S(1)} %add.185), kind=kOutput, calls=%fused_computation.7 | convolution fusion | flops 509614848 | bytes 12386592 | tf_op jit(solution)/shard_map/rb,bad->rad/dot_general | solution.py:91
  124.3 1.0 copy.60
  125.4 2.9 %fusion.19 = f32[12,2,3,48,3,128]{5,3,4,2,1,0:T(8,128)S(1)} fusion(bf16[12,2,3,48,768,1]{4,3,5,2,1,0:T(8,128)(2,1)S(1)} %bitcast.67, bf16[3,768,128,1,1,1]{2,1,0,5,4,3:T(8,128)(2,1)S(1)} %bitcast.73), kind=kOutput, calls=%fused_computation.53 | convolution fusion | flops 2038431744 | bytes 11206656 | tf_op jit(solution)/shard_map/rad,kdm->rakm/dot_general | solution.py:92
  128.3 0.5 slice_bitcast_fusion.1
  128.8 3.1 %fusion.2 = (f32[12,3,48,3,128]{4,2,3,1,0:T(8,128)S(1)}, f32[48,128]{1,0:T(8,128)S(1)}) fusion(f32[12,3]{1,0:T(8,128)S(1)} %copy.66, f32[12,3,48,3,128]{4,2,3,1,0:T(8,128)S(1)} %broadcast_add_fusion, f32[12,3,48,3,128]{4,2,3,1,0:T(8,128)S(1)} %get-tuple-element.8, f32[12,3,48,3,128]{4,2,3,1,0:T(8,128)S(1)} %get-tuple-element.7, ...), kind=kLoop, calls=%fused_computation.9 | loop fusion | flops 13264896 | bytes 10641876 | tf_op jit(solution)/shard_map/reduce_sum | solution.py:110
  131.9 0.4 fusion.3
  132.3 1.6 fusion.6
  134.0 1.7 fusion.8
  135.6 1.1 copy.70
  136.8 3.6 %collective-permute-start = (f32[48,128]{1,0:T(8,128)S(1)}, f32[48,128]{1,0:T(8,128)S(1)}, u32[]{:S(2)}, u32[]{:S(2)}) collective-permute-start(f32[48,128]{1,0:T(8,128)S(1)} %get-tuple-element.3), channel_id=1, source_target_pairs={{0,16},{16,0},{32,48},{48,32},{64,80},{80,64},{96,112},{112,96},{1... | collective-permute-start | bytes 73736 | tf_op jit(solution)/shard_map/ppermute | solution.py:51
  140.3 2.2 %collective-permute-done = f32[48,128]{1,0:T(8,128)S(1)} collective-permute-done((f32[48,128]{1,0:T(8,128)S(1)}, f32[48,128]{1,0:T(8,128)S(1)}, u32[]{:S(2)}, u32[]{:S(2)}) %collective-permute-start) | collective-permute-done | bytes 24608 | tf_op jit(solution)/shard_map/ppermute | solution.py:51
  142.5 4.6 %collective-permute-start.1 = (f32[48,128]{1,0:T(8,128)S(1)}, f32[48,128]{1,0:T(8,128)S(1)}, u32[]{:S(2)}, u32[]{:S(2)}) collective-permute-start(f32[48,128]{1,0:T(8,128)S(1)} %add.207), channel_id=1, source_target_pairs={{0,32},{16,48},{32,0},{48,16},{64,96},{80,112},{96,64},{112,80},{1... | collective-permute-start | bytes 73736 | tf_op jit(solution)/shard_map/ppermute | solution.py:51
  147.1 2.0 %collective-permute-done.1 = f32[48,128]{1,0:T(8,128)S(1)} collective-permute-done((f32[48,128]{1,0:T(8,128)S(1)}, f32[48,128]{1,0:T(8,128)S(1)}, u32[]{:S(2)}, u32[]{:S(2)}) %collective-permute-start.1) | collective-permute-done | bytes 24608 | tf_op jit(solution)/shard_map/ppermute | solution.py:51
  149.1 3.8 %collective-permute-start.2 = (f32[48,128]{1,0:T(8,128)S(1)}, f32[48,128]{1,0:T(8,128)S(1)}, u32[]{:S(2)}, u32[]{:S(2)}) collective-permute-start(f32[48,128]{1,0:T(8,128)S(1)} %add.208), channel_id=1, source_target_pairs={{0,64},{16,80},{32,96},{48,112},{64,0},{80,16},{96,32},{112,48},{1... | collective-permute-start | bytes 73736 | tf_op jit(solution)/shard_map/ppermute | solution.py:51
  152.9 1.9 collective-permute-done.2
  154.8 5.5 %collective-permute-start.3 = (f32[48,128]{1,0:T(8,128)S(1)}, f32[48,128]{1,0:T(8,128)S(1)}, u32[]{:S(2)}, u32[]{:S(2)}) collective-permute-start(f32[48,128]{1,0:T(8,128)S(1)} %add.209), channel_id=1, source_target_pairs={{0,128},{16,144},{32,160},{48,176},{64,192},{80,208},{96,224},{112... | collective-permute-start | bytes 73736 | tf_op jit(solution)/shard_map/ppermute | solution.py:51
  160.4 1.8 collective-permute-done.3
  162.2 5.7 %collective-permute-start.4 = (f32[48,128]{1,0:T(8,128)S(1)}, f32[48,128]{1,0:T(8,128)S(1)}, u32[]{:S(2)}, u32[]{:S(2)}) collective-permute-start(f32[48,128]{1,0:T(8,128)S(1)} %add.210), channel_id=1, source_target_pairs={{0,256},{16,272},{32,288},{48,304},{64,320},{80,336},{96,352},{112... | collective-permute-start | bytes 73736 | tf_op jit(solution)/shard_map/ppermute | solution.py:51
  167.9 7.2 %reduce-scatter.2.cloned.1.call-done = f32[1,2,48,3,128]{4,2,3,1,0:T(8,128)} async-done(((f32[8,2,48,3,128]{4,2,3,1,0:T(8,128)}), f32[1,2,48,3,128]{4,2,3,1,0:T(8,128)}) %reduce-scatter.2.cloned.1.call-update) | async-done | bytes 147472 | tf_op jit(solution)/shard_map/reduce_scatter | solution.py:48
  175.1 0.9 dynamic-slice_bitcast_fusion
  176.0 8.0 %collective-permute-start.5 = (f32[48,3,128]{2,0,1:T(8,128)S(1)}, f32[48,3,128]{2,0,1:T(8,128)S(1)}, u32[]{:S(2)}, u32[]{:S(2)}) collective-permute-start(f32[48,3,128]{2,0,1:T(8,128)S(1)} %dynamic-slice_bitcast_fusion), channel_id=1, source_target_pairs={{0,2},{2,0},{1,3},{3,1},{4,6},{6,4},{5,7},{7,5},{8,10},{10,8},{9,1... | collective-permute-start | bytes 221192 | tf_op jit(solution)/shard_map/ppermute | solution.py:41
  184.0 0.6 add_multiply_fusion
  184.6 2.5 %collective-permute-done.5 = f32[48,3,128]{2,0,1:T(8,128)S(1)} collective-permute-done((f32[48,3,128]{2,0,1:T(8,128)S(1)}, f32[48,3,128]{2,0,1:T(8,128)S(1)}, u32[]{:S(2)}, u32[]{:S(2)}) %collective-permute-start.5) | collective-permute-done | bytes 73760 | tf_op jit(solution)/shard_map/ppermute | solution.py:41
  187.1 1.5 fusion.11
  (46 shorter events, 1.5 us)
Async XLA Ops:
  7.2 40.0 %copy-start = (f32[64]{0:T(128)S(1)}, f32[64]{0:T(128)}, u32[]{:S(2)}) copy-start(f32[64]{0:T(128)} %param.10) | copy-start | bytes 772
  7.2 36.4 %copy-start.1 = (s32[32]{0:T(128)S(1)}, s32[32]{0:T(128)}, u32[]{:S(2)}) copy-start(s32[32]{0:T(128)} %param.13) | copy-start | bytes 388
  7.2 36.7 %copy-start.4 = (s32[12,2]{0,1:T(2,128)S(1)}, s32[12,2]{0,1:T(2,128)}, u32[]{:S(2)}) copy-start(s32[12,2]{0,1:T(2,128)} %param.15) | copy-start | bytes 292
  7.2 109.2 %all-gather.2.cloned.1.call-start = ((), (), s32[]{:S(2)}) async-start(), calls=%async_computation.2 | async-start | bytes 7962624 | tf_op jit(solution)/shard_map/all_gather | solution.py:15
  33.4 27.4 %all-to-all-start = ((bf16[16,3,48,128]{3,2,1,0:T(8,128)(2,1)}), bf16[16,3,48,128]{3,2,1,0:T(8,128)(2,1)S(1)}, u32[]{:S(2)}, u32[]{:S(2)}) async-start(bf16[16,3,48,128]{3,2,1,0:T(8,128)(2,1)} %broadcast_in_dim.20), calls=%async_computation | async-start | bytes 1179648 | tf_op jit(solution)/shard_map/all_to_all | solution.py:21
  43.5 131.5 %reduce-scatter.2.cloned.1.call-start = ((), (), s32[]{:S(2)}) async-start(), calls=%async_computation.3 | async-start | bytes 1327104 | tf_op jit(solution)/shard_map/reduce_scatter | solution.py:48
  44.1 0.7 copy-start.2
  47.2 3.0 %copy-start.6 = (f32[48]{0:T(128)S(1)}, f32[48]{0:T(128)}, u32[]{:S(2)}) copy-start(f32[48]{0:T(128)} %param.11) | copy-start | bytes 580
  47.2 4.7 %copy-start.5 = (f32[128]{0:T(128)S(1)}, f32[128]{0:T(128)}, u32[]{:S(2)}) copy-start(f32[128]{0:T(128)} %param.12) | copy-start | bytes 1540
  124.3 1.1 copy-start.3
  136.8 5.7 %collective-permute-start = (f32[48,128]{1,0:T(8,128)S(1)}, f32[48,128]{1,0:T(8,128)S(1)}, u32[]{:S(2)}, u32[]{:S(2)}) collective-permute-start(f32[48,128]{1,0:T(8,128)S(1)} %get-tuple-element.3), channel_id=1, source_target_pairs={{0,16},{16,0},{32,48},{48,32},{64,80},{80,64},{96,112},{112,96},{1... | collective-permute-start | bytes 73736 | tf_op jit(solution)/shard_map/ppermute | solution.py:51
  142.5 6.6 %collective-permute-start.1 = (f32[48,128]{1,0:T(8,128)S(1)}, f32[48,128]{1,0:T(8,128)S(1)}, u32[]{:S(2)}, u32[]{:S(2)}) collective-permute-start(f32[48,128]{1,0:T(8,128)S(1)} %add.207), channel_id=1, source_target_pairs={{0,32},{16,48},{32,0},{48,16},{64,96},{80,112},{96,64},{112,80},{1... | collective-permute-start | bytes 73736 | tf_op jit(solution)/shard_map/ppermute | solution.py:51
  149.1 5.7 %collective-permute-start.2 = (f32[48,128]{1,0:T(8,128)S(1)}, f32[48,128]{1,0:T(8,128)S(1)}, u32[]{:S(2)}, u32[]{:S(2)}) collective-permute-start(f32[48,128]{1,0:T(8,128)S(1)} %add.208), channel_id=1, source_target_pairs={{0,64},{16,80},{32,96},{48,112},{64,0},{80,16},{96,32},{112,48},{1... | collective-permute-start | bytes 73736 | tf_op jit(solution)/shard_map/ppermute | solution.py:51
  154.8 7.3 %collective-permute-start.3 = (f32[48,128]{1,0:T(8,128)S(1)}, f32[48,128]{1,0:T(8,128)S(1)}, u32[]{:S(2)}, u32[]{:S(2)}) collective-permute-start(f32[48,128]{1,0:T(8,128)S(1)} %add.209), channel_id=1, source_target_pairs={{0,128},{16,144},{32,160},{48,176},{64,192},{80,208},{96,224},{112... | collective-permute-start | bytes 73736 | tf_op jit(solution)/shard_map/ppermute | solution.py:51
  162.2 21.8 %collective-permute-start.4 = (f32[48,128]{1,0:T(8,128)S(1)}, f32[48,128]{1,0:T(8,128)S(1)}, u32[]{:S(2)}, u32[]{:S(2)}) collective-permute-start(f32[48,128]{1,0:T(8,128)S(1)} %add.210), channel_id=1, source_target_pairs={{0,256},{16,272},{32,288},{48,304},{64,320},{80,336},{96,352},{112... | collective-permute-start | bytes 73736 | tf_op jit(solution)/shard_map/ppermute | solution.py:51
  176.0 11.1 %collective-permute-start.5 = (f32[48,3,128]{2,0,1:T(8,128)S(1)}, f32[48,3,128]{2,0,1:T(8,128)S(1)}, u32[]{:S(2)}, u32[]{:S(2)}) collective-permute-start(f32[48,3,128]{2,0,1:T(8,128)S(1)} %dynamic-slice_bitcast_fusion), channel_id=1, source_target_pairs={{0,2},{2,0},{1,3},{3,1},{4,6},{6,4},{5,7},{7,5},{8,10},{10,8},{9,1... | collective-permute-start | bytes 221192 | tf_op jit(solution)/shard_map/ppermute | solution.py:41
Sparse Core Ops, SparseCore 0:
  31.8 84.5 all-gather.1
  136.9 38.1 reduce-scatter.1

commit v10 on v6

--- a/solution.py
+++ b/solution.py
@@ -84,7 +84,7 @@
     pair_live = slots < block_sizes[triples][..., None]
     rows = pair_root[..., None] * BMAX + slots
 
-    everything = whole_of(amps, TRI, 0)
+    everything = lax.all_gather(joined_along(from_everyone(amps, "tri_1"), 0), "tri_0", axis=0, tiled=True)
     table = joined_along(from_everyone(vvvo, VIR), 1)
 
     pick = (rows.reshape(-1)[:, None] == jnp.arange(nrow, dtype=jnp.int32)).astype(bf16)

time: 193 us -> 198 us (1.026)
  blocking collectives: 24.4 us -> 29.4 us
    all_to_all x0 -> x1, blocking collectives: none -> 29.4 us  [from_everyone(): return lax.all_to_all(copies, axis, split_axis=0, concat_axis=0, tiled=True)]
    all_gather x1 -> x0, blocking collectives: 24.4 us -> none  [whole_of(): nearer = lax.all_gather(x, axes[-1], axis=dim, tiled=True)]
    all_to_all x1, waiting for transfers between devices: 6.34 us -> 8.79 us  [from_everyone(): return lax.all_to_all(copies, axis, split_axis=0, concat_axis=0, tiled=True)]
  transfers between devices with their start and end apart: 10 -> 10, of which waited for: 8 -> 8; matrix products, arithmetic and copies ran while one was open for 7% -> 6% of each run, Pallas kernels for 0% -> 0%
where the time goes in v10:
time: 198 us
  waiting for transfers between devices  79.9 us (40%)
  starting transfers between devices  39.5 us (20%)
  blocking collectives  29.4 us (15%)
  between operations  14.4 us (7%)
  matrix products  14.1 us (7%)
  local copies, waits for them, and re-layouts  10.9 us (6%)
  other arithmetic  9.5 us (5%)
    all_gather x1, waiting for transfers between devices, body(): lax.all_gather(joined_along(from_everyone(amps, 'tri_1'), 0), 'tri_0', ax...  56.3 us
    all_to_all x1, blocking collectives, from_everyone(): return lax.all_to_all(copies, axis, split_axis=0, concat_axis=0, tiled=True)  29.4 us
    ppermute x5, starting transfers between devices, reduce_tails(): dens = dens + lax.ppermute(dens, TRI, perm)  18.9 us
    ppermute x5, waiting for transfers between devices, reduce_tails(): dens = dens + lax.ppermute(dens, TRI, perm)  10.8 us
    all_to_all x1, starting transfers between devices, from_everyone(): return lax.all_to_all(copies, axis, split_axis=0, concat_axis=0, tiled=True)  10.5 us
    ppermute x2, starting transfers between devices, halve(): return keep + lax.ppermute(send, axis, [(0, 1), (1, 0)])  9.92 us
    all_to_all x1, waiting for transfers between devices, from_everyone(): return lax.all_to_all(copies, axis, split_axis=0, concat_axis=0, tiled=True)  8.79 us
    dot_general x1, matrix products, body(): jnp.einsum('rb,bad->rad', pick, everything, preferred_element_type=bf16)  7.92 us
  transfers between devices with their start and end apart: 10, of which 8 were waited for; matrix products, arithmetic and copies ran while one was open for 6% of the time, Pallas kernels for 0%

profile of v10, /device:TPU:6, one launch (start us, length us, event | category | flops | bytes accessed | tf_op | source)
XLA Modules:
  0.0 197.7 jit_solution(179821079893105240)
XLA Ops:
  7.3 1.0 broadcast_in_dim.22
  8.3 29.4 %all_to_all.10 = bf16[4,3,48,768]{3,2,1,0:T(8,128)(2,1)} all-to-all(bf16[4,3,48,768]{3,2,1,0:T(8,128)(2,1)S(1)} %broadcast_in_dim.22), channel_id=1, replica_groups=mesh['tri_0'=8,'tri_1'=4,'vx'=4,'vz'=2,'vc'=2] {'tri_1'}, dimensions={0} | all-to-all | bytes 1769472 | tf_op jit(solution)/shard_map/all_to_all | solution.py:21
  37.7 0.9 broadcast_in_dim.23
  38.6 10.5 %all-to-all-start.1 = ((bf16[16,3,48,128]{3,2,1,0:T(8,128)(2,1)}), bf16[16,3,48,128]{3,2,1,0:T(8,128)(2,1)S(1)}, u32[]{:S(2)}, u32[]{:S(2)}) async-start(bf16[16,3,48,128]{3,2,1,0:T(8,128)(2,1)} %broadcast_in_dim.23), calls=%async_computation.1 | async-start | bytes 1179648 | tf_op jit(solution)/shard_map/all_to_all | solution.py:21
  49.4 0.1 reduce
  49.7 0.7 gather_fusion
  50.4 0.7 gather_fusion.1
  51.1 0.6 fusion.16
  51.7 0.7 gather_fusion.3
  52.6 0.1 reshape.203
  52.8 1.2 gather_fusion.4
  54.0 0.1 reshape.202
  54.1 0.7 fusion.18
  54.8 0.6 gather_fusion.2
  56.3 0.1 add.196
  56.4 0.1 copy.60
  56.5 0.1 copy.59
  56.6 0.7 iota_compare_fusion.2
  57.4 0.1 broadcast_and_fusion
  57.6 0.2 broadcast_add_fusion
  57.8 8.8 %all-to-all-done.1 = bf16[16,3,48,128]{3,2,1,0:T(8,128)(2,1)S(1)} async-done(((bf16[16,3,48,128]{3,2,1,0:T(8,128)(2,1)}), bf16[16,3,48,128]{3,2,1,0:T(8,128)(2,1)S(1)}, u32[]{:S(2)}, u32[]{:S(2)}) %all-to-all-start.1) | async-done | bytes 589856 | tf_op jit(solution)/shard_map/all_to_all | solution.py:21
  66.6 0.9 copy.63
  67.5 56.3 %all-gather.2.cloned.1.call-done = bf16[96,48,768]{2,1,0:T(8,128)(2,1)} async-done(((bf16[12,48,768]{2,1,0:T(8,128)(2,1)}), bf16[96,48,768]{2,1,0:T(8,128)(2,1)}) %all-gather.2.cloned.1.call-update) | async-done | bytes 7077904 | tf_op jit(solution)/shard_map/all_gather | solution.py:87
  123.8 7.9 %fusion = bf16[72,48,768]{2,0,1:T(8,128)(2,1)S(1)} fusion(bf16[96,48,768]{2,1,0:T(8,128)(2,1)} %all-gather.2.cloned.1.call-done, s32[72]{0:T(128)S(1)} %add.196), kind=kOutput, calls=%fused_computation.7 | convolution fusion | flops 509614848 | bytes 12386592 | tf_op jit(solution)/shard_map/rb,bad->rad/dot_general | solution.py:91
  131.7 1.0 copy.62
  132.8 2.9 %fusion.20 = f32[12,2,3,48,3,128]{5,3,4,2,1,0:T(8,128)S(1)} fusion(bf16[12,2,3,48,768,1]{4,3,5,2,1,0:T(8,128)(2,1)S(1)} %bitcast.72, bf16[3,768,128,1,1,1]{2,1,0,5,4,3:T(8,128)(2,1)S(1)} %bitcast.78), kind=kOutput, calls=%fused_computation.58 | convolution fusion | flops 2038431744 | bytes 11206656 | tf_op jit(solution)/shard_map/rad,kdm->rakm/dot_general | solution.py:92
  135.7 0.5 slice_bitcast_fusion.1
  136.2 3.1 %fusion.2 = (f32[12,3,48,3,128]{4,2,3,1,0:T(8,128)S(1)}, f32[48,128]{1,0:T(8,128)S(1)}) fusion(f32[12,3]{1,0:T(8,128)S(1)} %copy.68, f32[12,3,48,3,128]{4,2,3,1,0:T(8,128)S(1)} %broadcast_add_fusion, f32[12,3,48,3,128]{4,2,3,1,0:T(8,128)S(1)} %get-tuple-element.8, f32[12,3,48,3,128]{4,2,3,1,0:T(8,128)S(1)} %get-tuple-element.7, ...), kind=kLoop, calls=%fused_computation.9 | loop fusion | flops 13264896 | bytes 10641876 | tf_op jit(solution)/shard_map/reduce_sum | solution.py:110
  139.3 0.4 fusion.3
  139.7 1.6 fusion.6
  141.4 1.7 fusion.8
  143.2 1.9 collective-permute-start.5
  145.1 2.0 collective-permute-done.5
  147.1 0.9 fusion.11
  148.0 3.5 %collective-permute-start = (f32[48,128]{1,0:T(8,128)S(1)}, f32[48,128]{1,0:T(8,128)S(1)}, u32[]{:S(2)}, u32[]{:S(2)}) collective-permute-start(f32[48,128]{1,0:T(8,128)S(1)} %get-tuple-element.3), channel_id=1, source_target_pairs={{0,16},{16,0},{32,48},{48,32},{64,80},{80,64},{96,112},{112,96},{1... | collective-permute-start | bytes 73736 | tf_op jit(solution)/shard_map/ppermute | solution.py:49
  151.5 2.2 %collective-permute-done = f32[48,128]{1,0:T(8,128)S(1)} collective-permute-done((f32[48,128]{1,0:T(8,128)S(1)}, f32[48,128]{1,0:T(8,128)S(1)}, u32[]{:S(2)}, u32[]{:S(2)}) %collective-permute-start) | collective-permute-done | bytes 24608 | tf_op jit(solution)/shard_map/ppermute | solution.py:49
  153.7 4.6 %collective-permute-start.1 = (f32[48,128]{1,0:T(8,128)S(1)}, f32[48,128]{1,0:T(8,128)S(1)}, u32[]{:S(2)}, u32[]{:S(2)}) collective-permute-start(f32[48,128]{1,0:T(8,128)S(1)} %add.218), channel_id=1, source_target_pairs={{0,32},{16,48},{32,0},{48,16},{64,96},{80,112},{96,64},{112,80},{1... | collective-permute-start | bytes 73736 | tf_op jit(solution)/shard_map/ppermute | solution.py:49
  158.3 2.0 %collective-permute-done.1 = f32[48,128]{1,0:T(8,128)S(1)} collective-permute-done((f32[48,128]{1,0:T(8,128)S(1)}, f32[48,128]{1,0:T(8,128)S(1)}, u32[]{:S(2)}, u32[]{:S(2)}) %collective-permute-start.1) | collective-permute-done | bytes 24608 | tf_op jit(solution)/shard_map/ppermute | solution.py:49
  160.3 2.1 %collective-permute-start.2 = (f32[48,128]{1,0:T(8,128)S(1)}, f32[48,128]{1,0:T(8,128)S(1)}, u32[]{:S(2)}, u32[]{:S(2)}) collective-permute-start(f32[48,128]{1,0:T(8,128)S(1)} %add.219), channel_id=1, source_target_pairs={{0,64},{16,80},{32,96},{48,112},{64,0},{80,16},{96,32},{112,48},{1... | collective-permute-start | bytes 73736 | tf_op jit(solution)/shard_map/ppermute | solution.py:49
  162.4 3.6 %collective-permute-done.2 = f32[48,128]{1,0:T(8,128)S(1)} collective-permute-done((f32[48,128]{1,0:T(8,128)S(1)}, f32[48,128]{1,0:T(8,128)S(1)}, u32[]{:S(2)}, u32[]{:S(2)}) %collective-permute-start.2) | collective-permute-done | bytes 24608 | tf_op jit(solution)/shard_map/ppermute | solution.py:49
  166.0 3.6 %collective-permute-start.3 = (f32[48,128]{1,0:T(8,128)S(1)}, f32[48,128]{1,0:T(8,128)S(1)}, u32[]{:S(2)}, u32[]{:S(2)}) collective-permute-start(f32[48,128]{1,0:T(8,128)S(1)} %add.220), channel_id=1, source_target_pairs={{0,128},{16,144},{32,160},{48,176},{64,192},{80,208},{96,224},{112... | collective-permute-start | bytes 73736 | tf_op jit(solution)/shard_map/ppermute | solution.py:49
  169.7 3.0 %collective-permute-done.3 = f32[48,128]{1,0:T(8,128)S(1)} collective-permute-done((f32[48,128]{1,0:T(8,128)S(1)}, f32[48,128]{1,0:T(8,128)S(1)}, u32[]{:S(2)}, u32[]{:S(2)}) %collective-permute-start.3) | collective-permute-done | bytes 24608 | tf_op jit(solution)/shard_map/ppermute | solution.py:49
  172.6 5.1 %collective-permute-start.4 = (f32[48,128]{1,0:T(8,128)S(1)}, f32[48,128]{1,0:T(8,128)S(1)}, u32[]{:S(2)}, u32[]{:S(2)}) collective-permute-start(f32[48,128]{1,0:T(8,128)S(1)} %add.221), channel_id=1, source_target_pairs={{0,256},{16,272},{32,288},{48,304},{64,320},{80,336},{96,352},{112... | collective-permute-start | bytes 73736 | tf_op jit(solution)/shard_map/ppermute | solution.py:49
  177.8 0.9 dynamic-slice_bitcast_fusion
  178.7 8.0 %collective-permute-start.6 = (f32[48,3,128]{2,0,1:T(8,128)S(1)}, f32[48,3,128]{2,0,1:T(8,128)S(1)}, u32[]{:S(2)}, u32[]{:S(2)}) collective-permute-start(f32[48,3,128]{2,0,1:T(8,128)S(1)} %dynamic-slice_bitcast_fusion), channel_id=1, source_target_pairs={{0,2},{2,0},{1,3},{3,1},{4,6},{6,4},{5,7},{7,5},{8,10},{10,8},{9,1... | collective-permute-start | bytes 221192 | tf_op jit(solution)/shard_map/ppermute | solution.py:41
  186.7 0.6 add_multiply_fusion
  187.3 2.0 %collective-permute-done.6 = f32[48,3,128]{2,0,1:T(8,128)S(1)} collective-permute-done((f32[48,3,128]{2,0,1:T(8,128)S(1)}, f32[48,3,128]{2,0,1:T(8,128)S(1)}, u32[]{:S(2)}, u32[]{:S(2)}) %collective-permute-start.6) | collective-permute-done | bytes 73760 | tf_op jit(solution)/shard_map/ppermute | solution.py:41
  189.3 1.5 fusion.12
  (53 shorter events, 1.8 us)
Async XLA Ops:
  7.2 45.6 %copy-start = (f32[64]{0:T(128)S(1)}, f32[64]{0:T(128)}, u32[]{:S(2)}) copy-start(f32[64]{0:T(128)} %param.10) | copy-start | bytes 772
  7.2 30.5 %copy-start.4 = (bf16[3,48,128]{2,1,0:T(8,128)(2,1)S(1)}, bf16[3,48,128]{2,1,0:T(8,128)(2,1)}, u32[]{:S(2)}) copy-start(bf16[3,48,128]{2,1,0:T(8,128)(2,1)} %param.9) | copy-start | bytes 110596
  7.2 42.0 %copy-start.1 = (s32[32]{0:T(128)S(1)}, s32[32]{0:T(128)}, u32[]{:S(2)}) copy-start(s32[32]{0:T(128)} %param.13) | copy-start | bytes 388
  7.2 42.3 %copy-start.5 = (s32[12,2]{0,1:T(2,128)S(1)}, s32[12,2]{0,1:T(2,128)}, u32[]{:S(2)}) copy-start(s32[12,2]{0,1:T(2,128)} %param.15) | copy-start | bytes 292
  7.2 116.6 %all-gather.2.cloned.1.call-start = ((), (), s32[]{:S(2)}) async-start(), calls=%async_computation.3 | async-start | bytes 7962624 | tf_op jit(solution)/shard_map/all_gather | solution.py:87
  38.6 28.0 %all-to-all-start.1 = ((bf16[16,3,48,128]{3,2,1,0:T(8,128)(2,1)}), bf16[16,3,48,128]{3,2,1,0:T(8,128)(2,1)S(1)}, u32[]{:S(2)}, u32[]{:S(2)}) async-start(bf16[16,3,48,128]{3,2,1,0:T(8,128)(2,1)} %broadcast_in_dim.23), calls=%async_computation.1 | async-start | bytes 1179648 | tf_op jit(solution)/shard_map/all_to_all | solution.py:21
  49.1 128.6 %reduce-scatter.2.cloned.1.call-start = ((), (), s32[]{:S(2)}) async-start(), calls=%async_computation.4 | async-start | bytes 737280 | tf_op jit(solution)/shard_map/reduce_scatter | solution.py:51
  49.7 0.7 copy-start.2
  52.8 3.0 %copy-start.7 = (f32[48]{0:T(128)S(1)}, f32[48]{0:T(128)}, u32[]{:S(2)}) copy-start(f32[48]{0:T(128)} %param.11) | copy-start | bytes 580
  52.8 4.7 %copy-start.6 = (f32[128]{0:T(128)S(1)}, f32[128]{0:T(128)}, u32[]{:S(2)}) copy-start(f32[128]{0:T(128)} %param.12) | copy-start | bytes 1540
  131.7 1.1 copy-start.3
  143.2 3.9 %collective-permute-start.5 = (f32[4,2,48,3,128]{4,2,3,1,0:T(8,128)S(1)}, f32[4,2,48,3,128]{4,2,3,1,0:T(8,128)S(1)}, u32[]{:S(2)}, u32[]{:S(2)}) collective-permute-start(f32[4,2,48,3,128]{4,2,3,1,0:T(8,128)S(1)} %bitcast.79), channel_id=1, source_target_pairs={{0,1},{1,0},{2,3},{3,2},{4,5},{5,4},{6,7},{7,6},{8,9},{9,8},{10,11... | collective-permute-start | bytes 1769480 | tf_op jit(solution)/shard_map/ppermute | solution.py:41
  148.0 5.7 %collective-permute-start = (f32[48,128]{1,0:T(8,128)S(1)}, f32[48,128]{1,0:T(8,128)S(1)}, u32[]{:S(2)}, u32[]{:S(2)}) collective-permute-start(f32[48,128]{1,0:T(8,128)S(1)} %get-tuple-element.3), channel_id=1, source_target_pairs={{0,16},{16,0},{32,48},{48,32},{64,80},{80,64},{96,112},{112,96},{1... | collective-permute-start | bytes 73736 | tf_op jit(solution)/shard_map/ppermute | solution.py:49
  153.7 6.6 %collective-permute-start.1 = (f32[48,128]{1,0:T(8,128)S(1)}, f32[48,128]{1,0:T(8,128)S(1)}, u32[]{:S(2)}, u32[]{:S(2)}) collective-permute-start(f32[48,128]{1,0:T(8,128)S(1)} %add.218), channel_id=1, source_target_pairs={{0,32},{16,48},{32,0},{48,16},{64,96},{80,112},{96,64},{112,80},{1... | collective-permute-start | bytes 73736 | tf_op jit(solution)/shard_map/ppermute | solution.py:49
  160.3 5.7 %collective-permute-start.2 = (f32[48,128]{1,0:T(8,128)S(1)}, f32[48,128]{1,0:T(8,128)S(1)}, u32[]{:S(2)}, u32[]{:S(2)}) collective-permute-start(f32[48,128]{1,0:T(8,128)S(1)} %add.219), channel_id=1, source_target_pairs={{0,64},{16,80},{32,96},{48,112},{64,0},{80,16},{96,32},{112,48},{1... | collective-permute-start | bytes 73736 | tf_op jit(solution)/shard_map/ppermute | solution.py:49
  166.0 6.6 %collective-permute-start.3 = (f32[48,128]{1,0:T(8,128)S(1)}, f32[48,128]{1,0:T(8,128)S(1)}, u32[]{:S(2)}, u32[]{:S(2)}) collective-permute-start(f32[48,128]{1,0:T(8,128)S(1)} %add.220), channel_id=1, source_target_pairs={{0,128},{16,144},{32,160},{48,176},{64,192},{80,208},{96,224},{112... | collective-permute-start | bytes 73736 | tf_op jit(solution)/shard_map/ppermute | solution.py:49
  172.6 14.0 %collective-permute-start.4 = (f32[48,128]{1,0:T(8,128)S(1)}, f32[48,128]{1,0:T(8,128)S(1)}, u32[]{:S(2)}, u32[]{:S(2)}) collective-permute-start(f32[48,128]{1,0:T(8,128)S(1)} %add.221), channel_id=1, source_target_pairs={{0,256},{16,272},{32,288},{48,304},{64,320},{80,336},{96,352},{112... | collective-permute-start | bytes 73736 | tf_op jit(solution)/shard_map/ppermute | solution.py:49
  178.7 10.6 %collective-permute-start.6 = (f32[48,3,128]{2,0,1:T(8,128)S(1)}, f32[48,3,128]{2,0,1:T(8,128)S(1)}, u32[]{:S(2)}, u32[]{:S(2)}) collective-permute-start(f32[48,3,128]{2,0,1:T(8,128)S(1)} %dynamic-slice_bitcast_fusion), channel_id=1, source_target_pairs={{0,2},{2,0},{1,3},{3,1},{4,6},{6,4},{5,7},{7,5},{8,10},{10,8},{9,1... | collective-permute-start | bytes 221192 | tf_op jit(solution)/shard_map/ppermute | solution.py:41
Sparse Core Ops, SparseCore 0:
  37.8 85.9 all-gather.1
  148.1 24.5 reduce-scatter.1

commit v11 on v6

--- a/solution.py
+++ b/solution.py
@@ -88,7 +88,8 @@
     table = joined_along(from_everyone(vvvo, VIR), 1)
 
     pick = (rows.reshape(-1)[:, None] == jnp.arange(nrow, dtype=jnp.int32)).astype(bf16)
-    picked = jnp.einsum("rb,bad->rad", pick, everything, preferred_element_type=bf16)
+    flat = everything.reshape(everything.shape[0], -1)
+    picked = jnp.dot(pick, flat, preferred_element_type=bf16).reshape(-1, *everything.shape[1:])
     proj = jnp.einsum("rad,kdm->rakm", picked, table, preferred_element_type=f32)
     nv, nk, nm = proj.shape[1], proj.shape[2], proj.shape[3]
     proj = proj.reshape(npair, 2, BMAX, nv, nk, nm)

time: 193 us -> 194 us (level)
  transfers between devices with their start and end apart: 10 -> 10, of which waited for: 8 -> 8; matrix products, arithmetic and copies ran while one was open for 7% -> 6% of each run, Pallas kernels for 0% -> 0%
where the time goes in v11:
time: 194 us; the launch traced here: 193 us
  waiting for transfers between devices  79.3 us (41%)
  starting transfers between devices  39.4 us (20%)
  blocking collectives  24.4 us (13%)
  matrix products  15.4 us (8%)
  between operations  14.4 us (7%)
  local copies, waits for them, and re-layouts  10.6 us (5%)
  other arithmetic  9.44 us (5%)
    all_gather x1, waiting for transfers between devices, whole_of(): nearer = lax.all_gather(x, axes[-1], axis=dim, tiled=True)  58 us
    all_gather x1, blocking collectives, whole_of(): nearer = lax.all_gather(x, axes[-1], axis=dim, tiled=True)  24.4 us
    ppermute x5, starting transfers between devices, reduce_tails(): dens = dens + lax.ppermute(dens, TRI, perm)  18.9 us
    ppermute x5, waiting for transfers between devices, reduce_tails(): dens = dens + lax.ppermute(dens, TRI, perm)  10.8 us
    all_to_all x1, starting transfers between devices, from_everyone(): return lax.all_to_all(copies, axis, split_axis=0, concat_axis=0, tiled=True)  10.5 us
    ppermute x2, starting transfers between devices, halve(): return keep + lax.ppermute(send, axis, [(0, 1), (1, 0)])  9.86 us
    dot_general x1, matrix products, body(): jnp.dot(pick, flat, preferred_element_type=bf16)  8.05 us
    all_to_all x1, waiting for transfers between devices, from_everyone(): return lax.all_to_all(copies, axis, split_axis=0, concat_axis=0, tiled=True)  6.41 us
  transfers between devices with their start and end apart: 10, of which 8 were waited for; matrix products, arithmetic and copies ran while one was open for 6% of the time, Pallas kernels for 0%

profile of v11, /device:TPU:6, one launch (start us, length us, event | category | flops | bytes accessed | tf_op | source)
XLA Modules:
  0.0 193.0 jit_solution(13370416083359274855)
XLA Ops:
  7.2 24.4 %all_gather.6 = bf16[12,48,768]{2,1,0:T(8,128)(2,1)} all-gather(bf16[3,48,768]{2,1,0:T(8,128)(2,1)} %param.8), channel_id=1, replica_groups=mesh['tri_0'=8,'tri_1'=4,'vx'=4,'vz'=2,'vc'=2] {'tri_1'}, dimensions={0}, use_global_device_ids=true | all-gather | bytes 1105920 | tf_op jit(solution)/shard_map/all_gather | solution.py:15
  31.7 1.7 broadcast_in_dim.20
  33.4 10.5 %all-to-all-start = ((bf16[16,3,48,128]{3,2,1,0:T(8,128)(2,1)}), bf16[16,3,48,128]{3,2,1,0:T(8,128)(2,1)S(1)}, u32[]{:S(2)}, u32[]{:S(2)}) async-start(bf16[16,3,48,128]{3,2,1,0:T(8,128)(2,1)} %broadcast_in_dim.20), calls=%async_computation | async-start | bytes 1179648 | tf_op jit(solution)/shard_map/all_to_all | solution.py:21
  44.2 0.7 gather_fusion.1
  44.9 0.7 gather_fusion
  46.1 0.1 reduce
  46.2 0.6 fusion.28
  46.9 0.7 gather_fusion.3
  47.8 0.1 reshape.221
  47.9 0.7 fusion.30
  48.6 0.6 gather_fusion.2
  49.2 1.2 gather_fusion.4
  50.5 0.1 reshape.220
  50.7 0.1 copy.64
  50.8 0.1 copy.65
  51.1 0.1 copy.74
  51.3 0.6 iota_compare_fusion.2
  52.0 0.1 broadcast_and_fusion
  52.2 0.2 broadcast_add_fusion
  52.5 6.4 %all-to-all-done = bf16[16,3,48,128]{3,2,1,0:T(8,128)(2,1)S(1)} async-done(((bf16[16,3,48,128]{3,2,1,0:T(8,128)(2,1)}), bf16[16,3,48,128]{3,2,1,0:T(8,128)(2,1)S(1)}, u32[]{:S(2)}, u32[]{:S(2)}) %all-to-all-start) | async-done | bytes 589856 | tf_op jit(solution)/shard_map/all_to_all | solution.py:21
  58.9 0.9 copy.68
  59.8 58.0 %all-gather.2.cloned.1.call-done = bf16[96,48,768]{2,1,0:T(8,128)(2,1)} async-done(((bf16[12,48,768]{2,1,0:T(8,128)(2,1)}), bf16[96,48,768]{2,1,0:T(8,128)(2,1)}) %all-gather.2.cloned.1.call-update) | async-done | bytes 7077904 | tf_op jit(solution)/shard_map/all_gather | solution.py:15
  117.8 8.1 %fusion = bf16[12,2,3,48,768]{4,0,3,2,1:T(8,128)(2,1)S(1)} fusion(bf16[48,768,96,1,1]{1,0,2,4,3:T(8,128)(2,1)} %bitcast.82, s32[12,2,3]{0,2,1:T(4,128)S(1)} %iota_add_fusion), kind=kOutput, calls=%fused_computation.7 | convolution fusion | flops 509614848 | bytes 12386592 | tf_op jit(solution)/shard_map/dot_general | solution.py:92
  125.8 0.2 slice_bitcast_fusion
  126.1 0.8 copy-done.3
  126.9 3.9 %fusion.3 = f32[12,2,3,48,3,128]{5,3,4,2,1,0:T(8,128)S(1)} fusion(bf16[3,768,128,1,1,1]{2,1,0,5,4,3:T(8,128)(2,1)S(1)} %bitcast.85, bf16[12,2,3,48,768,1]{4,0,3,2,1,5:T(8,128)(2,1)S(1)} %bitcast.81), kind=kOutput, calls=%fused_computation.10 | convolution fusion | flops 2038431744 | bytes 11206656 | tf_op jit(solution)/shard_map/rad,kdm->rakm/dot_general | solution.py:93
  130.8 0.5 slice_bitcast_fusion.2
  131.3 3.1 %fusion.2 = (f32[12,3,48,3,128]{4,2,3,1,0:T(8,128)S(1)}, f32[48,128]{1,0:T(8,128)S(1)}) fusion(f32[12,3]{1,0:T(8,128)S(1)} %copy.74, f32[12,3,48,3,128]{4,2,3,1,0:T(8,128)S(1)} %broadcast_add_fusion, f32[12,3,48,3,128]{4,2,3,1,0:T(8,128)S(1)} %get-tuple-element.8, f32[12,3,48,3,128]{4,2,3,1,0:T(8,128)S(1)} %get-tuple-element.7, ...), kind=kLoop, calls=%fused_computation.9 | loop fusion | flops 13264896 | bytes 10641876 | tf_op jit(solution)/shard_map/reduce_sum | solution.py:111
  134.4 0.4 fusion.5
  134.9 1.6 fusion.12
  136.5 1.8 fusion.18
  138.4 1.9 collective-permute-start.5
  140.4 2.0 %collective-permute-done.5 = f32[4,2,48,3,128]{4,2,3,1,0:T(8,128)S(1)} collective-permute-done((f32[4,2,48,3,128]{4,2,3,1,0:T(8,128)S(1)}, f32[4,2,48,3,128]{4,2,3,1,0:T(8,128)S(1)}, u32[]{:S(2)}, u32[]{:S(2)}) %collective-permute-start.5) | collective-permute-done | bytes 589856 | tf_op jit(solution)/shard_map/ppermute | solution.py:41
  142.3 0.9 fusion.23
  143.2 3.6 %collective-permute-start = (f32[48,128]{1,0:T(8,128)S(1)}, f32[48,128]{1,0:T(8,128)S(1)}, u32[]{:S(2)}, u32[]{:S(2)}) collective-permute-start(f32[48,128]{1,0:T(8,128)S(1)} %get-tuple-element.3), channel_id=1, source_target_pairs={{0,16},{16,0},{32,48},{48,32},{64,80},{80,64},{96,112},{112,96},{1... | collective-permute-start | bytes 73736 | tf_op jit(solution)/shard_map/ppermute | solution.py:49
  146.8 2.2 %collective-permute-done = f32[48,128]{1,0:T(8,128)S(1)} collective-permute-done((f32[48,128]{1,0:T(8,128)S(1)}, f32[48,128]{1,0:T(8,128)S(1)}, u32[]{:S(2)}, u32[]{:S(2)}) %collective-permute-start) | collective-permute-done | bytes 24608 | tf_op jit(solution)/shard_map/ppermute | solution.py:49
  149.0 4.6 %collective-permute-start.1 = (f32[48,128]{1,0:T(8,128)S(1)}, f32[48,128]{1,0:T(8,128)S(1)}, u32[]{:S(2)}, u32[]{:S(2)}) collective-permute-start(f32[48,128]{1,0:T(8,128)S(1)} %add.215), channel_id=1, source_target_pairs={{0,32},{16,48},{32,0},{48,16},{64,96},{80,112},{96,64},{112,80},{1... | collective-permute-start | bytes 73736 | tf_op jit(solution)/shard_map/ppermute | solution.py:49
  153.6 2.0 %collective-permute-done.1 = f32[48,128]{1,0:T(8,128)S(1)} collective-permute-done((f32[48,128]{1,0:T(8,128)S(1)}, f32[48,128]{1,0:T(8,128)S(1)}, u32[]{:S(2)}, u32[]{:S(2)}) %collective-permute-start.1) | collective-permute-done | bytes 24608 | tf_op jit(solution)/shard_map/ppermute | solution.py:49
  155.6 2.0 %collective-permute-start.2 = (f32[48,128]{1,0:T(8,128)S(1)}, f32[48,128]{1,0:T(8,128)S(1)}, u32[]{:S(2)}, u32[]{:S(2)}) collective-permute-start(f32[48,128]{1,0:T(8,128)S(1)} %add.216), channel_id=1, source_target_pairs={{0,64},{16,80},{32,96},{48,112},{64,0},{80,16},{96,32},{112,48},{1... | collective-permute-start | bytes 73736 | tf_op jit(solution)/shard_map/ppermute | solution.py:49
  157.6 3.7 %collective-permute-done.2 = f32[48,128]{1,0:T(8,128)S(1)} collective-permute-done((f32[48,128]{1,0:T(8,128)S(1)}, f32[48,128]{1,0:T(8,128)S(1)}, u32[]{:S(2)}, u32[]{:S(2)}) %collective-permute-start.2) | collective-permute-done | bytes 24608 | tf_op jit(solution)/shard_map/ppermute | solution.py:49
  161.3 3.6 %collective-permute-start.3 = (f32[48,128]{1,0:T(8,128)S(1)}, f32[48,128]{1,0:T(8,128)S(1)}, u32[]{:S(2)}, u32[]{:S(2)}) collective-permute-start(f32[48,128]{1,0:T(8,128)S(1)} %add.217), channel_id=1, source_target_pairs={{0,128},{16,144},{32,160},{48,176},{64,192},{80,208},{96,224},{112... | collective-permute-start | bytes 73736 | tf_op jit(solution)/shard_map/ppermute | solution.py:49
  164.9 3.0 %collective-permute-done.3 = f32[48,128]{1,0:T(8,128)S(1)} collective-permute-done((f32[48,128]{1,0:T(8,128)S(1)}, f32[48,128]{1,0:T(8,128)S(1)}, u32[]{:S(2)}, u32[]{:S(2)}) %collective-permute-start.3) | collective-permute-done | bytes 24608 | tf_op jit(solution)/shard_map/ppermute | solution.py:49
  167.9 5.2 %collective-permute-start.4 = (f32[48,128]{1,0:T(8,128)S(1)}, f32[48,128]{1,0:T(8,128)S(1)}, u32[]{:S(2)}, u32[]{:S(2)}) collective-permute-start(f32[48,128]{1,0:T(8,128)S(1)} %add.218), channel_id=1, source_target_pairs={{0,256},{16,272},{32,288},{48,304},{64,320},{80,336},{96,352},{112... | collective-permute-start | bytes 73736 | tf_op jit(solution)/shard_map/ppermute | solution.py:49
  173.1 0.9 dynamic-slice_bitcast_fusion
  174.0 7.9 %collective-permute-start.6 = (f32[48,3,128]{2,0,1:T(8,128)S(1)}, f32[48,3,128]{2,0,1:T(8,128)S(1)}, u32[]{:S(2)}, u32[]{:S(2)}) collective-permute-start(f32[48,3,128]{2,0,1:T(8,128)S(1)} %dynamic-slice_bitcast_fusion), channel_id=1, source_target_pairs={{0,2},{2,0},{1,3},{3,1},{4,6},{6,4},{5,7},{7,5},{8,10},{10,8},{9,1... | collective-permute-start | bytes 221192 | tf_op jit(solution)/shard_map/ppermute | solution.py:41
  182.0 0.6 add_multiply_fusion
  182.6 2.0 %collective-permute-done.6 = f32[48,3,128]{2,0,1:T(8,128)S(1)} collective-permute-done((f32[48,3,128]{2,0,1:T(8,128)S(1)}, f32[48,3,128]{2,0,1:T(8,128)S(1)}, u32[]{:S(2)}, u32[]{:S(2)}) %collective-permute-start.6) | collective-permute-done | bytes 73760 | tf_op jit(solution)/shard_map/ppermute | solution.py:41
  184.6 1.5 fusion.24
  (50 shorter events, 1.7 us)
Async XLA Ops:
  7.2 41.4 %copy-start = (f32[64]{0:T(128)S(1)}, f32[64]{0:T(128)}, u32[]{:S(2)}) copy-start(f32[64]{0:T(128)} %param.10) | copy-start | bytes 772
  7.2 36.8 %copy-start.4 = (s32[12,2]{0,1:T(2,128)S(1)}, s32[12,2]{0,1:T(2,128)}, u32[]{:S(2)}) copy-start(s32[12,2]{0,1:T(2,128)} %param.15) | copy-start | bytes 292
  7.2 37.0 %copy-start.2 = (s32[32]{0:T(128)S(1)}, s32[32]{0:T(128)}, u32[]{:S(2)}) copy-start(s32[32]{0:T(128)} %param.14) | copy-start | bytes 388
  7.2 110.6 %all-gather.2.cloned.1.call-start = ((), (), s32[]{:S(2)}) async-start(), calls=%async_computation.2 | async-start | bytes 7962624 | tf_op jit(solution)/shard_map/all_gather | solution.py:15
  33.4 25.5 %all-to-all-start = ((bf16[16,3,48,128]{3,2,1,0:T(8,128)(2,1)}), bf16[16,3,48,128]{3,2,1,0:T(8,128)(2,1)S(1)}, u32[]{:S(2)}, u32[]{:S(2)}) async-start(bf16[16,3,48,128]{3,2,1,0:T(8,128)(2,1)} %broadcast_in_dim.20), calls=%async_computation | async-start | bytes 1179648 | tf_op jit(solution)/shard_map/all_to_all | solution.py:21
  43.9 129.2 %reduce-scatter.2.cloned.1.call-start = ((), (), s32[]{:S(2)}) async-start(), calls=%async_computation.3 | async-start | bytes 737280 | tf_op jit(solution)/shard_map/reduce_scatter | solution.py:51
  44.2 0.7 copy-start.1
  49.2 1.4 copy-start.6
  49.2 2.9 %copy-start.5 = (f32[128]{0:T(128)S(1)}, f32[128]{0:T(128)}, u32[]{:S(2)}) copy-start(f32[128]{0:T(128)} %param.12) | copy-start | bytes 1540
  125.8 1.1 copy-start.3
  138.4 3.9 %collective-permute-start.5 = (f32[4,2,48,3,128]{4,2,3,1,0:T(8,128)S(1)}, f32[4,2,48,3,128]{4,2,3,1,0:T(8,128)S(1)}, u32[]{:S(2)}, u32[]{:S(2)}) collective-permute-start(f32[4,2,48,3,128]{4,2,3,1,0:T(8,128)S(1)} %bitcast.86), channel_id=1, source_target_pairs={{0,1},{1,0},{2,3},{3,2},{4,5},{5,4},{6,7},{7,6},{8,9},{9,8},{10,11... | collective-permute-start | bytes 1769480 | tf_op jit(solution)/shard_map/ppermute | solution.py:41
  143.2 5.7 %collective-permute-start = (f32[48,128]{1,0:T(8,128)S(1)}, f32[48,128]{1,0:T(8,128)S(1)}, u32[]{:S(2)}, u32[]{:S(2)}) collective-permute-start(f32[48,128]{1,0:T(8,128)S(1)} %get-tuple-element.3), channel_id=1, source_target_pairs={{0,16},{16,0},{32,48},{48,32},{64,80},{80,64},{96,112},{112,96},{1... | collective-permute-start | bytes 73736 | tf_op jit(solution)/shard_map/ppermute | solution.py:49
  149.0 6.6 %collective-permute-start.1 = (f32[48,128]{1,0:T(8,128)S(1)}, f32[48,128]{1,0:T(8,128)S(1)}, u32[]{:S(2)}, u32[]{:S(2)}) collective-permute-start(f32[48,128]{1,0:T(8,128)S(1)} %add.215), channel_id=1, source_target_pairs={{0,32},{16,48},{32,0},{48,16},{64,96},{80,112},{96,64},{112,80},{1... | collective-permute-start | bytes 73736 | tf_op jit(solution)/shard_map/ppermute | solution.py:49
  155.6 5.7 %collective-permute-start.2 = (f32[48,128]{1,0:T(8,128)S(1)}, f32[48,128]{1,0:T(8,128)S(1)}, u32[]{:S(2)}, u32[]{:S(2)}) collective-permute-start(f32[48,128]{1,0:T(8,128)S(1)} %add.216), channel_id=1, source_target_pairs={{0,64},{16,80},{32,96},{48,112},{64,0},{80,16},{96,32},{112,48},{1... | collective-permute-start | bytes 73736 | tf_op jit(solution)/shard_map/ppermute | solution.py:49
  161.3 6.6 %collective-permute-start.3 = (f32[48,128]{1,0:T(8,128)S(1)}, f32[48,128]{1,0:T(8,128)S(1)}, u32[]{:S(2)}, u32[]{:S(2)}) collective-permute-start(f32[48,128]{1,0:T(8,128)S(1)} %add.217), channel_id=1, source_target_pairs={{0,128},{16,144},{32,160},{48,176},{64,192},{80,208},{96,224},{112... | collective-permute-start | bytes 73736 | tf_op jit(solution)/shard_map/ppermute | solution.py:49
  167.9 14.0 %collective-permute-start.4 = (f32[48,128]{1,0:T(8,128)S(1)}, f32[48,128]{1,0:T(8,128)S(1)}, u32[]{:S(2)}, u32[]{:S(2)}) collective-permute-start(f32[48,128]{1,0:T(8,128)S(1)} %add.218), channel_id=1, source_target_pairs={{0,256},{16,272},{32,288},{48,304},{64,320},{80,336},{96,352},{112... | collective-permute-start | bytes 73736 | tf_op jit(solution)/shard_map/ppermute | solution.py:49
  174.0 10.6 %collective-permute-start.6 = (f32[48,3,128]{2,0,1:T(8,128)S(1)}, f32[48,3,128]{2,0,1:T(8,128)S(1)}, u32[]{:S(2)}, u32[]{:S(2)}) collective-permute-start(f32[48,3,128]{2,0,1:T(8,128)S(1)} %dynamic-slice_bitcast_fusion), channel_id=1, source_target_pairs={{0,2},{2,0},{1,3},{3,1},{4,6},{6,4},{5,7},{7,5},{8,10},{10,8},{9,1... | collective-permute-start | bytes 221192 | tf_op jit(solution)/shard_map/ppermute | solution.py:41
Sparse Core Ops, SparseCore 0:
  31.8 85.9 all-gather.1
  143.4 24.5 reduce-scatter.1

commit v12 on v6

--- a/solution.py
+++ b/solution.py
@@ -3,6 +3,7 @@
 from jax import lax
 from jax.sharding import Mesh
 from jax.sharding import PartitionSpec as P
+
 
 BMAX = 3
 TRI = ("tri_0", "tri_1")
@@ -27,13 +28,6 @@
     return pieces.reshape(*lengths[:dim], lengths[dim] * lengths[dim + 1], *lengths[dim + 2 :])
 
 
-def sent_and_summed(x, axis, dim):
-    before, after = (x.shape[:dim], x.shape[dim + 1 :])
-    pieces = jnp.moveaxis(x.reshape(*before, lax.axis_size(axis), -1, *after), dim, 0)
-    arrived = lax.all_to_all(pieces, axis, split_axis=0, concat_axis=0, tiled=True)
-    return arrived.sum(axis=0)
-
-
 def halve(x, axis, dim):
     mine = lax.axis_index(axis)
     keep = lax.dynamic_index_in_dim(x, mine, axis=dim, keepdims=False)
@@ -53,17 +47,7 @@
     return grad, dens
 
 
-def butterfly_sum(x, axes):
-    count = lax.axis_size(axes)
-    bit = 1
-    while bit < count:
-        perm = [(i, i ^ bit) for i in range(count)]
-        x = x + lax.ppermute(x, axes, perm)
-        bit *= 2
-    return x
-
-
-def body(amps, vvvo, occ_gap, vir_gap, pair_gap, block_sizes, roots, triples):
+def body_inner(amps, vvvo, occ_gap, vir_gap, pair_gap, block_sizes, roots, triples):
     tri_count = lax.axis_size(TRI)
     me = lax.axis_index(TRI)
     npair = triples.shape[0]
@@ -116,7 +100,7 @@
     grad = jnp.einsum("qiad,qiakm->dkm", left_rows, hi, preferred_element_type=f32)
     grad = grad + jnp.einsum("qiad,qiakm->dkm", left_rows, lo, preferred_element_type=f32)
     grad = grad.reshape(lax.axis_size("vx"), lax.axis_size("vz"), lax.axis_size("vc"), -1, grad.shape[1], grad.shape[2])
-    grad, density = reduce_tails(grad, dens_part, (0, 1, 2, 3, 4))
+    grad, density = reduce_tails(grad, dens_part, (4, 0, 1, 2, 3))
     grad = jnp.transpose(grad, (1, 0, 2))
     density = density / float(tri_count * npair)
     return density, grad
@@ -127,7 +111,7 @@
     vir_hi = mesh.shape["vir"] // 4
     finer = Mesh(mesh.devices.reshape(tri_hi, 4, vir_hi, 2, 2), TRI + VIR)
     return jax.shard_map(
-        body,
+        body_inner,
         mesh=finer,
         in_specs=(
             P(TRI, VIR, None),

time: 193 us -> 195 us (1.010)
  transfers between devices with their start and end apart: 10 -> 10, of which waited for: 8 -> 8; matrix products, arithmetic and copies ran while one was open for 7% -> 6% of each run, Pallas kernels for 0% -> 0%
where the time goes in v12:
time: 195 us; the launch traced here: 193 us
  waiting for transfers between devices  80.7 us (41%)
  starting transfers between devices  39.5 us (20%)
  blocking collectives  24.4 us (13%)
  between operations  14.4 us (7%)
  matrix products  14.1 us (7%)
  local copies, waits for them, and re-layouts  10.7 us (5%)
  other arithmetic  9.5 us (5%)
    all_gather x1, waiting for transfers between devices, whole_of(): nearer = lax.all_gather(x, axes[-1], axis=dim, tiled=True)  58 us
    all_gather x1, blocking collectives, whole_of(): nearer = lax.all_gather(x, axes[-1], axis=dim, tiled=True)  24.4 us
    ppermute x5, starting transfers between devices, reduce_tails(): dens = dens + lax.ppermute(dens, TRI, perm)  19 us
    ppermute x5, waiting for transfers between devices, reduce_tails(): dens = dens + lax.ppermute(dens, TRI, perm)  12.4 us
    all_to_all x1, starting transfers between devices, from_everyone(): return lax.all_to_all(copies, axis, split_axis=0, concat_axis=0, tiled=True)  10.5 us
    ppermute x2, starting transfers between devices, halve(): return keep + lax.ppermute(send, axis, [(0, 1), (1, 0)])  9.93 us
    dot_general x1, matrix products, body_inner(): jnp.einsum('rb,bad->rad', pick, everything, preferred_element_type=bf16)  7.92 us
    all_to_all x1, waiting for transfers between devices, from_everyone(): return lax.all_to_all(copies, axis, split_axis=0, concat_axis=0, tiled=True)  6.34 us
  transfers between devices with their start and end apart: 10, of which 8 were waited for; matrix products, arithmetic and copies ran while one was open for 6% of the time, Pallas kernels for 0%

profile of v12, /device:TPU:6, one launch (start us, length us, event | category | flops | bytes accessed | tf_op | source)
XLA Modules:
  0.0 193.4 jit_solution(1895969140295007876)
XLA Ops:
  7.2 24.4 %all_gather.6 = bf16[12,48,768]{2,1,0:T(8,128)(2,1)} all-gather(bf16[3,48,768]{2,1,0:T(8,128)(2,1)} %param.8), channel_id=1, replica_groups=mesh['tri_0'=8,'tri_1'=4,'vx'=4,'vz'=2,'vc'=2] {'tri_1'}, dimensions={0}, use_global_device_ids=true | all-gather | bytes 1105920 | tf_op jit(solution)/shard_map/all_gather | solution.py:16
  31.7 1.7 broadcast_in_dim.20
  33.4 10.5 %all-to-all-start = ((bf16[16,3,48,128]{3,2,1,0:T(8,128)(2,1)}), bf16[16,3,48,128]{3,2,1,0:T(8,128)(2,1)S(1)}, u32[]{:S(2)}, u32[]{:S(2)}) async-start(bf16[16,3,48,128]{3,2,1,0:T(8,128)(2,1)} %broadcast_in_dim.20), calls=%async_computation | async-start | bytes 1179648 | tf_op jit(solution)/shard_map/all_to_all | solution.py:22
  44.1 0.1 reduce
  44.5 0.7 gather_fusion
  45.2 0.7 gather_fusion.1
  45.9 0.6 fusion.16
  46.5 0.7 gather_fusion.3
  47.4 0.1 reshape.199
  47.5 1.2 gather_fusion.4
  48.8 0.1 reshape.198
  48.9 0.7 fusion.18
  49.6 0.6 gather_fusion.2
  50.7 0.1 copy.68
  51.0 0.1 add.196
  51.1 0.1 copy.60
  51.2 0.1 copy.59
  51.4 0.7 iota_compare_fusion.2
  52.1 0.1 broadcast_and_fusion
  52.3 0.2 broadcast_add_fusion
  52.6 6.3 %all-to-all-done = bf16[16,3,48,128]{3,2,1,0:T(8,128)(2,1)S(1)} async-done(((bf16[16,3,48,128]{3,2,1,0:T(8,128)(2,1)}), bf16[16,3,48,128]{3,2,1,0:T(8,128)(2,1)S(1)}, u32[]{:S(2)}, u32[]{:S(2)}) %all-to-all-start) | async-done | bytes 589856 | tf_op jit(solution)/shard_map/all_to_all | solution.py:22
  58.9 0.9 copy.63
  59.8 58.0 %all-gather.2.cloned.1.call-done = bf16[96,48,768]{2,1,0:T(8,128)(2,1)} async-done(((bf16[12,48,768]{2,1,0:T(8,128)(2,1)}), bf16[96,48,768]{2,1,0:T(8,128)(2,1)}) %all-gather.2.cloned.1.call-update) | async-done | bytes 7077904 | tf_op jit(solution)/shard_map/all_gather | solution.py:16
  117.8 7.9 %fusion = bf16[72,48,768]{2,0,1:T(8,128)(2,1)S(1)} fusion(bf16[96,48,768]{2,1,0:T(8,128)(2,1)} %all-gather.2.cloned.1.call-done, s32[72]{0:T(128)S(1)} %add.196), kind=kOutput, calls=%fused_computation.7 | convolution fusion | flops 509614848 | bytes 12386592 | tf_op jit(solution)/shard_map/rb,bad->rad/dot_general | solution.py:75
  125.7 1.0 copy.62
  126.8 2.9 %fusion.20 = f32[12,2,3,48,3,128]{5,3,4,2,1,0:T(8,128)S(1)} fusion(bf16[12,2,3,48,768,1]{4,3,5,2,1,0:T(8,128)(2,1)S(1)} %bitcast.71, bf16[3,768,128,1,1,1]{2,1,0,5,4,3:T(8,128)(2,1)S(1)} %bitcast.76), kind=kOutput, calls=%fused_computation.58 | convolution fusion | flops 2038431744 | bytes 11206656 | tf_op jit(solution)/shard_map/rad,kdm->rakm/dot_general | solution.py:76
  129.7 0.5 slice_bitcast_fusion.1
  130.2 3.1 %fusion.2 = (f32[12,3,48,3,128]{4,2,3,1,0:T(8,128)S(1)}, f32[48,128]{1,0:T(8,128)S(1)}) fusion(f32[12,3]{1,0:T(8,128)S(1)} %copy.68, f32[12,3,48,3,128]{4,2,3,1,0:T(8,128)S(1)} %broadcast_add_fusion, f32[12,3,48,3,128]{4,2,3,1,0:T(8,128)S(1)} %get-tuple-element.8, f32[12,3,48,3,128]{4,2,3,1,0:T(8,128)S(1)} %get-tuple-element.7, ...), kind=kLoop, calls=%fused_computation.9 | loop fusion | flops 13264896 | bytes 10641876 | tf_op jit(solution)/shard_map/reduce_sum | solution.py:94
  133.3 0.4 fusion.3
  133.7 1.6 fusion.6
  135.3 1.7 fusion.8
  137.2 1.9 collective-permute-start.5
  139.1 2.0 %collective-permute-done.5 = f32[4,2,48,3,128]{4,2,3,1,0:T(8,128)S(1)} collective-permute-done((f32[4,2,48,3,128]{4,2,3,1,0:T(8,128)S(1)}, f32[4,2,48,3,128]{4,2,3,1,0:T(8,128)S(1)}, u32[]{:S(2)}, u32[]{:S(2)}) %collective-permute-start.5) | collective-permute-done | bytes 589856 | tf_op jit(solution)/shard_map/ppermute | solution.py:35
  141.1 0.9 fusion.11
  142.0 5.1 %collective-permute-start = (f32[48,128]{1,0:T(8,128)S(1)}, f32[48,128]{1,0:T(8,128)S(1)}, u32[]{:S(2)}, u32[]{:S(2)}) collective-permute-start(f32[48,128]{1,0:T(8,128)S(1)} %get-tuple-element.3), channel_id=1, source_target_pairs={{0,256},{16,272},{32,288},{48,304},{64,320},{80,336},{96,352},{112... | collective-permute-start | bytes 73736 | tf_op jit(solution)/shard_map/ppermute | solution.py:43
  147.1 4.5 %collective-permute-done = f32[48,128]{1,0:T(8,128)S(1)} collective-permute-done((f32[48,128]{1,0:T(8,128)S(1)}, f32[48,128]{1,0:T(8,128)S(1)}, u32[]{:S(2)}, u32[]{:S(2)}) %collective-permute-start) | collective-permute-done | bytes 24608 | tf_op jit(solution)/shard_map/ppermute | solution.py:43
  151.6 3.5 %collective-permute-start.1 = (f32[48,128]{1,0:T(8,128)S(1)}, f32[48,128]{1,0:T(8,128)S(1)}, u32[]{:S(2)}, u32[]{:S(2)}) collective-permute-start(f32[48,128]{1,0:T(8,128)S(1)} %add.218), channel_id=1, source_target_pairs={{0,16},{16,0},{32,48},{48,32},{64,80},{80,64},{96,112},{112,96},{1... | collective-permute-start | bytes 73736 | tf_op jit(solution)/shard_map/ppermute | solution.py:43
  155.1 2.2 %collective-permute-done.1 = f32[48,128]{1,0:T(8,128)S(1)} collective-permute-done((f32[48,128]{1,0:T(8,128)S(1)}, f32[48,128]{1,0:T(8,128)S(1)}, u32[]{:S(2)}, u32[]{:S(2)}) %collective-permute-start.1) | collective-permute-done | bytes 24608 | tf_op jit(solution)/shard_map/ppermute | solution.py:43
  157.3 4.6 %collective-permute-start.2 = (f32[48,128]{1,0:T(8,128)S(1)}, f32[48,128]{1,0:T(8,128)S(1)}, u32[]{:S(2)}, u32[]{:S(2)}) collective-permute-start(f32[48,128]{1,0:T(8,128)S(1)} %add.219), channel_id=1, source_target_pairs={{0,32},{16,48},{32,0},{48,16},{64,96},{80,112},{96,64},{112,80},{1... | collective-permute-start | bytes 73736 | tf_op jit(solution)/shard_map/ppermute | solution.py:43
  161.9 2.0 %collective-permute-done.2 = f32[48,128]{1,0:T(8,128)S(1)} collective-permute-done((f32[48,128]{1,0:T(8,128)S(1)}, f32[48,128]{1,0:T(8,128)S(1)}, u32[]{:S(2)}, u32[]{:S(2)}) %collective-permute-start.2) | collective-permute-done | bytes 24608 | tf_op jit(solution)/shard_map/ppermute | solution.py:43
  163.9 2.0 %collective-permute-start.3 = (f32[48,128]{1,0:T(8,128)S(1)}, f32[48,128]{1,0:T(8,128)S(1)}, u32[]{:S(2)}, u32[]{:S(2)}) collective-permute-start(f32[48,128]{1,0:T(8,128)S(1)} %add.220), channel_id=1, source_target_pairs={{0,64},{16,80},{32,96},{48,112},{64,0},{80,16},{96,32},{112,48},{1... | collective-permute-start | bytes 73736 | tf_op jit(solution)/shard_map/ppermute | solution.py:43
  165.9 3.7 %collective-permute-done.3 = f32[48,128]{1,0:T(8,128)S(1)} collective-permute-done((f32[48,128]{1,0:T(8,128)S(1)}, f32[48,128]{1,0:T(8,128)S(1)}, u32[]{:S(2)}, u32[]{:S(2)}) %collective-permute-start.3) | collective-permute-done | bytes 24608 | tf_op jit(solution)/shard_map/ppermute | solution.py:43
  169.6 3.8 %collective-permute-start.4 = (f32[48,128]{1,0:T(8,128)S(1)}, f32[48,128]{1,0:T(8,128)S(1)}, u32[]{:S(2)}, u32[]{:S(2)}) collective-permute-start(f32[48,128]{1,0:T(8,128)S(1)} %add.221), channel_id=1, source_target_pairs={{0,128},{16,144},{32,160},{48,176},{64,192},{80,208},{96,224},{112... | collective-permute-start | bytes 73736 | tf_op jit(solution)/shard_map/ppermute | solution.py:43
  173.4 0.9 dynamic-slice_bitcast_fusion
  174.3 8.0 %collective-permute-start.6 = (f32[48,3,128]{2,0,1:T(8,128)S(1)}, f32[48,3,128]{2,0,1:T(8,128)S(1)}, u32[]{:S(2)}, u32[]{:S(2)}) collective-permute-start(f32[48,3,128]{2,0,1:T(8,128)S(1)} %dynamic-slice_bitcast_fusion), channel_id=1, source_target_pairs={{0,2},{2,0},{1,3},{3,1},{4,6},{6,4},{5,7},{7,5},{8,10},{10,8},{9,1... | collective-permute-start | bytes 221192 | tf_op jit(solution)/shard_map/ppermute | solution.py:35
  182.4 0.6 add_multiply_fusion
  183.0 2.0 %collective-permute-done.6 = f32[48,3,128]{2,0,1:T(8,128)S(1)} collective-permute-done((f32[48,3,128]{2,0,1:T(8,128)S(1)}, f32[48,3,128]{2,0,1:T(8,128)S(1)}, u32[]{:S(2)}, u32[]{:S(2)}) %collective-permute-start.6) | collective-permute-done | bytes 73760 | tf_op jit(solution)/shard_map/ppermute | solution.py:35
  185.0 1.5 fusion.12
  (50 shorter events, 1.7 us)
Async XLA Ops:
  7.2 40.3 %copy-start = (f32[64]{0:T(128)S(1)}, f32[64]{0:T(128)}, u32[]{:S(2)}) copy-start(f32[64]{0:T(128)} %param.10) | copy-start | bytes 772
  7.2 36.8 %copy-start.1 = (s32[32]{0:T(128)S(1)}, s32[32]{0:T(128)}, u32[]{:S(2)}) copy-start(s32[32]{0:T(128)} %param.13) | copy-start | bytes 388
  7.2 37.0 %copy-start.4 = (s32[12,2]{0,1:T(2,128)S(1)}, s32[12,2]{0,1:T(2,128)}, u32[]{:S(2)}) copy-start(s32[12,2]{0,1:T(2,128)} %param.15) | copy-start | bytes 292
  7.2 110.6 %all-gather.2.cloned.1.call-start = ((), (), s32[]{:S(2)}) async-start(), calls=%async_computation.2 | async-start | bytes 7962624 | tf_op jit(solution)/shard_map/all_gather | solution.py:16
  33.4 25.5 %all-to-all-start = ((bf16[16,3,48,128]{3,2,1,0:T(8,128)(2,1)}), bf16[16,3,48,128]{3,2,1,0:T(8,128)(2,1)S(1)}, u32[]{:S(2)}, u32[]{:S(2)}) async-start(bf16[16,3,48,128]{3,2,1,0:T(8,128)(2,1)} %broadcast_in_dim.20), calls=%async_computation | async-start | bytes 1179648 | tf_op jit(solution)/shard_map/all_to_all | solution.py:22
  43.9 129.5 %reduce-scatter.2.cloned.1.call-start = ((), (), s32[]{:S(2)}) async-start(), calls=%async_computation.3 | async-start | bytes 737280 | tf_op jit(solution)/shard_map/reduce_scatter | solution.py:45
  44.4 0.7 copy-start.2
  47.5 3.0 %copy-start.6 = (f32[48]{0:T(128)S(1)}, f32[48]{0:T(128)}, u32[]{:S(2)}) copy-start(f32[48]{0:T(128)} %param.11) | copy-start | bytes 580
  47.5 4.7 %copy-start.5 = (f32[128]{0:T(128)S(1)}, f32[128]{0:T(128)}, u32[]{:S(2)}) copy-start(f32[128]{0:T(128)} %param.12) | copy-start | bytes 1540
  125.7 1.1 copy-start.3
  137.2 3.9 %collective-permute-start.5 = (f32[4,2,48,3,128]{4,2,3,1,0:T(8,128)S(1)}, f32[4,2,48,3,128]{4,2,3,1,0:T(8,128)S(1)}, u32[]{:S(2)}, u32[]{:S(2)}) collective-permute-start(f32[4,2,48,3,128]{4,2,3,1,0:T(8,128)S(1)} %bitcast.77), channel_id=1, source_target_pairs={{0,1},{1,0},{2,3},{3,2},{4,5},{5,4},{6,7},{7,6},{8,9},{9,8},{10,11... | collective-permute-start | bytes 1769480 | tf_op jit(solution)/shard_map/ppermute | solution.py:35
  142.0 9.6 %collective-permute-start = (f32[48,128]{1,0:T(8,128)S(1)}, f32[48,128]{1,0:T(8,128)S(1)}, u32[]{:S(2)}, u32[]{:S(2)}) collective-permute-start(f32[48,128]{1,0:T(8,128)S(1)} %get-tuple-element.3), channel_id=1, source_target_pairs={{0,256},{16,272},{32,288},{48,304},{64,320},{80,336},{96,352},{112... | collective-permute-start | bytes 73736 | tf_op jit(solution)/shard_map/ppermute | solution.py:43
  151.6 5.7 %collective-permute-start.1 = (f32[48,128]{1,0:T(8,128)S(1)}, f32[48,128]{1,0:T(8,128)S(1)}, u32[]{:S(2)}, u32[]{:S(2)}) collective-permute-start(f32[48,128]{1,0:T(8,128)S(1)} %add.218), channel_id=1, source_target_pairs={{0,16},{16,0},{32,48},{48,32},{64,80},{80,64},{96,112},{112,96},{1... | collective-permute-start | bytes 73736 | tf_op jit(solution)/shard_map/ppermute | solution.py:43
  157.3 6.6 %collective-permute-start.2 = (f32[48,128]{1,0:T(8,128)S(1)}, f32[48,128]{1,0:T(8,128)S(1)}, u32[]{:S(2)}, u32[]{:S(2)}) collective-permute-start(f32[48,128]{1,0:T(8,128)S(1)} %add.219), channel_id=1, source_target_pairs={{0,32},{16,48},{32,0},{48,16},{64,96},{80,112},{96,64},{112,80},{1... | collective-permute-start | bytes 73736 | tf_op jit(solution)/shard_map/ppermute | solution.py:43
  163.9 5.7 %collective-permute-start.3 = (f32[48,128]{1,0:T(8,128)S(1)}, f32[48,128]{1,0:T(8,128)S(1)}, u32[]{:S(2)}, u32[]{:S(2)}) collective-permute-start(f32[48,128]{1,0:T(8,128)S(1)} %add.220), channel_id=1, source_target_pairs={{0,64},{16,80},{32,96},{48,112},{64,0},{80,16},{96,32},{112,48},{1... | collective-permute-start | bytes 73736 | tf_op jit(solution)/shard_map/ppermute | solution.py:43
  169.6 12.7 %collective-permute-start.4 = (f32[48,128]{1,0:T(8,128)S(1)}, f32[48,128]{1,0:T(8,128)S(1)}, u32[]{:S(2)}, u32[]{:S(2)}) collective-permute-start(f32[48,128]{1,0:T(8,128)S(1)} %add.221), channel_id=1, source_target_pairs={{0,128},{16,144},{32,160},{48,176},{64,192},{80,208},{96,224},{112... | collective-permute-start | bytes 73736 | tf_op jit(solution)/shard_map/ppermute | solution.py:43
  174.3 10.7 %collective-permute-start.6 = (f32[48,3,128]{2,0,1:T(8,128)S(1)}, f32[48,3,128]{2,0,1:T(8,128)S(1)}, u32[]{:S(2)}, u32[]{:S(2)}) collective-permute-start(f32[48,3,128]{2,0,1:T(8,128)S(1)} %dynamic-slice_bitcast_fusion), channel_id=1, source_target_pairs={{0,2},{2,0},{1,3},{3,1},{4,6},{6,4},{5,7},{7,5},{8,10},{10,8},{9,1... | collective-permute-start | bytes 221192 | tf_op jit(solution)/shard_map/ppermute | solution.py:35
Sparse Core Ops, SparseCore 0:
  31.8 85.9 all-gather.1
  142.1 24.6 reduce-scatter.1
